TPU v7x, 1024 devices: a whole 8x8x8 slice. The times are simulated.
1024 devices in a mesh: row: 16 (over z_lo, x), col: 64 (over z_hi, y, core).
Axes of the slice: x: 8, y: 8, z: 8 (z_hi: 4, z_lo: 2; z = z_hi * 2 + z_lo), core: 2. Of those that a mesh axis runs over, the one named last changes fastest.
Arguments:
- features: bfloat16 [131072, 512], P(('row', 'col')), may hold values from -6 to 6
- adj_tiles: bfloat16 [16, 512, 128, 128], P('row', 'col'), may hold values from -0.1875 to 0.1875
- tile_rows: int32 [16, 512], P('row', 'col'), may hold values from 0 to 63, as said below
- tile_cols: int32 [16, 512], P('row', 'col'), may hold values from 0 to 15
- tile_count: int32 [16, 64], P('row', 'col'), may hold values from 1 to 8, as said below
- weight: bfloat16 [1024, 512], replicated, may hold values from -0.25 to 0.25
- cotangent: bfloat16 [131072, 512], P(('row', 'col')), may hold values from -6 to 6
Outputs:
- hidden: bfloat16 [131072, 512], P(('row', 'col'))
- weight_grad: float32 [1024, 512], replicated
Inputs may be any that keep to these rules, and one draw needn't show every extreme that they name: `tile_count`: some device has all 8 slots live. `tile_rows`: every slot of device (r, c) names tile row (c + k) mod 64 with 0 <= k < 4; slot 0 of every device has k = 3.
All inputs are finite; a program needn't handle non-finite values.
Results may differ from a plain program's by a relative error of at most 0.0035.
Values may be sent and summed in bfloat16 or wider, within the bound.
No kernel may reach another device: no remote copies, remote signals or barrier semaphores. Data moves between devices by JAX's collectives and lax.ppermute only.
A program may use at most 32 MiB of HBM per device.

v0:
```python
import jax
import jax.numpy as jnp
from jax import lax
from jax.sharding import PartitionSpec as P

REACH = 4


def from_behind(value, axis, steps):
    count = lax.axis_size(axis)
    pairs = [(source, (source + steps) % count) for source in range(count)]
    return lax.ppermute(value, axis, pairs)


def tile_forward(adj_tiles, rows_idx, cols_idx, count, source, num_rows):
    width = source.shape[1]
    tile_size = adj_tiles.shape[1]
    blocks = source.reshape(-1, tile_size, width)
    chosen = jnp.take(blocks, cols_idx, axis=0)
    products = jnp.einsum("tij,tjx->tix", adj_tiles, chosen, preferred_element_type=jnp.float32)
    live_mask = (jnp.arange(adj_tiles.shape[0]) < count).astype(jnp.float32)
    placing = (rows_idx[:, None] == jnp.arange(num_rows)[None, :]).astype(jnp.float32) * live_mask[
        :, None
    ]
    return jnp.einsum("tr,tix->rix", placing, products, precision=lax.Precision.HIGHEST)


def tile_backward(adj_tiles, rows_idx, cols_idx, count, source, num_cols):
    width = source.shape[1]
    tile_size = adj_tiles.shape[1]
    blocks = source.reshape(-1, tile_size, width)
    chosen = jnp.take(blocks, rows_idx, axis=0)
    products = jnp.einsum("tji,tjx->tix", adj_tiles, chosen, preferred_element_type=jnp.float32)
    live_mask = (jnp.arange(adj_tiles.shape[0]) < count).astype(jnp.float32)
    placing = (cols_idx[:, None] == jnp.arange(num_cols)[None, :]).astype(jnp.float32) * live_mask[
        :, None
    ]
    total = jnp.einsum("tc,tix->cix", placing, products, precision=lax.Precision.HIGHEST)
    return total.reshape(num_cols * tile_size, width)


def body(features, adj_tiles, tile_rows, tile_cols, tile_count, weight, cotangent):
    width = features.shape[1]
    own_nodes = features.shape[0]
    row_count = lax.axis_size("row")
    col_count = lax.axis_size("col")
    my_tiles = adj_tiles[0]
    my_cols = tile_cols[0]
    count = tile_count[0, 0]
    position = lax.axis_index("col")
    offsets = (tile_rows[0] - position) % col_count
    w_self = weight[:width]
    w_neigh = weight[width:]
    col_feats = lax.all_gather(features, "row", axis=0, tiled=True)
    projected = jnp.dot(col_feats, w_neigh, preferred_element_type=jnp.float32).astype(jnp.bfloat16)
    stacked_sums = tile_forward(my_tiles, offsets, my_cols, count, projected, REACH)
    neighbour = stacked_sums[0]
    for step in range(1, REACH):
        neighbour = neighbour + from_behind(stacked_sums[step], "col", step)
    pre_act = jnp.dot(features, w_self, preferred_element_type=jnp.float32) + neighbour
    hidden = jax.nn.silu(pre_act).astype(jnp.bfloat16)
    sigmoid_z = jax.nn.sigmoid(pre_act)
    slope = sigmoid_z * (1.0 + pre_act * (1.0 - sigmoid_z))
    upstream = (cotangent.astype(jnp.float32) * slope).astype(jnp.bfloat16)
    grad_self = jnp.dot(features.T, upstream, preferred_element_type=jnp.float32)
    window_rows = [upstream]
    for step in range(1, REACH):
        window_rows.append(from_behind(upstream, "col", -step))
    window = jnp.concatenate(window_rows, axis=0)
    spread = tile_backward(my_tiles, offsets, my_cols, count, window, row_count)
    grad_neigh = jnp.dot(col_feats.astype(jnp.float32).T, spread, precision=lax.Precision.HIGHEST)
    stacked = jnp.concatenate([grad_self, grad_neigh], axis=0)
    summed = lax.psum(stacked, ("row", "col"))
    total_nodes = own_nodes * row_count * col_count
    weight_grad = summed * float(total_nodes) ** (-0.5)
    return (hidden, weight_grad)


def solution(mesh):
    in_specs = (
        P(("row", "col"), None),
        P("row", "col", None, None),
        P("row", "col"),
        P("row", "col"),
        P("row", "col"),
        P(),
        P(("row", "col"), None),
    )
    out_specs = (P(("row", "col"), None), P())
    return jax.shard_map(body, mesh=mesh, in_specs=in_specs, out_specs=out_specs, check_vma=False)
```

profile of v0, /device:TPU:1, one launch (start us, length us, event | category | flops | bytes accessed | tf_op | source)
XLA Modules:
  0.0 477.5 jit_solution(13981861673999278861)
XLA Ops:
  7.2 0.0 copy-start
  7.2 0.0 all-gather.2.cloned.1.call-start
  7.2 0.7 all-gather.2.cloned.1.call-update
  7.9 0.0 all-reduce.2.cloned.1.call-start
  8.6 0.7 fusion.33
  9.3 0.7 compare_and_fusion.1
  9.9 0.7 compare_and_fusion
  10.6 79.6 %all-gather.2.cloned.1.call-done = bf16[2048,512]{1,0:T(8,128)(2,1)} async-done(((bf16[128,512]{1,0:T(8,128)(2,1)}), bf16[2048,512]{1,0:T(8,128)(2,1)}) %all-gather.2.cloned.1.call-update) | async-done | bytes 2097168 | tf_op jit(solution)/shard_map/all_gather | solution.py:54
  90.2 2.9 convolution_convert_fusion
  93.1 0.6 gather_fusion
  93.8 0.0 copy-done
  93.8 0.6 fusion.6
  94.4 2.0 copy.18
  96.3 3.4 fusion.2
  99.7 0.0 copy-start.4
  99.7 0.0 copy-start.2
  99.7 0.0 copy-start.7
  99.7 0.0 copy-start.8
  99.8 0.8 fusion.40
  100.6 14.2 %collective-permute-start.2 = (f32[128,512]{1,0:T(8,128)S(1)}, f32[128,512]{1,0:T(8,128)S(1)}, u32[]{:S(2)}, u32[]{:S(2)}) collective-permute-start(f32[128,512]{1,0:T(8,128)S(1)} %bitcast.68), channel_id=1, source_target_pairs={{0,3},{1,4},{2,5},{3,6},{4,7},{5,8},{6,9},{7,10},{8,11},{9,12},{10... | collective-permute-start | bytes 786440 | tf_op jit(solution)/shard_map/ppermute | solution.py:12
  114.8 3.1 collective-permute-start.1
  118.0 1.9 collective-permute-start
  119.9 0.0 copy-done.4
  120.0 13.7 %collective-permute-done.2 = f32[128,512]{1,0:T(8,128)S(1)} collective-permute-done((f32[128,512]{1,0:T(8,128)S(1)}, f32[128,512]{1,0:T(8,128)S(1)}, u32[]{:S(2)}, u32[]{:S(2)}) %collective-permute-start.2) | collective-permute-done | bytes 262176 | tf_op jit(solution)/shard_map/ppermute | solution.py:12
  133.7 8.8 %collective-permute-done.1 = f32[128,512]{1,0:T(8,128)S(1)} collective-permute-done((f32[128,512]{1,0:T(8,128)S(1)}, f32[128,512]{1,0:T(8,128)S(1)}, u32[]{:S(2)}, u32[]{:S(2)}) %collective-permute-start.1) | collective-permute-done | bytes 262176 | tf_op jit(solution)/shard_map/ppermute | solution.py:12
  142.5 0.0 collective-permute-done
  142.5 0.0 copy-done.2
  142.5 0.0 copy-done.7
  142.5 0.0 copy-done.8
  142.5 1.0 multiply_convert_fusion
  143.5 1.9 collective-permute-start.5
  145.4 5.2 %collective-permute-start.4 = (bf16[128,512]{1,0:T(8,128)(2,1)S(1)}, bf16[128,512]{1,0:T(8,128)(2,1)S(1)}, u32[]{:S(2)}, u32[]{:S(2)}) collective-permute-start(bf16[128,512]{1,0:T(8,128)(2,1)S(1)} %get-tuple-element.4), channel_id=1, source_target_pairs={{0,62},{1,63},{2,0},{3,1},{4,2},{5,3},{6,4},{7,5},{8,6},{9,7},{10,... | collective-permute-start | bytes 393224 | tf_op jit(solution)/shard_map/ppermute | solution.py:12
  150.6 5.4 %collective-permute-start.3 = (bf16[128,512]{1,0:T(8,128)(2,1)S(1)}, bf16[128,512]{1,0:T(8,128)(2,1)S(1)}, u32[]{:S(2)}, u32[]{:S(2)}) collective-permute-start(bf16[128,512]{1,0:T(8,128)(2,1)S(1)} %get-tuple-element.4), channel_id=1, source_target_pairs={{0,63},{1,0},{2,1},{3,2},{4,3},{5,4},{6,5},{7,6},{8,7},{9,8},{10,9... | collective-permute-start | bytes 393224 | tf_op jit(solution)/shard_map/ppermute | solution.py:12
  156.0 1.3 convolution_bitcast_fusion.1
  157.3 0.0 collective-permute-done.5
  157.3 1.4 collective-permute-done.4
  158.8 1.6 collective-permute-done.3
  160.4 0.6 gather_fusion.1
  161.0 0.6 fusion.4
  161.6 0.0 copy-start.5
  161.6 2.0 copy.19
  163.6 0.0 copy-done.5
  163.6 5.3 %fusion = f32[16,128,512]{2,0,1:T(8,128)S(1)} fusion(f32[8,512,128]{1,0,2:T(8,128)} %copy.19, f32[8]{0:T(128)S(1)} %get-tuple-element.10, s32[8]{0:T(128)S(1)} %bitcast.71), kind=kOutput, calls=%fused_computation.4 | convolution fusion | flops 100663552 | bytes 6291520 | tf_op jit(solution)/shard_map/tc,tix->cix/dot_general | solution.py:38
  168.9 0.0 copy-start.6
  168.9 2.4 copy.17
  171.4 0.0 copy-done.6
  171.4 0.0 copy-start.1
  171.4 3.6 convolution_bitcast_fusion
  175.0 0.0 copy-done.1
  175.0 1.5 pad_maximum_fusion
  176.5 0.0 copy-start.3
  176.5 0.0 all-reduce.2.cloned.1.call-update
  176.5 0.9 copy-done.3
  177.5 0.7 multiply_convert_fusion.1
  178.2 289.3 %all-reduce.2.cloned.1.call-done = f32[1024,512]{1,0:T(8,128)} async-done(((f32[1024,512]{1,0:T(8,128)}), f32[1024,512]{1,0:T(8,128)}) %all-reduce.2.cloned.1.call-update) | async-done | bytes 2097168 | tf_op jit(solution)/shard_map/psum | solution.py:73
  467.5 3.2 broadcast_multiply_fusion
  (7 shorter events, 0.1 us)
Async XLA Ops:
  7.2 86.6 %copy-start = (bf16[1,8,128,128]{3,2,1,0:T(8,128)(2,1)S(1)}, bf16[1,8,128,128]{3,2,1,0:T(8,128)(2,1)}, u32[]{:S(2)}) copy-start(bf16[1,8,128,128]{3,2,1,0:T(8,128)(2,1)} %param.8) | copy-start | bytes 786436
  7.2 83.0 %all-gather.2.cloned.1.call-start = ((), (), s32[]{:S(2)}) async-start(), calls=%async_computation | async-start | bytes 2228224 | tf_op jit(solution)/shard_map/all_gather | solution.py:54
  7.9 459.6 %all-reduce.2.cloned.1.call-start = ((), (), s32[]{:S(2)}) async-start(), calls=%async_computation.1 | async-start | bytes 4194304 | tf_op jit(solution)/shard_map/psum | solution.py:73
  99.7 20.2 %copy-start.4 = (s32[1,8]{1,0:T(1,128)S(1)}, s32[1,8]{1,0:T(1,128)}, u32[]{:S(2)}) copy-start(s32[1,8]{1,0:T(1,128)} %param.9) | copy-start | bytes 100
  99.7 42.8 %copy-start.2 = (bf16[128,512]{1,0:T(8,128)(2,1)S(1)}, bf16[128,512]{1,0:T(8,128)(2,1)}, u32[]{:S(2)}) copy-start(bf16[128,512]{1,0:T(8,128)(2,1)} %param.7) | copy-start | bytes 393220
  99.7 42.8 %copy-start.7 = (bf16[1024,512]{1,0:T(8,128)(2,1)S(1)}, bf16[1024,512]{1,0:T(8,128)(2,1)}, u32[]{:S(2)}) copy-start(bf16[1024,512]{1,0:T(8,128)(2,1)} %param.12) | copy-start | bytes 3145732
  99.7 42.8 %copy-start.8 = (bf16[128,512]{1,0:T(8,128)(2,1)S(1)}, bf16[128,512]{1,0:T(8,128)(2,1)}, u32[]{:S(2)}) copy-start(bf16[128,512]{1,0:T(8,128)(2,1)} %param.13) | copy-start | bytes 393220
  100.6 33.2 %collective-permute-start.2 = (f32[128,512]{1,0:T(8,128)S(1)}, f32[128,512]{1,0:T(8,128)S(1)}, u32[]{:S(2)}, u32[]{:S(2)}) collective-permute-start(f32[128,512]{1,0:T(8,128)S(1)} %bitcast.68), channel_id=1, source_target_pairs={{0,3},{1,4},{2,5},{3,6},{4,7},{5,8},{6,9},{7,10},{8,11},{9,12},{10... | collective-permute-start | bytes 786440 | tf_op jit(solution)/shard_map/ppermute | solution.py:12
  114.8 27.7 %collective-permute-start.1 = (f32[128,512]{1,0:T(8,128)S(1)}, f32[128,512]{1,0:T(8,128)S(1)}, u32[]{:S(2)}, u32[]{:S(2)}) collective-permute-start(f32[128,512]{1,0:T(8,128)S(1)} %bitcast.69), channel_id=1, source_target_pairs={{0,2},{1,3},{2,4},{3,5},{4,6},{5,7},{6,8},{7,9},{8,10},{9,11},{10,... | collective-permute-start | bytes 786440 | tf_op jit(solution)/shard_map/ppermute | solution.py:12
  118.0 24.5 %collective-permute-start = (f32[128,512]{1,0:T(8,128)S(1)}, f32[128,512]{1,0:T(8,128)S(1)}, u32[]{:S(2)}, u32[]{:S(2)}) collective-permute-start(f32[128,512]{1,0:T(8,128)S(1)} %bitcast.70), channel_id=1, source_target_pairs={{0,1},{1,2},{2,3},{3,4},{4,5},{5,6},{6,7},{7,8},{8,9},{9,10},{10,1... | collective-permute-start | bytes 786440 | tf_op jit(solution)/shard_map/ppermute | solution.py:12
  143.5 13.8 %collective-permute-start.5 = (bf16[128,512]{1,0:T(8,128)(2,1)S(1)}, bf16[128,512]{1,0:T(8,128)(2,1)S(1)}, u32[]{:S(2)}, u32[]{:S(2)}) collective-permute-start(bf16[128,512]{1,0:T(8,128)(2,1)S(1)} %get-tuple-element.4), channel_id=1, source_target_pairs={{0,61},{1,62},{2,63},{3,0},{4,1},{5,2},{6,3},{7,4},{8,5},{9,6},{10... | collective-permute-start | bytes 393224 | tf_op jit(solution)/shard_map/ppermute | solution.py:12
  145.4 13.3 %collective-permute-start.4 = (bf16[128,512]{1,0:T(8,128)(2,1)S(1)}, bf16[128,512]{1,0:T(8,128)(2,1)S(1)}, u32[]{:S(2)}, u32[]{:S(2)}) collective-permute-start(bf16[128,512]{1,0:T(8,128)(2,1)S(1)} %get-tuple-element.4), channel_id=1, source_target_pairs={{0,62},{1,63},{2,0},{3,1},{4,2},{5,3},{6,4},{7,5},{8,6},{9,7},{10,... | collective-permute-start | bytes 393224 | tf_op jit(solution)/shard_map/ppermute | solution.py:12
  150.6 9.8 %collective-permute-start.3 = (bf16[128,512]{1,0:T(8,128)(2,1)S(1)}, bf16[128,512]{1,0:T(8,128)(2,1)S(1)}, u32[]{:S(2)}, u32[]{:S(2)}) collective-permute-start(bf16[128,512]{1,0:T(8,128)(2,1)S(1)} %get-tuple-element.4), channel_id=1, source_target_pairs={{0,63},{1,0},{2,1},{3,2},{4,3},{5,4},{6,5},{7,6},{8,7},{9,8},{10,9... | collective-permute-start | bytes 393224 | tf_op jit(solution)/shard_map/ppermute | solution.py:12
  161.6 2.0 copy-start.5
  168.9 2.4 copy-start.6
  171.4 3.6 copy-start.1
  176.5 0.9 copy-start.3
Sparse Core Ops, SparseCore 0:
  10.7 79.4 all-gather.1
  176.7 290.7 all-reduce.1
where the time goes:
time: 478 us; the launch traced here: 477 us
  waiting for transfers between devices  395 us (83%)
  starting transfers between devices  31.8 us (7%)
  matrix products  18.7 us (4%)
  between operations  15 us (3%)
  local copies, waits for them, and re-layouts  9.39 us (2%)
  other arithmetic  7.43 us (2%)
    psum x1, waiting for transfers between devices, body(): summed = lax.psum(stacked, ('row', 'col'))  289 us
    all_gather x1, waiting for transfers between devices, body(): col_feats = lax.all_gather(features, 'row', axis=0, tiled=True)  79.6 us
    ppermute x6, starting transfers between devices, from_behind(): return lax.ppermute(value, axis, pairs)  31.8 us
    ppermute x6, waiting for transfers between devices, from_behind(): return lax.ppermute(value, axis, pairs)  25.6 us
  transfers between devices with their start and end apart: 8, of which 6 were waited for; matrix products, arithmetic and copies ran while one was open for 1% of the time, Pallas kernels for 0%

commit v1 on v0

v1 whole, which is shorter than its diff:
```python
import jax
import jax.numpy as jnp
from jax import lax
from jax.sharding import Mesh, PartitionSpec as P

REACH = 4
ROW = ("zlo", "x")
COL = ("zhi", "y", "core")
ALL = ROW + COL


def from_behind(value, steps):
    count = lax.axis_size(COL)
    pairs = [(source, (source + steps) % count) for source in range(count)]
    return lax.ppermute(value, COL, pairs)


def reduce_all(stacked):
    part = stacked
    for axis in ("core", "y", "x"):
        part = lax.psum_scatter(part, axis, scatter_dimension=0, tiled=True)
    part = lax.psum(part, ("zhi", "zlo"))
    for axis in ("x", "y", "core"):
        part = lax.all_gather(part, axis, axis=0, tiled=True)
    return part


def gather_row(features):
    return lax.all_gather(features, ROW, axis=0, tiled=True)


def body(features, adj_tiles, tile_rows, tile_cols, tile_count, weight, cotangent):
    width = features.shape[1]
    own_nodes = features.shape[0]
    tile_size = adj_tiles.shape[2]
    row_count = lax.axis_size(ROW)
    col_count = lax.axis_size(COL)
    tiles = adj_tiles[0]
    slots = tiles.shape[0]
    cols = tile_cols[0]
    live = jnp.arange(slots) < tile_count[0, 0]
    offsets = (tile_rows[0] - lax.axis_index(COL)) % col_count
    w_self = weight[:width]
    w_neigh = weight[width:]

    col_feats = gather_row(features)
    chosen = jnp.take(col_feats.reshape(row_count, tile_size, width), cols, axis=0)
    projected = jnp.dot(chosen.reshape(slots * tile_size, width), w_neigh,
                        preferred_element_type=jnp.float32).astype(jnp.bfloat16)
    placing = (offsets[None, :] == jnp.arange(REACH)[:, None]) & live[None, :]
    placed = jnp.where(placing[:, :, None, None], tiles[None], jnp.zeros_like(tiles[None]))
    placed = placed.transpose(0, 2, 1, 3).reshape(REACH * tile_size, slots * tile_size)
    stacked_sums = jnp.dot(placed, projected, preferred_element_type=jnp.float32)
    stacked_sums = stacked_sums.reshape(REACH, tile_size, width)
    neighbour = stacked_sums[0]
    for step in range(1, REACH):
        neighbour = neighbour + from_behind(stacked_sums[step], step)

    pre_act = jnp.dot(features, w_self, preferred_element_type=jnp.float32) + neighbour
    hidden = jax.nn.silu(pre_act).astype(jnp.bfloat16)
    sigmoid_z = jax.nn.sigmoid(pre_act)
    slope = sigmoid_z * (1.0 + pre_act * (1.0 - sigmoid_z))
    upstream = (cotangent.astype(jnp.float32) * slope).astype(jnp.bfloat16)
    grad_self = jnp.dot(features.T, upstream, preferred_element_type=jnp.float32)

    window = [upstream] + [from_behind(upstream, -step) for step in range(1, REACH)]
    window = jnp.stack(window)
    reached = jnp.take(window, offsets, axis=0).reshape(slots * tile_size, width)
    mixed = jnp.einsum("tij,tjx->tix", tiles, chosen, preferred_element_type=jnp.float32)
    mixed = jnp.where(live[:, None, None], mixed, 0.0).reshape(slots * tile_size, width)
    high = mixed.astype(jnp.bfloat16)
    low = (mixed - high.astype(jnp.float32)).astype(jnp.bfloat16)
    grad_neigh = jnp.dot(high.T, reached, preferred_element_type=jnp.float32)
    grad_neigh = grad_neigh + jnp.dot(low.T, reached, preferred_element_type=jnp.float32)

    stacked = jnp.concatenate([grad_self, grad_neigh], axis=0)
    summed = reduce_all(stacked)
    total_nodes = own_nodes * row_count * col_count
    weight_grad = summed * float(total_nodes) ** (-0.5)
    return (hidden, weight_grad)


def solution(mesh):
    rows, cols = mesh.devices.shape
    fine = Mesh(mesh.devices.reshape(2, rows // 2, 4, cols // 8, 2), ALL)
    in_specs = (
        P(ALL, None),
        P(ROW, COL, None, None),
        P(ROW, COL),
        P(ROW, COL),
        P(ROW, COL),
        P(),
        P(ALL, None),
    )
    out_specs = (P(ALL, None), P())
    return jax.shard_map(body, mesh=fine, in_specs=in_specs, out_specs=out_specs, check_vma=False)
```

time: 478 us -> 410 us (0.86)
  waiting for transfers between devices: 395 us -> 290 us
  blocking collectives: 0 us -> 45.3 us
  matrix products: 18.7 us -> 9.7 us
    psum x1 -> x0, waiting for transfers between devices: 289 us -> none  [body(): summed = lax.psum(stacked, ('row', 'col'))]
    reduce_scatter x0 -> x3, waiting for transfers between devices: none -> 103 us  [reduce_all(): part = lax.psum_scatter(part, axis, scatter_dimension=0, tiled=True)]
    all_gather x1 -> x3, waiting for transfers between devices: 79.6 us -> 161 us  [the longest x2 84.4 us: reduce_all(): part = lax.all_gather(part, axis, axis=0, tiled=True)]
    psum x0 -> x1, blocking collectives: none -> 25.1 us  [reduce_all(): part = lax.psum(part, ('zhi', 'zlo'))]
    all_gather x0 -> x1, blocking collectives: none -> 20.2 us  [reduce_all(): part = lax.all_gather(part, axis, axis=0, tiled=True)]
    dot_general x6 -> x4, matrix products: 16.4 us -> 7.09 us  [the longest x1 3.64 us: body(): jnp.dot(placed, projected, preferred_element_type=jnp.float32)]
    dot_general x3 -> x0, local copies, waits for them, and re-layouts: 6.36 us -> none  [the longest x1 2.43 us: tile_backward(): jnp.einsum('tc,tix->cix', placing, products, precision=lax.Precision.HIGH...]
  transfers between devices with their start and end apart: 8 -> 12, of which waited for: 6 -> 10; matrix products, arithmetic and copies ran while one was open for 1% -> 2% of each run, Pallas kernels for 0% -> 0%
where the time goes in v1:
time: 410 us; the launch traced here: 409 us
  waiting for transfers between devices  290 us (71%)
  blocking collectives  45.3 us (11%)
  starting transfers between devices  32 us (8%)
  between operations  14.9 us (4%)
  other arithmetic  10.1 us (2%)
  matrix products  9.7 us (2%)
  local copies, waits for them, and re-layouts  6.59 us (2%)
    reduce_scatter x3, waiting for transfers between devices, reduce_all(): part = lax.psum_scatter(part, axis, scatter_dimension=0, tiled=True)  103 us
    all_gather x2, waiting for transfers between devices, reduce_all(): part = lax.all_gather(part, axis, axis=0, tiled=True)  84.4 us
    all_gather x1, waiting for transfers between devices, gather_row(): return lax.all_gather(features, ROW, axis=0, tiled=True)  76.9 us
    ppermute x6, starting transfers between devices, from_behind(): return lax.ppermute(value, COL, pairs)  31.8 us
    ppermute x6, waiting for transfers between devices, from_behind(): return lax.ppermute(value, COL, pairs)  25.2 us
    psum x1, blocking collectives, reduce_all(): part = lax.psum(part, ('zhi', 'zlo'))  25.1 us
    all_gather x1, blocking collectives, reduce_all(): part = lax.all_gather(part, axis, axis=0, tiled=True)  20.2 us
  transfers between devices with their start and end apart: 12, of which 10 were waited for; matrix products, arithmetic and copies ran while one was open for 2% of the time, Pallas kernels for 0%

profile of v1, /device:TPU:1, one launch (start us, length us, event | category | flops | bytes accessed | tf_op | source)
XLA Modules:
  0.0 408.9 jit_solution(5248622592430930393)
XLA Ops:
  7.2 0.0 all-gather.4.cloned.1.call-start
  7.2 0.7 all-gather.4.cloned.1.call-update
  7.9 0.0 reduce-scatter.4.cloned.1.call-start
  8.6 1.1 copy.9
  9.7 0.7 fusion.29
  10.4 0.7 fusion.30
  11.1 0.7 compare_and_fusion.1
  11.8 0.7 fusion.25
  12.4 0.7 compare_and_fusion
  13.1 0.1 broadcast_bitcast_fusion
  13.2 0.1 broadcast_select_fusion.1
  13.3 76.9 %all-gather.4.cloned.1.call-done = bf16[2048,512]{1,0:T(8,128)(2,1)} async-done(((bf16[128,512]{1,0:T(8,128)(2,1)}), bf16[2048,512]{1,0:T(8,128)(2,1)}) %all-gather.4.cloned.1.call-update) | async-done | bytes 2097168 | tf_op jit(solution)/shard_map/all_gather | solution.py:29
  90.2 2.2 gather_fusion
  92.4 1.2 bitcast_select_fusion
  93.6 3.6 fusion.4
  97.2 1.2 fusion.37
  98.4 0.0 copy-start.3
  98.4 0.0 copy-start.4
  98.4 0.0 copy-start.5
  98.4 14.4 %collective-permute-start.2 = (f32[128,512]{1,0:T(8,128)S(1)}, f32[128,512]{1,0:T(8,128)S(1)}, u32[]{:S(2)}, u32[]{:S(2)}) collective-permute-start(f32[128,512]{1,0:T(8,128)S(1)} %get-tuple-element.5), channel_id=1, source_target_pairs={{0,3},{1,4},{2,5},{3,6},{4,7},{5,8},{6,9},{7,10},{8,11},{9,12},{10... | collective-permute-start | bytes 786440 | tf_op jit(solution)/shard_map/ppermute | solution.py:15
  112.8 3.1 collective-permute-start.1
  116.0 1.9 collective-permute-start
  117.9 0.0 copy-done.2
  117.9 0.6 fusion.10
  118.5 13.3 %collective-permute-done.2 = f32[128,512]{1,0:T(8,128)S(1)} collective-permute-done((f32[128,512]{1,0:T(8,128)S(1)}, f32[128,512]{1,0:T(8,128)S(1)}, u32[]{:S(2)}, u32[]{:S(2)}) %collective-permute-start.2) | collective-permute-done | bytes 262176 | tf_op jit(solution)/shard_map/ppermute | solution.py:15
  131.8 8.7 %collective-permute-done.1 = f32[128,512]{1,0:T(8,128)S(1)} collective-permute-done((f32[128,512]{1,0:T(8,128)S(1)}, f32[128,512]{1,0:T(8,128)S(1)}, u32[]{:S(2)}, u32[]{:S(2)}) %collective-permute-start.1) | collective-permute-done | bytes 262176 | tf_op jit(solution)/shard_map/ppermute | solution.py:15
  140.5 0.0 collective-permute-done
  140.5 0.0 copy-done.3
  140.5 0.0 copy-done.4
  140.5 0.0 copy-done.5
  140.5 1.3 multiply_convert_fusion
  141.8 1.9 collective-permute-start.5
  143.7 5.2 %collective-permute-start.4 = (bf16[128,512]{1,0:T(8,128)(2,1)S(1)}, bf16[128,512]{1,0:T(8,128)(2,1)S(1)}, u32[]{:S(2)}, u32[]{:S(2)}) collective-permute-start(bf16[128,512]{1,0:T(8,128)(2,1)S(1)} %get-tuple-element.2), channel_id=1, source_target_pairs={{0,62},{1,63},{2,0},{3,1},{4,2},{5,3},{6,4},{7,5},{8,6},{9,7},{10,... | collective-permute-start | bytes 393224 | tf_op jit(solution)/shard_map/ppermute | solution.py:15
  148.9 5.2 %collective-permute-start.3 = (bf16[128,512]{1,0:T(8,128)(2,1)S(1)}, bf16[128,512]{1,0:T(8,128)(2,1)S(1)}, u32[]{:S(2)}, u32[]{:S(2)}) collective-permute-start(bf16[128,512]{1,0:T(8,128)(2,1)S(1)} %get-tuple-element.2), channel_id=1, source_target_pairs={{0,63},{1,0},{2,1},{3,2},{4,3},{5,4},{6,5},{7,6},{8,7},{9,8},{10,9... | collective-permute-start | bytes 393224 | tf_op jit(solution)/shard_map/ppermute | solution.py:15
  154.1 1.3 convolution_bitcast_fusion.1
  155.5 0.0 collective-permute-done.5
  155.5 1.6 collective-permute-done.4
  157.1 1.6 collective-permute-done.3
  158.7 0.1 pad_maximum_fusion.1
  158.8 1.6 gather_fusion.1
  160.4 2.1 fusion.2
  162.5 0.0 copy-done.1
  162.5 0.0 copy-start
  162.5 0.8 fusion.3
  163.3 0.4 copy-done
  163.7 1.5 pad_maximum_fusion
  165.2 0.0 reduce-scatter.4.cloned.1.call-update
  165.2 0.0 reduce-scatter.6.cloned.1.call-start
  165.3 17.4 %reduce-scatter.4.cloned.1.call-done = f32[512,512]{1,0:T(8,128)} async-done(((f32[1024,512]{1,0:T(8,128)}), f32[512,512]{1,0:T(8,128)}) %reduce-scatter.4.cloned.1.call-update) | async-done | bytes 1048592 | tf_op jit(solution)/shard_map/reduce_scatter | solution.py:21
  182.7 0.0 reduce-scatter.6.cloned.1.call-update
  182.7 0.0 reduce-scatter.8.cloned.1.call-start
  182.7 42.6 %reduce-scatter.6.cloned.1.call-done = f32[64,512]{1,0:T(8,128)} async-done(((f32[512,512]{1,0:T(8,128)}), f32[64,512]{1,0:T(8,128)}) %reduce-scatter.6.cloned.1.call-update) | async-done | bytes 131088 | tf_op jit(solution)/shard_map/reduce_scatter | solution.py:21
  225.3 0.0 reduce-scatter.8.cloned.1.call-update
  225.3 0.0 all-gather.6.cloned.1.call-start
  225.4 43.0 %reduce-scatter.8.cloned.1.call-done = f32[8,512]{1,0:T(8,128)} async-done(((f32[64,512]{1,0:T(8,128)}), f32[8,512]{1,0:T(8,128)}) %reduce-scatter.8.cloned.1.call-update) | async-done | bytes 16400 | tf_op jit(solution)/shard_map/reduce_scatter | solution.py:21
  268.3 25.1 %psum.7 = f32[8,512]{1,0:T(8,128)S(1)} all-reduce(f32[8,512]{1,0:T(8,128)} %reduce-scatter.8.cloned.1.call-done), channel_id=1, replica_groups=mesh['zlo'=2,'x'=8,'zhi'=4,'y'=8,'core'=2] {'zhi','zlo'}, use_global_device_ids=true, to_apply=%region_3.4 | all-reduce | flops 4096 | bytes 32768 | tf_op jit(solution)/shard_map/psum | solution.py:22
  293.4 20.2 %all_gather.13 = f32[64,512]{1,0:T(8,128)} all-gather(f32[8,512]{1,0:T(8,128)S(1)} %psum.7), channel_id=1, replica_groups=mesh['zlo'=2,'x'=8,'zhi'=4,'y'=8,'core'=2] {'x'}, dimensions={0}, use_global_device_ids=true | all-gather | bytes 147456 | tf_op jit(solution)/shard_map/all_gather | solution.py:24
  313.6 0.0 all-gather.6.cloned.1.call-update
  313.7 0.0 all-gather.8.cloned.1.call-start
  313.7 54.0 %all-gather.6.cloned.1.call-done = f32[512,512]{1,0:T(8,128)} async-done(((f32[64,512]{1,0:T(8,128)}), f32[512,512]{1,0:T(8,128)}) %all-gather.6.cloned.1.call-update) | async-done | bytes 1048592 | tf_op jit(solution)/shard_map/all_gather | solution.py:24
  367.7 0.0 all-gather.8.cloned.1.call-update
  367.7 0.7 multiply_convert_fusion.1
  368.5 30.4 %all-gather.8.cloned.1.call-done = f32[1024,512]{1,0:T(8,128)} async-done(((f32[512,512]{1,0:T(8,128)}), f32[1024,512]{1,0:T(8,128)}) %all-gather.8.cloned.1.call-update) | async-done | bytes 2097168 | tf_op jit(solution)/shard_map/all_gather | solution.py:24
  398.9 3.2 broadcast_multiply_fusion
  (6 shorter events, 0.0 us)
Async XLA Ops:
  7.2 83.0 %all-gather.4.cloned.1.call-start = ((), (), s32[]{:S(2)}) async-start(), calls=%async_computation.3 | async-start | bytes 2228224 | tf_op jit(solution)/shard_map/all_gather | solution.py:29
  7.9 174.8 %reduce-scatter.4.cloned.1.call-start = ((), (), s32[]{:S(2)}) async-start(), calls=%async_computation.4 | async-start | bytes 3145728 | tf_op jit(solution)/shard_map/reduce_scatter | solution.py:21
  93.6 24.3 %copy-start.2 = (bf16[1,8,128,128]{3,2,1,0:T(8,128)(2,1)S(1)}, bf16[1,8,128,128]{3,2,1,0:T(8,128)(2,1)}, u32[]{:S(2)}) copy-start(bf16[1,8,128,128]{3,2,1,0:T(8,128)(2,1)} %param.8) | copy-start | bytes 786436
  98.4 42.1 %copy-start.3 = (bf16[128,512]{1,0:T(8,128)(2,1)S(1)}, bf16[128,512]{1,0:T(8,128)(2,1)}, u32[]{:S(2)}) copy-start(bf16[128,512]{1,0:T(8,128)(2,1)} %param.7) | copy-start | bytes 393220
  98.4 42.1 %copy-start.4 = (bf16[1024,512]{1,0:T(8,128)(2,1)S(1)}, bf16[1024,512]{1,0:T(8,128)(2,1)}, u32[]{:S(2)}) copy-start(bf16[1024,512]{1,0:T(8,128)(2,1)} %param.12) | copy-start | bytes 3145732
  98.4 42.1 %copy-start.5 = (bf16[128,512]{1,0:T(8,128)(2,1)S(1)}, bf16[128,512]{1,0:T(8,128)(2,1)}, u32[]{:S(2)}) copy-start(bf16[128,512]{1,0:T(8,128)(2,1)} %param.13) | copy-start | bytes 393220
  98.4 33.3 %collective-permute-start.2 = (f32[128,512]{1,0:T(8,128)S(1)}, f32[128,512]{1,0:T(8,128)S(1)}, u32[]{:S(2)}, u32[]{:S(2)}) collective-permute-start(f32[128,512]{1,0:T(8,128)S(1)} %get-tuple-element.5), channel_id=1, source_target_pairs={{0,3},{1,4},{2,5},{3,6},{4,7},{5,8},{6,9},{7,10},{8,11},{9,12},{10... | collective-permute-start | bytes 786440 | tf_op jit(solution)/shard_map/ppermute | solution.py:15
  112.8 27.7 %collective-permute-start.1 = (f32[128,512]{1,0:T(8,128)S(1)}, f32[128,512]{1,0:T(8,128)S(1)}, u32[]{:S(2)}, u32[]{:S(2)}) collective-permute-start(f32[128,512]{1,0:T(8,128)S(1)} %get-tuple-element.6), channel_id=1, source_target_pairs={{0,2},{1,3},{2,4},{3,5},{4,6},{5,7},{6,8},{7,9},{8,10},{9,11},{10,... | collective-permute-start | bytes 786440 | tf_op jit(solution)/shard_map/ppermute | solution.py:15
  116.0 24.5 %collective-permute-start = (f32[128,512]{1,0:T(8,128)S(1)}, f32[128,512]{1,0:T(8,128)S(1)}, u32[]{:S(2)}, u32[]{:S(2)}) collective-permute-start(f32[128,512]{1,0:T(8,128)S(1)} %get-tuple-element.4), channel_id=1, source_target_pairs={{0,1},{1,2},{2,3},{3,4},{4,5},{5,6},{6,7},{7,8},{8,9},{9,10},{10,1... | collective-permute-start | bytes 786440 | tf_op jit(solution)/shard_map/ppermute | solution.py:15
  141.8 13.7 %collective-permute-start.5 = (bf16[128,512]{1,0:T(8,128)(2,1)S(1)}, bf16[128,512]{1,0:T(8,128)(2,1)S(1)}, u32[]{:S(2)}, u32[]{:S(2)}) collective-permute-start(bf16[128,512]{1,0:T(8,128)(2,1)S(1)} %get-tuple-element.2), channel_id=1, source_target_pairs={{0,61},{1,62},{2,63},{3,0},{4,1},{5,2},{6,3},{7,4},{8,5},{9,6},{10... | collective-permute-start | bytes 393224 | tf_op jit(solution)/shard_map/ppermute | solution.py:15
  143.7 13.3 %collective-permute-start.4 = (bf16[128,512]{1,0:T(8,128)(2,1)S(1)}, bf16[128,512]{1,0:T(8,128)(2,1)S(1)}, u32[]{:S(2)}, u32[]{:S(2)}) collective-permute-start(bf16[128,512]{1,0:T(8,128)(2,1)S(1)} %get-tuple-element.2), channel_id=1, source_target_pairs={{0,62},{1,63},{2,0},{3,1},{4,2},{5,3},{6,4},{7,5},{8,6},{9,7},{10,... | collective-permute-start | bytes 393224 | tf_op jit(solution)/shard_map/ppermute | solution.py:15
  148.9 9.8 %collective-permute-start.3 = (bf16[128,512]{1,0:T(8,128)(2,1)S(1)}, bf16[128,512]{1,0:T(8,128)(2,1)S(1)}, u32[]{:S(2)}, u32[]{:S(2)}) collective-permute-start(bf16[128,512]{1,0:T(8,128)(2,1)S(1)} %get-tuple-element.2), channel_id=1, source_target_pairs={{0,63},{1,0},{2,1},{3,2},{4,3},{5,4},{6,5},{7,6},{8,7},{9,8},{10,9... | collective-permute-start | bytes 393224 | tf_op jit(solution)/shard_map/ppermute | solution.py:15
  160.4 2.1 copy-start.1
  162.5 1.2 copy-start
  165.2 60.1 %reduce-scatter.6.cloned.1.call-start = ((), (), s32[]{:S(2)}) async-start(), calls=%async_computation.5 | async-start | bytes 1179648 | tf_op jit(solution)/shard_map/reduce_scatter | solution.py:21
  182.7 85.7 %reduce-scatter.8.cloned.1.call-start = ((), (), s32[]{:S(2)}) async-start(), calls=%async_computation.6 | async-start | bytes 147456 | tf_op jit(solution)/shard_map/reduce_scatter | solution.py:21
  225.3 142.4 %all-gather.6.cloned.1.call-start = ((), (), s32[]{:S(2)}) async-start(), calls=%async_computation.7 | async-start | bytes 1179648 | tf_op jit(solution)/shard_map/all_gather | solution.py:24
  313.7 85.2 %all-gather.8.cloned.1.call-start = ((), (), s32[]{:S(2)}) async-start(), calls=%async_computation.8 | async-start | bytes 3145728 | tf_op jit(solution)/shard_map/all_gather | solution.py:24
Sparse Core Ops, SparseCore 0:
  10.7 79.4 all-gather.3
  165.3 17.2 reduce-scatter.3
  186.4 38.8 reduce-scatter.5
  228.9 39.4 reduce-scatter.7
  313.8 53.8 all-gather.5
  370.2 28.5 all-gather.7

commit v2 on v1

--- a/solution.py
+++ b/solution.py
@@ -15,18 +15,29 @@
     return lax.ppermute(value, COL, pairs)
 
 
+def exchange_sum(part, axes):
+    peers = lax.axis_size(axes)
+    pieces = part.reshape(peers, part.shape[0] // peers, part.shape[1])
+    pieces = lax.all_to_all(pieces, axes, 0, 0, tiled=True)
+    return pieces.sum(axis=0)
+
+
+def exchange_gather(part, axes):
+    peers = lax.axis_size(axes)
+    copies = jnp.broadcast_to(part[None], (peers,) + part.shape)
+    copies = lax.all_to_all(copies, axes, 0, 0, tiled=True)
+    return copies.reshape(peers * part.shape[0], *part.shape[1:])
+
+
 def reduce_all(stacked):
-    part = stacked
-    for axis in ("core", "y", "x"):
-        part = lax.psum_scatter(part, axis, scatter_dimension=0, tiled=True)
-    part = lax.psum(part, ("zhi", "zlo"))
-    for axis in ("x", "y", "core"):
-        part = lax.all_gather(part, axis, axis=0, tiled=True)
-    return part
+    part = exchange_sum(stacked, COL)
+    part = exchange_sum(part, ROW)
+    part = exchange_gather(part, ROW)
+    return exchange_gather(part, COL)
 
 
 def gather_row(features):
-    return lax.all_gather(features, ROW, axis=0, tiled=True)
+    return exchange_gather(features, ROW)
 
 
 def body(features, adj_tiles, tile_rows, tile_cols, tile_count, weight, cotangent):

time: 410 us -> 293 us (0.71)
  waiting for transfers between devices: 290 us -> 124 us
  blocking collectives: 45.3 us -> 85.8 us
  starting transfers between devices: 32 us -> 57.9 us
  between operations: 14.9 us -> 1.57 us
  other arithmetic: 10.1 us -> 4.16 us
    all_gather x3 -> x0, waiting for transfers between devices: 161 us -> none  [the longest x2 84.4 us: reduce_all(): part = lax.all_gather(part, axis, axis=0, tiled=True)]
    reduce_scatter x3 -> x0, waiting for transfers between devices: 103 us -> none  [reduce_all(): part = lax.psum_scatter(part, axis, scatter_dimension=0, tiled=True)]
    all_to_all x0 -> x2, waiting for transfers between devices: none -> 90.7 us  [exchange_gather(): copies = lax.all_to_all(copies, axes, 0, 0, tiled=True)]
    all_to_all x0 -> x3, blocking collectives: none -> 85.8 us  [the longest x2 75.9 us: exchange_sum(): pieces = lax.all_to_all(pieces, axes, 0, 0, tiled=True)]
    all_to_all x0 -> x2, starting transfers between devices: none -> 26.4 us  [exchange_gather(): copies = lax.all_to_all(copies, axes, 0, 0, tiled=True)]
    psum x1 -> x0, blocking collectives: 25.1 us -> none  [reduce_all(): part = lax.psum(part, ('zhi', 'zlo'))]
    all_gather x1 -> x0, blocking collectives: 20.2 us -> none  [reduce_all(): part = lax.all_gather(part, axis, axis=0, tiled=True)]
    ppermute x6, waiting for transfers between devices: 25.2 us -> 32.9 us  [from_behind(): return lax.ppermute(value, COL, pairs)]
  transfers between devices with their start and end apart: 12 -> 8, of which waited for: 10 -> 6; matrix products, arithmetic and copies ran while one was open for 2% -> 1% of each run, Pallas kernels for 0% -> 0%
where the time goes in v2:
time: 293 us; the launch traced here: 292 us
  waiting for transfers between devices  124 us (42%)
  blocking collectives  85.8 us (29%)
  starting transfers between devices  57.9 us (20%)
  matrix products  9.32 us (3%)
  local copies, waits for them, and re-layouts  9.12 us (3%)
  other arithmetic  4.16 us (1%)
    all_to_all x2, waiting for transfers between devices, exchange_gather(): copies = lax.all_to_all(copies, axes, 0, 0, tiled=True)  90.7 us
    all_to_all x2, blocking collectives, exchange_sum(): pieces = lax.all_to_all(pieces, axes, 0, 0, tiled=True)  75.9 us
    ppermute x6, waiting for transfers between devices, from_behind(): return lax.ppermute(value, COL, pairs)  32.9 us
    ppermute x6, starting transfers between devices, from_behind(): return lax.ppermute(value, COL, pairs)  31.5 us
    all_to_all x2, starting transfers between devices, exchange_gather(): copies = lax.all_to_all(copies, axes, 0, 0, tiled=True)  26.4 us
    all_to_all x1, blocking collectives, exchange_gather(): copies = lax.all_to_all(copies, axes, 0, 0, tiled=True)  9.99 us
  transfers between devices with their start and end apart: 8, of which 6 were waited for; matrix products, arithmetic and copies ran while one was open for 1% of the time, Pallas kernels for 0%

profile of v2, /device:TPU:1, one launch (start us, length us, event | category | flops | bytes accessed | tf_op | source)
XLA Modules:
  0.0 291.5 jit_solution(4396878961398665790)
XLA Ops:
  0.6 2.4 broadcast_in_dim.99
  3.1 0.0 copy-start.2
  3.1 0.0 copy-start.7
  3.1 0.0 copy-start.8
  3.1 10.3 %all-to-all-start = ((bf16[16,128,512]{2,1,0:T(8,128)(2,1)}), bf16[16,128,512]{2,1,0:T(8,128)(2,1)S(1)}, u32[]{:S(2)}, u32[]{:S(2)}) async-start(bf16[16,128,512]{2,1,0:T(8,128)(2,1)} %broadcast_in_dim.99), calls=%async_computation | async-start | bytes 4194304 | tf_op jit(solution)/shard_map/all_to_all | solution.py:28
  14.0 0.0 copy-done.2
  14.0 0.2 copy.11
  14.2 0.0 copy-done.7
  14.2 0.0 copy-done.8
  14.3 0.1 broadcast_bitcast_fusion
  14.4 1.1 broadcast_select_fusion.1
  15.5 38.6 %all-to-all-done = bf16[16,128,512]{2,1,0:T(8,128)(2,1)S(1)} async-done(((bf16[16,128,512]{2,1,0:T(8,128)(2,1)}), bf16[16,128,512]{2,1,0:T(8,128)(2,1)S(1)}, u32[]{:S(2)}, u32[]{:S(2)}) %all-to-all-start) | async-done | bytes 2097184 | tf_op jit(solution)/shard_map/all_to_all | solution.py:28
  54.2 0.6 gather_fusion
  54.8 0.0 copy-start.3
  54.8 0.2 bitcast_select_fusion
  55.0 1.0 copy-done.3
  56.0 3.3 %fusion.4 = f32[512,512]{1,0:T(8,128)} fusion(bf16[1024,512]{1,0:T(8,128)(2,1)S(1)} %bitcast_select_fusion, bf16[64,8,8,128]{3,2,1,0:T(8,128)(2,1)S(1)} %bitcast.65, bf16[1024,512]{1,0:T(8,128)(2,1)} %param.12), kind=kOutput, calls=%fused_computation.12 | convolution fusion | flops 1074266112 | bytes 3670016 | tf_op jit(solution)/shard_map/dot_general | solution.py:64
  59.3 1.2 fusion.37
  60.4 0.0 copy-start.4
  60.5 0.0 copy-start.5
  60.5 0.0 copy-start.6
  60.5 13.5 %collective-permute-start.2 = (f32[128,512]{1,0:T(8,128)S(1)}, f32[128,512]{1,0:T(8,128)S(1)}, u32[]{:S(2)}, u32[]{:S(2)}) collective-permute-start(f32[128,512]{1,0:T(8,128)S(1)} %get-tuple-element.5), channel_id=1, source_target_pairs={{0,3},{1,4},{2,5},{3,6},{4,7},{5,8},{6,9},{7,10},{8,11},{9,12},{10... | collective-permute-start | bytes 786440 | tf_op jit(solution)/shard_map/ppermute | solution.py:15
  74.0 3.3 %collective-permute-start.1 = (f32[128,512]{1,0:T(8,128)S(1)}, f32[128,512]{1,0:T(8,128)S(1)}, u32[]{:S(2)}, u32[]{:S(2)}) collective-permute-start(f32[128,512]{1,0:T(8,128)S(1)} %get-tuple-element.6), channel_id=1, source_target_pairs={{0,2},{1,3},{2,4},{3,5},{4,6},{5,7},{6,8},{7,9},{8,10},{9,11},{10,... | collective-permute-start | bytes 786440 | tf_op jit(solution)/shard_map/ppermute | solution.py:15
  77.4 1.9 collective-permute-start
  79.3 0.6 fusion.10
  79.9 21.7 %collective-permute-done.2 = f32[128,512]{1,0:T(8,128)S(1)} collective-permute-done((f32[128,512]{1,0:T(8,128)S(1)}, f32[128,512]{1,0:T(8,128)S(1)}, u32[]{:S(2)}, u32[]{:S(2)}) %collective-permute-start.2) | collective-permute-done | bytes 262176 | tf_op jit(solution)/shard_map/ppermute | solution.py:15
  101.6 8.0 %collective-permute-done.1 = f32[128,512]{1,0:T(8,128)S(1)} collective-permute-done((f32[128,512]{1,0:T(8,128)S(1)}, f32[128,512]{1,0:T(8,128)S(1)}, u32[]{:S(2)}, u32[]{:S(2)}) %collective-permute-start.1) | collective-permute-done | bytes 262176 | tf_op jit(solution)/shard_map/ppermute | solution.py:15
  109.6 0.0 collective-permute-done
  109.6 0.0 copy-done.4
  109.6 0.0 copy-done.5
  109.6 0.0 copy-done.6
  109.6 1.3 multiply_convert_fusion
  110.9 1.9 collective-permute-start.5
  112.8 5.5 %collective-permute-start.4 = (bf16[128,512]{1,0:T(8,128)(2,1)S(1)}, bf16[128,512]{1,0:T(8,128)(2,1)S(1)}, u32[]{:S(2)}, u32[]{:S(2)}) collective-permute-start(bf16[128,512]{1,0:T(8,128)(2,1)S(1)} %get-tuple-element.2), channel_id=1, source_target_pairs={{0,62},{1,63},{2,0},{3,1},{4,2},{5,3},{6,4},{7,5},{8,6},{9,7},{10,... | collective-permute-start | bytes 393224 | tf_op jit(solution)/shard_map/ppermute | solution.py:15
  118.3 5.2 %collective-permute-start.3 = (bf16[128,512]{1,0:T(8,128)(2,1)S(1)}, bf16[128,512]{1,0:T(8,128)(2,1)S(1)}, u32[]{:S(2)}, u32[]{:S(2)}) collective-permute-start(bf16[128,512]{1,0:T(8,128)(2,1)S(1)} %get-tuple-element.2), channel_id=1, source_target_pairs={{0,63},{1,0},{2,1},{3,2},{4,3},{5,4},{6,5},{7,6},{8,7},{9,8},{10,9... | collective-permute-start | bytes 393224 | tf_op jit(solution)/shard_map/ppermute | solution.py:15
  123.6 1.3 convolution_bitcast_fusion.1
  124.9 0.0 collective-permute-done.5
  124.9 1.6 collective-permute-done.4
  126.5 1.6 collective-permute-done.3
  128.1 0.1 pad_maximum_fusion.1
  128.2 1.6 gather_fusion.1
  129.8 0.0 copy-start.1
  129.8 2.1 fusion.2
  131.9 0.0 copy-done.1
  131.9 0.0 copy-start
  131.9 0.8 fusion.3
  132.7 0.4 copy-done
  133.1 0.2 pad_maximum_fusion
  133.3 64.0 %all_to_all.25 = f32[64,16,512]{2,1,0:T(8,128)S(1)} all-to-all(f32[64,16,512]{2,1,0:T(8,128)S(1)} %bitcast.62), channel_id=1, replica_groups=mesh['zlo'=2,'x'=8,'zhi'=4,'y'=8,'core'=2] {'zhi','y','core'}, dimensions={0} | all-to-all | bytes 4194304 | tf_op jit(solution)/shard_map/all_to_all | solution.py:21
  197.3 0.1 reduce_sum.18
  197.4 11.9 %all_to_all.26 = f32[16,1,512]{2,1,0:T(1,128)S(1)} all-to-all(f32[16,1,512]{2,1,0:T(1,128)S(1)} %reshape.194), channel_id=1, replica_groups=mesh['zlo'=2,'x'=8,'zhi'=4,'y'=8,'core'=2] {'zlo','x'}, dimensions={0} | all-to-all | bytes 65536 | tf_op jit(solution)/shard_map/all_to_all | solution.py:21
  209.4 10.0 %all_to_all.27 = f32[16,1,512]{2,1,0:T(1,128)S(1)} all-to-all(f32[16,1,512]{2,1,0:T(1,128)S(1)} %broadcast_in_dim.106), channel_id=1, replica_groups=mesh['zlo'=2,'x'=8,'zhi'=4,'y'=8,'core'=2] {'zlo','x'}, dimensions={0} | all-to-all | bytes 65536 | tf_op jit(solution)/shard_map/all_to_all | solution.py:28
  219.4 1.6 broadcast_in_dim.108
  221.0 16.2 %all-to-all-start.4 = ((f32[64,16,512]{2,1,0:T(8,128)}), f32[64,16,512]{2,1,0:T(8,128)S(1)}, u32[]{:S(2)}, u32[]{:S(2)}) async-start(f32[64,16,512]{2,1,0:T(8,128)} %broadcast_in_dim.108), calls=%async_computation.4 | async-start | bytes 4194304 | tf_op jit(solution)/shard_map/all_to_all | solution.py:28
  237.2 0.7 multiply_convert_fusion.1
  237.9 52.1 %all-to-all-done.4 = f32[64,16,512]{2,1,0:T(8,128)S(1)} async-done(((f32[64,16,512]{2,1,0:T(8,128)}), f32[64,16,512]{2,1,0:T(8,128)S(1)}, u32[]{:S(2)}, u32[]{:S(2)}) %all-to-all-start.4) | async-done | bytes 2097184 | tf_op jit(solution)/shard_map/all_to_all | solution.py:28
  290.0 1.6 broadcast_multiply_fusion
  (13 shorter events, 0.2 us)
Async XLA Ops:
  3.1 10.9 %copy-start.2 = (bf16[1,8,128,128]{3,2,1,0:T(8,128)(2,1)S(1)}, bf16[1,8,128,128]{3,2,1,0:T(8,128)(2,1)}, u32[]{:S(2)}) copy-start(bf16[1,8,128,128]{3,2,1,0:T(8,128)(2,1)} %param.8) | copy-start | bytes 786436
  3.1 11.1 %copy-start.7 = (s32[1,8]{1,0:T(1,128)S(1)}, s32[1,8]{1,0:T(1,128)}, u32[]{:S(2)}) copy-start(s32[1,8]{1,0:T(1,128)} %param.10) | copy-start | bytes 100
  3.1 11.2 %copy-start.8 = (s32[1,8]{1,0:T(1,128)S(1)}, s32[1,8]{1,0:T(1,128)}, u32[]{:S(2)}) copy-start(s32[1,8]{1,0:T(1,128)} %param.9) | copy-start | bytes 100
  3.1 51.1 %all-to-all-start = ((bf16[16,128,512]{2,1,0:T(8,128)(2,1)}), bf16[16,128,512]{2,1,0:T(8,128)(2,1)S(1)}, u32[]{:S(2)}, u32[]{:S(2)}) async-start(bf16[16,128,512]{2,1,0:T(8,128)(2,1)} %broadcast_in_dim.99), calls=%async_computation | async-start | bytes 4194304 | tf_op jit(solution)/shard_map/all_to_all | solution.py:28
  54.8 1.2 copy-start.3
  60.4 49.1 %copy-start.4 = (bf16[128,512]{1,0:T(8,128)(2,1)S(1)}, bf16[128,512]{1,0:T(8,128)(2,1)}, u32[]{:S(2)}) copy-start(bf16[128,512]{1,0:T(8,128)(2,1)} %param.7) | copy-start | bytes 393220
  60.5 49.1 %copy-start.5 = (bf16[1024,512]{1,0:T(8,128)(2,1)S(1)}, bf16[1024,512]{1,0:T(8,128)(2,1)}, u32[]{:S(2)}) copy-start(bf16[1024,512]{1,0:T(8,128)(2,1)} %param.12) | copy-start | bytes 3145732
  60.5 49.1 %copy-start.6 = (bf16[128,512]{1,0:T(8,128)(2,1)S(1)}, bf16[128,512]{1,0:T(8,128)(2,1)}, u32[]{:S(2)}) copy-start(bf16[128,512]{1,0:T(8,128)(2,1)} %param.13) | copy-start | bytes 393220
  60.5 41.1 %collective-permute-start.2 = (f32[128,512]{1,0:T(8,128)S(1)}, f32[128,512]{1,0:T(8,128)S(1)}, u32[]{:S(2)}, u32[]{:S(2)}) collective-permute-start(f32[128,512]{1,0:T(8,128)S(1)} %get-tuple-element.5), channel_id=1, source_target_pairs={{0,3},{1,4},{2,5},{3,6},{4,7},{5,8},{6,9},{7,10},{8,11},{9,12},{10... | collective-permute-start | bytes 786440 | tf_op jit(solution)/shard_map/ppermute | solution.py:15
  74.0 35.5 %collective-permute-start.1 = (f32[128,512]{1,0:T(8,128)S(1)}, f32[128,512]{1,0:T(8,128)S(1)}, u32[]{:S(2)}, u32[]{:S(2)}) collective-permute-start(f32[128,512]{1,0:T(8,128)S(1)} %get-tuple-element.6), channel_id=1, source_target_pairs={{0,2},{1,3},{2,4},{3,5},{4,6},{5,7},{6,8},{7,9},{8,10},{9,11},{10,... | collective-permute-start | bytes 786440 | tf_op jit(solution)/shard_map/ppermute | solution.py:15
  77.4 32.2 %collective-permute-start = (f32[128,512]{1,0:T(8,128)S(1)}, f32[128,512]{1,0:T(8,128)S(1)}, u32[]{:S(2)}, u32[]{:S(2)}) collective-permute-start(f32[128,512]{1,0:T(8,128)S(1)} %get-tuple-element.4), channel_id=1, source_target_pairs={{0,1},{1,2},{2,3},{3,4},{4,5},{5,6},{6,7},{7,8},{8,9},{9,10},{10,1... | collective-permute-start | bytes 786440 | tf_op jit(solution)/shard_map/ppermute | solution.py:15
  110.9 14.0 %collective-permute-start.5 = (bf16[128,512]{1,0:T(8,128)(2,1)S(1)}, bf16[128,512]{1,0:T(8,128)(2,1)S(1)}, u32[]{:S(2)}, u32[]{:S(2)}) collective-permute-start(bf16[128,512]{1,0:T(8,128)(2,1)S(1)} %get-tuple-element.2), channel_id=1, source_target_pairs={{0,61},{1,62},{2,63},{3,0},{4,1},{5,2},{6,3},{7,4},{8,5},{9,6},{10... | collective-permute-start | bytes 393224 | tf_op jit(solution)/shard_map/ppermute | solution.py:15
  112.8 13.7 %collective-permute-start.4 = (bf16[128,512]{1,0:T(8,128)(2,1)S(1)}, bf16[128,512]{1,0:T(8,128)(2,1)S(1)}, u32[]{:S(2)}, u32[]{:S(2)}) collective-permute-start(bf16[128,512]{1,0:T(8,128)(2,1)S(1)} %get-tuple-element.2), channel_id=1, source_target_pairs={{0,62},{1,63},{2,0},{3,1},{4,2},{5,3},{6,4},{7,5},{8,6},{9,7},{10,... | collective-permute-start | bytes 393224 | tf_op jit(solution)/shard_map/ppermute | solution.py:15
  118.3 9.8 %collective-permute-start.3 = (bf16[128,512]{1,0:T(8,128)(2,1)S(1)}, bf16[128,512]{1,0:T(8,128)(2,1)S(1)}, u32[]{:S(2)}, u32[]{:S(2)}) collective-permute-start(bf16[128,512]{1,0:T(8,128)(2,1)S(1)} %get-tuple-element.2), channel_id=1, source_target_pairs={{0,63},{1,0},{2,1},{3,2},{4,3},{5,4},{6,5},{7,6},{8,7},{9,8},{10,9... | collective-permute-start | bytes 393224 | tf_op jit(solution)/shard_map/ppermute | solution.py:15
  129.8 2.1 copy-start.1
  131.9 1.2 copy-start
  221.0 69.0 %all-to-all-start.4 = ((f32[64,16,512]{2,1,0:T(8,128)}), f32[64,16,512]{2,1,0:T(8,128)S(1)}, u32[]{:S(2)}, u32[]{:S(2)}) async-start(f32[64,16,512]{2,1,0:T(8,128)} %broadcast_in_dim.108), calls=%async_computation.4 | async-start | bytes 4194304 | tf_op jit(solution)/shard_map/all_to_all | solution.py:28

commit v3 on v2

--- a/solution.py
+++ b/solution.py
@@ -30,10 +30,12 @@
 
 
 def reduce_all(stacked):
-    part = exchange_sum(stacked, COL)
+    part = exchange_sum(stacked, "core")
+    part = exchange_sum(part, ("zhi", "y"))
     part = exchange_sum(part, ROW)
     part = exchange_gather(part, ROW)
-    return exchange_gather(part, COL)
+    part = exchange_gather(part, ("zhi", "y"))
+    return exchange_gather(part, "core")
 
 
 def gather_row(features):

time: 293 us -> 249 us (0.85)
  waiting for transfers between devices: 124 us -> 95.7 us
  blocking collectives: 85.8 us -> 75.1 us
  starting transfers between devices: 57.9 us -> 51.8 us
    all_to_all x2, waiting for transfers between devices: 90.7 us -> 62.8 us  [exchange_gather(): copies = lax.all_to_all(copies, axes, 0, 0, tiled=True)]
    all_to_all x2 -> x3, blocking collectives: 75.9 us -> 54.7 us  [exchange_sum(): pieces = lax.all_to_all(pieces, axes, 0, 0, tiled=True)]
    all_to_all x1 -> x2, blocking collectives: 9.99 us -> 20.3 us  [exchange_gather(): copies = lax.all_to_all(copies, axes, 0, 0, tiled=True)]
    all_to_all x2, starting transfers between devices: 26.4 us -> 20.3 us  [exchange_gather(): copies = lax.all_to_all(copies, axes, 0, 0, tiled=True)]
  transfers between devices with their start and end apart: 8 -> 8, of which waited for: 6 -> 6; matrix products, arithmetic and copies ran while one was open for 1% -> 2% of each run, Pallas kernels for 0% -> 0%
where the time goes in v3:
time: 249 us; the launch traced here: 247 us
  waiting for transfers between devices  95.7 us (38%)
  blocking collectives  75.1 us (30%)
  starting transfers between devices  51.8 us (21%)
  matrix products  9.31 us (4%)
  local copies, waits for them, and re-layouts  8.89 us (4%)
  other arithmetic  4.34 us (2%)
    all_to_all x2, waiting for transfers between devices, exchange_gather(): copies = lax.all_to_all(copies, axes, 0, 0, tiled=True)  62.8 us
    all_to_all x3, blocking collectives, exchange_sum(): pieces = lax.all_to_all(pieces, axes, 0, 0, tiled=True)  54.7 us
    ppermute x6, waiting for transfers between devices, from_behind(): return lax.ppermute(value, COL, pairs)  32.9 us
    ppermute x6, starting transfers between devices, from_behind(): return lax.ppermute(value, COL, pairs)  31.5 us
    all_to_all x2, blocking collectives, exchange_gather(): copies = lax.all_to_all(copies, axes, 0, 0, tiled=True)  20.3 us
    all_to_all x2, starting transfers between devices, exchange_gather(): copies = lax.all_to_all(copies, axes, 0, 0, tiled=True)  20.3 us
  transfers between devices with their start and end apart: 8, of which 6 were waited for; matrix products, arithmetic and copies ran while one was open for 2% of the time, Pallas kernels for 0%

profile of v3, /device:TPU:1, one launch (start us, length us, event | category | flops | bytes accessed | tf_op | source)
XLA Modules:
  0.0 246.7 jit_solution(15251577011213719633)
XLA Ops:
  0.6 2.4 broadcast_in_dim.106
  3.1 0.0 copy-start.2
  3.1 0.0 copy-start.7
  3.1 0.0 copy-start.8
  3.1 10.3 %all-to-all-start = ((bf16[16,128,512]{2,1,0:T(8,128)(2,1)}), bf16[16,128,512]{2,1,0:T(8,128)(2,1)S(1)}, u32[]{:S(2)}, u32[]{:S(2)}) async-start(bf16[16,128,512]{2,1,0:T(8,128)(2,1)} %broadcast_in_dim.106), calls=%async_computation | async-start | bytes 4194304 | tf_op jit(solution)/shard_map/all_to_all | solution.py:28
  14.0 0.0 copy-done.2
  14.0 0.2 copy.13
  14.2 0.0 copy-done.7
  14.2 0.0 copy-done.8
  14.3 0.1 broadcast_bitcast_fusion
  14.4 1.1 broadcast_select_fusion.1
  15.5 38.6 %all-to-all-done = bf16[16,128,512]{2,1,0:T(8,128)(2,1)S(1)} async-done(((bf16[16,128,512]{2,1,0:T(8,128)(2,1)}), bf16[16,128,512]{2,1,0:T(8,128)(2,1)S(1)}, u32[]{:S(2)}, u32[]{:S(2)}) %all-to-all-start) | async-done | bytes 2097184 | tf_op jit(solution)/shard_map/all_to_all | solution.py:28
  54.2 0.6 gather_fusion
  54.8 0.0 copy-start.3
  54.8 0.2 bitcast_select_fusion
  55.0 1.0 copy-done.3
  56.0 3.3 %fusion.4 = f32[512,512]{1,0:T(8,128)} fusion(bf16[1024,512]{1,0:T(8,128)(2,1)S(1)} %bitcast_select_fusion, bf16[64,8,8,128]{3,2,1,0:T(8,128)(2,1)S(1)} %bitcast.70, bf16[1024,512]{1,0:T(8,128)(2,1)} %param.12), kind=kOutput, calls=%fused_computation.12 | convolution fusion | flops 1074266112 | bytes 3670016 | tf_op jit(solution)/shard_map/dot_general | solution.py:66
  59.3 1.2 fusion.37
  60.4 0.0 copy-start.4
  60.5 0.0 copy-start.5
  60.5 0.0 copy-start.6
  60.5 13.5 %collective-permute-start.2 = (f32[128,512]{1,0:T(8,128)S(1)}, f32[128,512]{1,0:T(8,128)S(1)}, u32[]{:S(2)}, u32[]{:S(2)}) collective-permute-start(f32[128,512]{1,0:T(8,128)S(1)} %get-tuple-element.5), channel_id=1, source_target_pairs={{0,3},{1,4},{2,5},{3,6},{4,7},{5,8},{6,9},{7,10},{8,11},{9,12},{10... | collective-permute-start | bytes 786440 | tf_op jit(solution)/shard_map/ppermute | solution.py:15
  74.0 3.3 %collective-permute-start.1 = (f32[128,512]{1,0:T(8,128)S(1)}, f32[128,512]{1,0:T(8,128)S(1)}, u32[]{:S(2)}, u32[]{:S(2)}) collective-permute-start(f32[128,512]{1,0:T(8,128)S(1)} %get-tuple-element.6), channel_id=1, source_target_pairs={{0,2},{1,3},{2,4},{3,5},{4,6},{5,7},{6,8},{7,9},{8,10},{9,11},{10,... | collective-permute-start | bytes 786440 | tf_op jit(solution)/shard_map/ppermute | solution.py:15
  77.4 1.9 collective-permute-start
  79.3 0.6 fusion.10
  79.9 21.7 %collective-permute-done.2 = f32[128,512]{1,0:T(8,128)S(1)} collective-permute-done((f32[128,512]{1,0:T(8,128)S(1)}, f32[128,512]{1,0:T(8,128)S(1)}, u32[]{:S(2)}, u32[]{:S(2)}) %collective-permute-start.2) | collective-permute-done | bytes 262176 | tf_op jit(solution)/shard_map/ppermute | solution.py:15
  101.6 8.0 %collective-permute-done.1 = f32[128,512]{1,0:T(8,128)S(1)} collective-permute-done((f32[128,512]{1,0:T(8,128)S(1)}, f32[128,512]{1,0:T(8,128)S(1)}, u32[]{:S(2)}, u32[]{:S(2)}) %collective-permute-start.1) | collective-permute-done | bytes 262176 | tf_op jit(solution)/shard_map/ppermute | solution.py:15
  109.6 0.0 collective-permute-done
  109.6 0.0 copy-done.4
  109.6 0.0 copy-done.5
  109.6 0.0 copy-done.6
  109.6 1.3 multiply_convert_fusion
  110.9 1.9 collective-permute-start.5
  112.8 5.5 %collective-permute-start.4 = (bf16[128,512]{1,0:T(8,128)(2,1)S(1)}, bf16[128,512]{1,0:T(8,128)(2,1)S(1)}, u32[]{:S(2)}, u32[]{:S(2)}) collective-permute-start(bf16[128,512]{1,0:T(8,128)(2,1)S(1)} %get-tuple-element.2), channel_id=1, source_target_pairs={{0,62},{1,63},{2,0},{3,1},{4,2},{5,3},{6,4},{7,5},{8,6},{9,7},{10,... | collective-permute-start | bytes 393224 | tf_op jit(solution)/shard_map/ppermute | solution.py:15
  118.3 5.2 %collective-permute-start.3 = (bf16[128,512]{1,0:T(8,128)(2,1)S(1)}, bf16[128,512]{1,0:T(8,128)(2,1)S(1)}, u32[]{:S(2)}, u32[]{:S(2)}) collective-permute-start(bf16[128,512]{1,0:T(8,128)(2,1)S(1)} %get-tuple-element.2), channel_id=1, source_target_pairs={{0,63},{1,0},{2,1},{3,2},{4,3},{5,4},{6,5},{7,6},{8,7},{9,8},{10,9... | collective-permute-start | bytes 393224 | tf_op jit(solution)/shard_map/ppermute | solution.py:15
  123.6 1.3 convolution_bitcast_fusion.1
  124.9 0.0 collective-permute-done.5
  124.9 1.6 collective-permute-done.4
  126.5 1.6 collective-permute-done.3
  128.1 0.1 pad_maximum_fusion.1
  128.2 1.6 gather_fusion.1
  129.8 0.0 copy-start.1
  129.8 2.1 fusion.2
  131.9 0.0 copy-done.1
  131.9 0.0 copy-start
  131.9 0.8 fusion.3
  132.7 0.4 copy-done
  133.1 0.2 pad_maximum_fusion
  133.3 5.1 %all_to_all.35 = f32[2,512,512]{2,1,0:T(8,128)S(1)} all-to-all(f32[2,512,512]{2,1,0:T(8,128)S(1)} %bitcast.65), channel_id=1, replica_groups=mesh['zlo'=2,'x'=8,'zhi'=4,'y'=8,'core'=2] {'core'}, dimensions={0} | all-to-all | bytes 4194304 | tf_op jit(solution)/shard_map/all_to_all | solution.py:21
  138.4 0.3 reduce_sum.27
  138.6 35.7 %all_to_all.36 = f32[32,16,512]{2,1,0:T(8,128)S(1)} all-to-all(f32[32,16,512]{2,1,0:T(8,128)S(1)} %bitcast.67), channel_id=1, replica_groups=mesh['zlo'=2,'x'=8,'zhi'=4,'y'=8,'core'=2] {'zhi','y'}, dimensions={0} | all-to-all | bytes 2097152 | tf_op jit(solution)/shard_map/all_to_all | solution.py:21
  174.3 0.1 reduce_sum.28
  174.4 14.0 %all_to_all.37 = f32[16,1,512]{2,1,0:T(1,128)S(1)} all-to-all(f32[16,1,512]{2,1,0:T(1,128)S(1)} %copy.15), channel_id=1, replica_groups=mesh['zlo'=2,'x'=8,'zhi'=4,'y'=8,'core'=2] {'zlo','x'}, dimensions={0} | all-to-all | bytes 65536 | tf_op jit(solution)/shard_map/all_to_all | solution.py:21
  188.5 9.9 %all_to_all.38 = f32[16,1,512]{2,1,0:T(1,128)S(1)} all-to-all(f32[16,1,512]{2,1,0:T(1,128)S(1)} %broadcast_in_dim.113), channel_id=1, replica_groups=mesh['zlo'=2,'x'=8,'zhi'=4,'y'=8,'core'=2] {'zlo','x'}, dimensions={0} | all-to-all | bytes 65536 | tf_op jit(solution)/shard_map/all_to_all | solution.py:28
  198.4 1.1 broadcast_in_dim.115
  199.5 10.0 %all-to-all-start.5 = ((f32[32,16,512]{2,1,0:T(8,128)}), f32[32,16,512]{2,1,0:T(8,128)S(1)}, u32[]{:S(2)}, u32[]{:S(2)}) async-start(f32[32,16,512]{2,1,0:T(8,128)} %broadcast_in_dim.115), calls=%async_computation.5 | async-start | bytes 2097152 | tf_op jit(solution)/shard_map/all_to_all | solution.py:28
  209.5 0.7 multiply_convert_fusion.1
  210.3 24.1 %all-to-all-done.5 = f32[32,16,512]{2,1,0:T(8,128)S(1)} async-done(((f32[32,16,512]{2,1,0:T(8,128)}), f32[32,16,512]{2,1,0:T(8,128)S(1)}, u32[]{:S(2)}, u32[]{:S(2)}) %all-to-all-start.5) | async-done | bytes 1048608 | tf_op jit(solution)/shard_map/all_to_all | solution.py:28
  234.4 0.2 broadcast_in_dim.117
  234.7 10.4 %all_to_all.39 = f32[2,512,512]{2,1,0:T(8,128)S(1)} all-to-all(f32[2,512,512]{2,1,0:T(8,128)S(1)} %broadcast_in_dim.117), channel_id=1, replica_groups=mesh['zlo'=2,'x'=8,'zhi'=4,'y'=8,'core'=2] {'core'}, dimensions={0} | all-to-all | bytes 4194304 | tf_op jit(solution)/shard_map/all_to_all | solution.py:28
  245.1 1.6 broadcast_multiply_fusion
  (13 shorter events, 0.2 us)
Async XLA Ops:
  3.1 10.9 %copy-start.2 = (bf16[1,8,128,128]{3,2,1,0:T(8,128)(2,1)S(1)}, bf16[1,8,128,128]{3,2,1,0:T(8,128)(2,1)}, u32[]{:S(2)}) copy-start(bf16[1,8,128,128]{3,2,1,0:T(8,128)(2,1)} %param.8) | copy-start | bytes 786436
  3.1 11.1 %copy-start.7 = (s32[1,8]{1,0:T(1,128)S(1)}, s32[1,8]{1,0:T(1,128)}, u32[]{:S(2)}) copy-start(s32[1,8]{1,0:T(1,128)} %param.10) | copy-start | bytes 100
  3.1 11.2 %copy-start.8 = (s32[1,8]{1,0:T(1,128)S(1)}, s32[1,8]{1,0:T(1,128)}, u32[]{:S(2)}) copy-start(s32[1,8]{1,0:T(1,128)} %param.9) | copy-start | bytes 100
  3.1 51.1 %all-to-all-start = ((bf16[16,128,512]{2,1,0:T(8,128)(2,1)}), bf16[16,128,512]{2,1,0:T(8,128)(2,1)S(1)}, u32[]{:S(2)}, u32[]{:S(2)}) async-start(bf16[16,128,512]{2,1,0:T(8,128)(2,1)} %broadcast_in_dim.106), calls=%async_computation | async-start | bytes 4194304 | tf_op jit(solution)/shard_map/all_to_all | solution.py:28
  54.8 1.2 copy-start.3
  60.4 49.1 %copy-start.4 = (bf16[128,512]{1,0:T(8,128)(2,1)S(1)}, bf16[128,512]{1,0:T(8,128)(2,1)}, u32[]{:S(2)}) copy-start(bf16[128,512]{1,0:T(8,128)(2,1)} %param.7) | copy-start | bytes 393220
  60.5 49.1 %copy-start.5 = (bf16[1024,512]{1,0:T(8,128)(2,1)S(1)}, bf16[1024,512]{1,0:T(8,128)(2,1)}, u32[]{:S(2)}) copy-start(bf16[1024,512]{1,0:T(8,128)(2,1)} %param.12) | copy-start | bytes 3145732
  60.5 49.1 %copy-start.6 = (bf16[128,512]{1,0:T(8,128)(2,1)S(1)}, bf16[128,512]{1,0:T(8,128)(2,1)}, u32[]{:S(2)}) copy-start(bf16[128,512]{1,0:T(8,128)(2,1)} %param.13) | copy-start | bytes 393220
  60.5 41.1 %collective-permute-start.2 = (f32[128,512]{1,0:T(8,128)S(1)}, f32[128,512]{1,0:T(8,128)S(1)}, u32[]{:S(2)}, u32[]{:S(2)}) collective-permute-start(f32[128,512]{1,0:T(8,128)S(1)} %get-tuple-element.5), channel_id=1, source_target_pairs={{0,3},{1,4},{2,5},{3,6},{4,7},{5,8},{6,9},{7,10},{8,11},{9,12},{10... | collective-permute-start | bytes 786440 | tf_op jit(solution)/shard_map/ppermute | solution.py:15
  74.0 35.5 %collective-permute-start.1 = (f32[128,512]{1,0:T(8,128)S(1)}, f32[128,512]{1,0:T(8,128)S(1)}, u32[]{:S(2)}, u32[]{:S(2)}) collective-permute-start(f32[128,512]{1,0:T(8,128)S(1)} %get-tuple-element.6), channel_id=1, source_target_pairs={{0,2},{1,3},{2,4},{3,5},{4,6},{5,7},{6,8},{7,9},{8,10},{9,11},{10,... | collective-permute-start | bytes 786440 | tf_op jit(solution)/shard_map/ppermute | solution.py:15
  77.4 32.2 %collective-permute-start = (f32[128,512]{1,0:T(8,128)S(1)}, f32[128,512]{1,0:T(8,128)S(1)}, u32[]{:S(2)}, u32[]{:S(2)}) collective-permute-start(f32[128,512]{1,0:T(8,128)S(1)} %get-tuple-element.4), channel_id=1, source_target_pairs={{0,1},{1,2},{2,3},{3,4},{4,5},{5,6},{6,7},{7,8},{8,9},{9,10},{10,1... | collective-permute-start | bytes 786440 | tf_op jit(solution)/shard_map/ppermute | solution.py:15
  110.9 14.0 %collective-permute-start.5 = (bf16[128,512]{1,0:T(8,128)(2,1)S(1)}, bf16[128,512]{1,0:T(8,128)(2,1)S(1)}, u32[]{:S(2)}, u32[]{:S(2)}) collective-permute-start(bf16[128,512]{1,0:T(8,128)(2,1)S(1)} %get-tuple-element.2), channel_id=1, source_target_pairs={{0,61},{1,62},{2,63},{3,0},{4,1},{5,2},{6,3},{7,4},{8,5},{9,6},{10... | collective-permute-start | bytes 393224 | tf_op jit(solution)/shard_map/ppermute | solution.py:15
  112.8 13.7 %collective-permute-start.4 = (bf16[128,512]{1,0:T(8,128)(2,1)S(1)}, bf16[128,512]{1,0:T(8,128)(2,1)S(1)}, u32[]{:S(2)}, u32[]{:S(2)}) collective-permute-start(bf16[128,512]{1,0:T(8,128)(2,1)S(1)} %get-tuple-element.2), channel_id=1, source_target_pairs={{0,62},{1,63},{2,0},{3,1},{4,2},{5,3},{6,4},{7,5},{8,6},{9,7},{10,... | collective-permute-start | bytes 393224 | tf_op jit(solution)/shard_map/ppermute | solution.py:15
  118.3 9.8 %collective-permute-start.3 = (bf16[128,512]{1,0:T(8,128)(2,1)S(1)}, bf16[128,512]{1,0:T(8,128)(2,1)S(1)}, u32[]{:S(2)}, u32[]{:S(2)}) collective-permute-start(bf16[128,512]{1,0:T(8,128)(2,1)S(1)} %get-tuple-element.2), channel_id=1, source_target_pairs={{0,63},{1,0},{2,1},{3,2},{4,3},{5,4},{6,5},{7,6},{8,7},{9,8},{10,9... | collective-permute-start | bytes 393224 | tf_op jit(solution)/shard_map/ppermute | solution.py:15
  129.8 2.1 copy-start.1
  131.9 1.2 copy-start
  199.5 34.9 %all-to-all-start.5 = ((f32[32,16,512]{2,1,0:T(8,128)}), f32[32,16,512]{2,1,0:T(8,128)S(1)}, u32[]{:S(2)}, u32[]{:S(2)}) async-start(f32[32,16,512]{2,1,0:T(8,128)} %broadcast_in_dim.115), calls=%async_computation.5 | async-start | bytes 2097152 | tf_op jit(solution)/shard_map/all_to_all | solution.py:28

commit v4 on v3

--- a/solution.py
+++ b/solution.py
@@ -31,10 +31,10 @@
 
 def reduce_all(stacked):
     part = exchange_sum(stacked, "core")
+    part = exchange_sum(part, ROW)
     part = exchange_sum(part, ("zhi", "y"))
-    part = exchange_sum(part, ROW)
+    part = exchange_gather(part, ("zhi", "y"))
     part = exchange_gather(part, ROW)
-    part = exchange_gather(part, ("zhi", "y"))
     return exchange_gather(part, "core")
 
 

time: 249 us -> 248 us (level)
  blocking collectives: 75.1 us -> 81.4 us
  starting transfers between devices: 51.8 us -> 48.7 us
  waiting for transfers between devices: 95.7 us -> 92.8 us
    all_to_all x2, blocking collectives: 20.3 us -> 25.3 us  [exchange_gather(): copies = lax.all_to_all(copies, axes, 0, 0, tiled=True)]
    all_to_all x2, starting transfers between devices: 20.3 us -> 17.3 us  [exchange_gather(): copies = lax.all_to_all(copies, axes, 0, 0, tiled=True)]
    all_to_all x2, waiting for transfers between devices: 62.8 us -> 59.9 us  [exchange_gather(): copies = lax.all_to_all(copies, axes, 0, 0, tiled=True)]
where the time goes in v4:
time: 248 us; the launch traced here: 247 us
  waiting for transfers between devices  92.8 us (37%)
  blocking collectives  81.4 us (33%)
  starting transfers between devices  48.7 us (20%)
  matrix products  9.31 us (4%)
  local copies, waits for them, and re-layouts  8.94 us (4%)
  other arithmetic  4.36 us (2%)
    all_to_all x2, waiting for transfers between devices, exchange_gather(): copies = lax.all_to_all(copies, axes, 0, 0, tiled=True)  59.9 us
    all_to_all x3, blocking collectives, exchange_sum(): pieces = lax.all_to_all(pieces, axes, 0, 0, tiled=True)  56.1 us
    ppermute x6, waiting for transfers between devices, from_behind(): return lax.ppermute(value, COL, pairs)  32.9 us
    ppermute x6, starting transfers between devices, from_behind(): return lax.ppermute(value, COL, pairs)  31.5 us
    all_to_all x2, blocking collectives, exchange_gather(): copies = lax.all_to_all(copies, axes, 0, 0, tiled=True)  25.3 us
    all_to_all x2, starting transfers between devices, exchange_gather(): copies = lax.all_to_all(copies, axes, 0, 0, tiled=True)  17.3 us
  transfers between devices with their start and end apart: 8, of which 6 were waited for; matrix products, arithmetic and copies ran while one was open for 2% of the time, Pallas kernels for 0%

profile of v4, /device:TPU:1, one launch (start us, length us, event | category | flops | bytes accessed | tf_op | source)
XLA Modules:
  0.0 247.1 jit_solution(1508042389825958217)
XLA Ops:
  0.6 2.4 broadcast_in_dim.106
  3.1 0.0 copy-start.2
  3.1 0.0 copy-start.7
  3.1 0.0 copy-start.8
  3.1 10.3 %all-to-all-start = ((bf16[16,128,512]{2,1,0:T(8,128)(2,1)}), bf16[16,128,512]{2,1,0:T(8,128)(2,1)S(1)}, u32[]{:S(2)}, u32[]{:S(2)}) async-start(bf16[16,128,512]{2,1,0:T(8,128)(2,1)} %broadcast_in_dim.106), calls=%async_computation | async-start | bytes 4194304 | tf_op jit(solution)/shard_map/all_to_all | solution.py:28
  14.0 0.0 copy-done.2
  14.0 0.2 copy.13
  14.2 0.0 copy-done.7
  14.2 0.0 copy-done.8
  14.3 0.1 broadcast_bitcast_fusion
  14.4 1.1 broadcast_select_fusion.1
  15.5 38.6 %all-to-all-done = bf16[16,128,512]{2,1,0:T(8,128)(2,1)S(1)} async-done(((bf16[16,128,512]{2,1,0:T(8,128)(2,1)}), bf16[16,128,512]{2,1,0:T(8,128)(2,1)S(1)}, u32[]{:S(2)}, u32[]{:S(2)}) %all-to-all-start) | async-done | bytes 2097184 | tf_op jit(solution)/shard_map/all_to_all | solution.py:28
  54.2 0.6 gather_fusion
  54.8 0.0 copy-start.3
  54.8 0.2 bitcast_select_fusion
  55.0 1.0 copy-done.3
  56.0 3.3 %fusion.4 = f32[512,512]{1,0:T(8,128)} fusion(bf16[1024,512]{1,0:T(8,128)(2,1)S(1)} %bitcast_select_fusion, bf16[64,8,8,128]{3,2,1,0:T(8,128)(2,1)S(1)} %bitcast.70, bf16[1024,512]{1,0:T(8,128)(2,1)} %param.12), kind=kOutput, calls=%fused_computation.12 | convolution fusion | flops 1074266112 | bytes 3670016 | tf_op jit(solution)/shard_map/dot_general | solution.py:66
  59.3 1.2 fusion.37
  60.4 0.0 copy-start.4
  60.5 0.0 copy-start.5
  60.5 0.0 copy-start.6
  60.5 13.5 %collective-permute-start.2 = (f32[128,512]{1,0:T(8,128)S(1)}, f32[128,512]{1,0:T(8,128)S(1)}, u32[]{:S(2)}, u32[]{:S(2)}) collective-permute-start(f32[128,512]{1,0:T(8,128)S(1)} %get-tuple-element.5), channel_id=1, source_target_pairs={{0,3},{1,4},{2,5},{3,6},{4,7},{5,8},{6,9},{7,10},{8,11},{9,12},{10... | collective-permute-start | bytes 786440 | tf_op jit(solution)/shard_map/ppermute | solution.py:15
  74.0 3.3 %collective-permute-start.1 = (f32[128,512]{1,0:T(8,128)S(1)}, f32[128,512]{1,0:T(8,128)S(1)}, u32[]{:S(2)}, u32[]{:S(2)}) collective-permute-start(f32[128,512]{1,0:T(8,128)S(1)} %get-tuple-element.6), channel_id=1, source_target_pairs={{0,2},{1,3},{2,4},{3,5},{4,6},{5,7},{6,8},{7,9},{8,10},{9,11},{10,... | collective-permute-start | bytes 786440 | tf_op jit(solution)/shard_map/ppermute | solution.py:15
  77.4 1.9 collective-permute-start
  79.3 0.6 fusion.10
  79.9 21.7 %collective-permute-done.2 = f32[128,512]{1,0:T(8,128)S(1)} collective-permute-done((f32[128,512]{1,0:T(8,128)S(1)}, f32[128,512]{1,0:T(8,128)S(1)}, u32[]{:S(2)}, u32[]{:S(2)}) %collective-permute-start.2) | collective-permute-done | bytes 262176 | tf_op jit(solution)/shard_map/ppermute | solution.py:15
  101.6 8.0 %collective-permute-done.1 = f32[128,512]{1,0:T(8,128)S(1)} collective-permute-done((f32[128,512]{1,0:T(8,128)S(1)}, f32[128,512]{1,0:T(8,128)S(1)}, u32[]{:S(2)}, u32[]{:S(2)}) %collective-permute-start.1) | collective-permute-done | bytes 262176 | tf_op jit(solution)/shard_map/ppermute | solution.py:15
  109.6 0.0 collective-permute-done
  109.6 0.0 copy-done.4
  109.6 0.0 copy-done.5
  109.6 0.0 copy-done.6
  109.6 1.3 multiply_convert_fusion
  110.9 1.9 collective-permute-start.5
  112.8 5.5 %collective-permute-start.4 = (bf16[128,512]{1,0:T(8,128)(2,1)S(1)}, bf16[128,512]{1,0:T(8,128)(2,1)S(1)}, u32[]{:S(2)}, u32[]{:S(2)}) collective-permute-start(bf16[128,512]{1,0:T(8,128)(2,1)S(1)} %get-tuple-element.2), channel_id=1, source_target_pairs={{0,62},{1,63},{2,0},{3,1},{4,2},{5,3},{6,4},{7,5},{8,6},{9,7},{10,... | collective-permute-start | bytes 393224 | tf_op jit(solution)/shard_map/ppermute | solution.py:15
  118.3 5.2 %collective-permute-start.3 = (bf16[128,512]{1,0:T(8,128)(2,1)S(1)}, bf16[128,512]{1,0:T(8,128)(2,1)S(1)}, u32[]{:S(2)}, u32[]{:S(2)}) collective-permute-start(bf16[128,512]{1,0:T(8,128)(2,1)S(1)} %get-tuple-element.2), channel_id=1, source_target_pairs={{0,63},{1,0},{2,1},{3,2},{4,3},{5,4},{6,5},{7,6},{8,7},{9,8},{10,9... | collective-permute-start | bytes 393224 | tf_op jit(solution)/shard_map/ppermute | solution.py:15
  123.6 1.3 convolution_bitcast_fusion.1
  124.9 0.0 collective-permute-done.5
  124.9 1.6 collective-permute-done.4
  126.5 1.6 collective-permute-done.3
  128.1 0.1 pad_maximum_fusion.1
  128.2 1.6 gather_fusion.1
  129.8 0.0 copy-start.1
  129.8 2.1 fusion.2
  131.9 0.0 copy-done.1
  131.9 0.0 copy-start
  131.9 0.8 fusion.3
  132.7 0.4 copy-done
  133.1 0.2 pad_maximum_fusion
  133.3 5.1 %all_to_all.35 = f32[2,512,512]{2,1,0:T(8,128)S(1)} all-to-all(f32[2,512,512]{2,1,0:T(8,128)S(1)} %bitcast.65), channel_id=1, replica_groups=mesh['zlo'=2,'x'=8,'zhi'=4,'y'=8,'core'=2] {'core'}, dimensions={0} | all-to-all | bytes 4194304 | tf_op jit(solution)/shard_map/all_to_all | solution.py:21
  138.4 0.3 reduce_sum.27
  138.6 30.8 %all_to_all.36 = f32[16,32,512]{2,1,0:T(8,128)S(1)} all-to-all(f32[16,32,512]{2,1,0:T(8,128)S(1)} %bitcast.67), channel_id=1, replica_groups=mesh['zlo'=2,'x'=8,'zhi'=4,'y'=8,'core'=2] {'zlo','x'}, dimensions={0} | all-to-all | bytes 2097152 | tf_op jit(solution)/shard_map/all_to_all | solution.py:21
  169.4 0.1 reduce_sum.28
  169.5 0.1 copy.15
  169.6 20.2 %all_to_all.37 = f32[32,1,512]{2,1,0:T(1,128)S(1)} all-to-all(f32[32,1,512]{2,1,0:T(1,128)S(1)} %copy.15), channel_id=1, replica_groups=mesh['zlo'=2,'x'=8,'zhi'=4,'y'=8,'core'=2] {'zhi','y'}, dimensions={0} | all-to-all | bytes 131072 | tf_op jit(solution)/shard_map/all_to_all | solution.py:21
  189.8 0.1 reduce_sum.29
  189.9 14.2 %all_to_all.38 = f32[32,1,512]{2,1,0:T(1,128)S(1)} all-to-all(f32[32,1,512]{2,1,0:T(1,128)S(1)} %broadcast_in_dim.113), channel_id=1, replica_groups=mesh['zlo'=2,'x'=8,'zhi'=4,'y'=8,'core'=2] {'zhi','y'}, dimensions={0} | all-to-all | bytes 131072 | tf_op jit(solution)/shard_map/all_to_all | solution.py:28
  204.1 1.1 broadcast_in_dim.115
  205.2 7.0 %all-to-all-start.5 = ((f32[16,32,512]{2,1,0:T(8,128)}), f32[16,32,512]{2,1,0:T(8,128)S(1)}, u32[]{:S(2)}, u32[]{:S(2)}) async-start(f32[16,32,512]{2,1,0:T(8,128)} %broadcast_in_dim.115), calls=%async_computation.5 | async-start | bytes 2097152 | tf_op jit(solution)/shard_map/all_to_all | solution.py:28
  212.3 0.7 multiply_convert_fusion.1
  213.0 21.2 %all-to-all-done.5 = f32[16,32,512]{2,1,0:T(8,128)S(1)} async-done(((f32[16,32,512]{2,1,0:T(8,128)}), f32[16,32,512]{2,1,0:T(8,128)S(1)}, u32[]{:S(2)}, u32[]{:S(2)}) %all-to-all-start.5) | async-done | bytes 1048608 | tf_op jit(solution)/shard_map/all_to_all | solution.py:28
  234.2 0.2 broadcast_in_dim.117
  234.5 11.1 %all_to_all.39 = f32[2,512,512]{2,1,0:T(8,128)S(1)} all-to-all(f32[2,512,512]{2,1,0:T(8,128)S(1)} %broadcast_in_dim.117), channel_id=1, replica_groups=mesh['zlo'=2,'x'=8,'zhi'=4,'y'=8,'core'=2] {'core'}, dimensions={0} | all-to-all | bytes 4194304 | tf_op jit(solution)/shard_map/all_to_all | solution.py:28
  245.5 1.6 broadcast_multiply_fusion
  (11 shorter events, 0.1 us)
Async XLA Ops:
  3.1 10.9 %copy-start.2 = (bf16[1,8,128,128]{3,2,1,0:T(8,128)(2,1)S(1)}, bf16[1,8,128,128]{3,2,1,0:T(8,128)(2,1)}, u32[]{:S(2)}) copy-start(bf16[1,8,128,128]{3,2,1,0:T(8,128)(2,1)} %param.8) | copy-start | bytes 786436
  3.1 11.1 %copy-start.7 = (s32[1,8]{1,0:T(1,128)S(1)}, s32[1,8]{1,0:T(1,128)}, u32[]{:S(2)}) copy-start(s32[1,8]{1,0:T(1,128)} %param.10) | copy-start | bytes 100
  3.1 11.2 %copy-start.8 = (s32[1,8]{1,0:T(1,128)S(1)}, s32[1,8]{1,0:T(1,128)}, u32[]{:S(2)}) copy-start(s32[1,8]{1,0:T(1,128)} %param.9) | copy-start | bytes 100
  3.1 51.1 %all-to-all-start = ((bf16[16,128,512]{2,1,0:T(8,128)(2,1)}), bf16[16,128,512]{2,1,0:T(8,128)(2,1)S(1)}, u32[]{:S(2)}, u32[]{:S(2)}) async-start(bf16[16,128,512]{2,1,0:T(8,128)(2,1)} %broadcast_in_dim.106), calls=%async_computation | async-start | bytes 4194304 | tf_op jit(solution)/shard_map/all_to_all | solution.py:28
  54.8 1.2 copy-start.3
  60.4 49.1 %copy-start.4 = (bf16[128,512]{1,0:T(8,128)(2,1)S(1)}, bf16[128,512]{1,0:T(8,128)(2,1)}, u32[]{:S(2)}) copy-start(bf16[128,512]{1,0:T(8,128)(2,1)} %param.7) | copy-start | bytes 393220
  60.5 49.1 %copy-start.5 = (bf16[1024,512]{1,0:T(8,128)(2,1)S(1)}, bf16[1024,512]{1,0:T(8,128)(2,1)}, u32[]{:S(2)}) copy-start(bf16[1024,512]{1,0:T(8,128)(2,1)} %param.12) | copy-start | bytes 3145732
  60.5 49.1 %copy-start.6 = (bf16[128,512]{1,0:T(8,128)(2,1)S(1)}, bf16[128,512]{1,0:T(8,128)(2,1)}, u32[]{:S(2)}) copy-start(bf16[128,512]{1,0:T(8,128)(2,1)} %param.13) | copy-start | bytes 393220
  60.5 41.1 %collective-permute-start.2 = (f32[128,512]{1,0:T(8,128)S(1)}, f32[128,512]{1,0:T(8,128)S(1)}, u32[]{:S(2)}, u32[]{:S(2)}) collective-permute-start(f32[128,512]{1,0:T(8,128)S(1)} %get-tuple-element.5), channel_id=1, source_target_pairs={{0,3},{1,4},{2,5},{3,6},{4,7},{5,8},{6,9},{7,10},{8,11},{9,12},{10... | collective-permute-start | bytes 786440 | tf_op jit(solution)/shard_map/ppermute | solution.py:15
  74.0 35.5 %collective-permute-start.1 = (f32[128,512]{1,0:T(8,128)S(1)}, f32[128,512]{1,0:T(8,128)S(1)}, u32[]{:S(2)}, u32[]{:S(2)}) collective-permute-start(f32[128,512]{1,0:T(8,128)S(1)} %get-tuple-element.6), channel_id=1, source_target_pairs={{0,2},{1,3},{2,4},{3,5},{4,6},{5,7},{6,8},{7,9},{8,10},{9,11},{10,... | collective-permute-start | bytes 786440 | tf_op jit(solution)/shard_map/ppermute | solution.py:15
  77.4 32.2 %collective-permute-start = (f32[128,512]{1,0:T(8,128)S(1)}, f32[128,512]{1,0:T(8,128)S(1)}, u32[]{:S(2)}, u32[]{:S(2)}) collective-permute-start(f32[128,512]{1,0:T(8,128)S(1)} %get-tuple-element.4), channel_id=1, source_target_pairs={{0,1},{1,2},{2,3},{3,4},{4,5},{5,6},{6,7},{7,8},{8,9},{9,10},{10,1... | collective-permute-start | bytes 786440 | tf_op jit(solution)/shard_map/ppermute | solution.py:15
  110.9 14.0 %collective-permute-start.5 = (bf16[128,512]{1,0:T(8,128)(2,1)S(1)}, bf16[128,512]{1,0:T(8,128)(2,1)S(1)}, u32[]{:S(2)}, u32[]{:S(2)}) collective-permute-start(bf16[128,512]{1,0:T(8,128)(2,1)S(1)} %get-tuple-element.2), channel_id=1, source_target_pairs={{0,61},{1,62},{2,63},{3,0},{4,1},{5,2},{6,3},{7,4},{8,5},{9,6},{10... | collective-permute-start | bytes 393224 | tf_op jit(solution)/shard_map/ppermute | solution.py:15
  112.8 13.7 %collective-permute-start.4 = (bf16[128,512]{1,0:T(8,128)(2,1)S(1)}, bf16[128,512]{1,0:T(8,128)(2,1)S(1)}, u32[]{:S(2)}, u32[]{:S(2)}) collective-permute-start(bf16[128,512]{1,0:T(8,128)(2,1)S(1)} %get-tuple-element.2), channel_id=1, source_target_pairs={{0,62},{1,63},{2,0},{3,1},{4,2},{5,3},{6,4},{7,5},{8,6},{9,7},{10,... | collective-permute-start | bytes 393224 | tf_op jit(solution)/shard_map/ppermute | solution.py:15
  118.3 9.8 %collective-permute-start.3 = (bf16[128,512]{1,0:T(8,128)(2,1)S(1)}, bf16[128,512]{1,0:T(8,128)(2,1)S(1)}, u32[]{:S(2)}, u32[]{:S(2)}) collective-permute-start(bf16[128,512]{1,0:T(8,128)(2,1)S(1)} %get-tuple-element.2), channel_id=1, source_target_pairs={{0,63},{1,0},{2,1},{3,2},{4,3},{5,4},{6,5},{7,6},{8,7},{9,8},{10,9... | collective-permute-start | bytes 393224 | tf_op jit(solution)/shard_map/ppermute | solution.py:15
  129.8 2.1 copy-start.1
  131.9 1.2 copy-start
  205.2 29.0 %all-to-all-start.5 = ((f32[16,32,512]{2,1,0:T(8,128)}), f32[16,32,512]{2,1,0:T(8,128)S(1)}, u32[]{:S(2)}, u32[]{:S(2)}) async-start(f32[16,32,512]{2,1,0:T(8,128)} %broadcast_in_dim.115), calls=%async_computation.5 | async-start | bytes 2097152 | tf_op jit(solution)/shard_map/all_to_all | solution.py:28

commit v5 on v4

--- a/solution.py
+++ b/solution.py
@@ -29,13 +29,14 @@
     return copies.reshape(peers * part.shape[0], *part.shape[1:])
 
 
-def reduce_all(stacked):
+def reduce_all(stacked, scale):
     part = exchange_sum(stacked, "core")
     part = exchange_sum(part, ROW)
     part = exchange_sum(part, ("zhi", "y"))
+    part = (part * scale).astype(jnp.bfloat16)
     part = exchange_gather(part, ("zhi", "y"))
     part = exchange_gather(part, ROW)
-    return exchange_gather(part, "core")
+    return exchange_gather(part, "core").astype(jnp.float32)
 
 
 def gather_row(features):
@@ -87,9 +88,8 @@
     grad_neigh = grad_neigh + jnp.dot(low.T, reached, preferred_element_type=jnp.float32)
 
     stacked = jnp.concatenate([grad_self, grad_neigh], axis=0)
-    summed = reduce_all(stacked)
     total_nodes = own_nodes * row_count * col_count
-    weight_grad = summed * float(total_nodes) ** (-0.5)
+    weight_grad = reduce_all(stacked, float(total_nodes) ** (-0.5))
     return (hidden, weight_grad)
 
 

time: 248 us -> 237 us (0.956)
  waiting for transfers between devices: 92.8 us -> 82.4 us
    all_to_all x2, waiting for transfers between devices: 59.9 us -> 49.4 us  [exchange_gather(): copies = lax.all_to_all(copies, axes, 0, 0, tiled=True)]
where the time goes in v5:
time: 237 us; the launch traced here: 236 us
  waiting for transfers between devices  82.4 us (35%)
  blocking collectives  79.4 us (34%)
  starting transfers between devices  48.7 us (21%)
  matrix products  9.3 us (4%)
  local copies, waits for them, and re-layouts  9.07 us (4%)
  other arithmetic  5.28 us (2%)
    all_to_all x3, blocking collectives, exchange_sum(): pieces = lax.all_to_all(pieces, axes, 0, 0, tiled=True)  56.1 us
    all_to_all x2, waiting for transfers between devices, exchange_gather(): copies = lax.all_to_all(copies, axes, 0, 0, tiled=True)  49.4 us
    ppermute x6, waiting for transfers between devices, from_behind(): return lax.ppermute(value, COL, pairs)  32.9 us
    ppermute x6, starting transfers between devices, from_behind(): return lax.ppermute(value, COL, pairs)  31.5 us
    all_to_all x2, blocking collectives, exchange_gather(): copies = lax.all_to_all(copies, axes, 0, 0, tiled=True)  23.4 us
    all_to_all x2, starting transfers between devices, exchange_gather(): copies = lax.all_to_all(copies, axes, 0, 0, tiled=True)  17.3 us
  transfers between devices with their start and end apart: 8, of which 6 were waited for; matrix products, arithmetic and copies ran while one was open for 2% of the time, Pallas kernels for 0%

profile of v5, /device:TPU:1, one launch (start us, length us, event | category | flops | bytes accessed | tf_op | source)
XLA Modules:
  0.0 235.8 jit_solution(4611528344903325277)
XLA Ops:
  0.6 2.4 %broadcast_in_dim.106 = bf16[16,128,512]{2,1,0:T(8,128)(2,1)} broadcast(bf16[128,512]{1,0:T(8,128)(2,1)} %param.7), dimensions={1,2} | broadcast | bytes 2228224 | tf_op jit(solution)/shard_map/broadcast_in_dim | solution.py:27
  3.1 0.0 copy-start.2
  3.1 0.0 copy-start.7
  3.1 0.0 copy-start.8
  3.1 10.3 %all-to-all-start = ((bf16[16,128,512]{2,1,0:T(8,128)(2,1)}), bf16[16,128,512]{2,1,0:T(8,128)(2,1)S(1)}, u32[]{:S(2)}, u32[]{:S(2)}) async-start(bf16[16,128,512]{2,1,0:T(8,128)(2,1)} %broadcast_in_dim.106), calls=%async_computation | async-start | bytes 4194304 | tf_op jit(solution)/shard_map/all_to_all | solution.py:28
  14.0 0.0 copy-done.2
  14.0 0.2 copy.15
  14.2 0.0 copy-done.7
  14.2 0.0 copy-done.8
  14.3 0.1 broadcast_bitcast_fusion
  14.4 1.1 broadcast_select_fusion.1
  15.5 38.7 %all-to-all-done = bf16[16,128,512]{2,1,0:T(8,128)(2,1)S(1)} async-done(((bf16[16,128,512]{2,1,0:T(8,128)(2,1)}), bf16[16,128,512]{2,1,0:T(8,128)(2,1)S(1)}, u32[]{:S(2)}, u32[]{:S(2)}) %all-to-all-start) | async-done | bytes 2097184 | tf_op jit(solution)/shard_map/all_to_all | solution.py:28
  54.2 0.6 gather_fusion
  54.8 0.0 copy-start.3
  54.8 0.2 bitcast_select_fusion
  55.0 1.0 copy-done.3
  56.0 3.3 %fusion.4 = f32[512,512]{1,0:T(8,128)} fusion(bf16[1024,512]{1,0:T(8,128)(2,1)S(1)} %bitcast_select_fusion, bf16[64,8,8,128]{3,2,1,0:T(8,128)(2,1)S(1)} %bitcast.71, bf16[1024,512]{1,0:T(8,128)(2,1)} %param.12), kind=kOutput, calls=%fused_computation.12 | convolution fusion | flops 1074266112 | bytes 3670016 | tf_op jit(solution)/shard_map/dot_general | solution.py:67
  59.3 1.2 fusion.37
  60.4 0.0 copy-start.4
  60.5 0.0 copy-start.5
  60.5 0.0 copy-start.6
  60.5 13.5 %collective-permute-start.2 = (f32[128,512]{1,0:T(8,128)S(1)}, f32[128,512]{1,0:T(8,128)S(1)}, u32[]{:S(2)}, u32[]{:S(2)}) collective-permute-start(f32[128,512]{1,0:T(8,128)S(1)} %get-tuple-element.5), channel_id=1, source_target_pairs={{0,3},{1,4},{2,5},{3,6},{4,7},{5,8},{6,9},{7,10},{8,11},{9,12},{10... | collective-permute-start | bytes 786440 | tf_op jit(solution)/shard_map/ppermute | solution.py:15
  74.0 3.3 %collective-permute-start.1 = (f32[128,512]{1,0:T(8,128)S(1)}, f32[128,512]{1,0:T(8,128)S(1)}, u32[]{:S(2)}, u32[]{:S(2)}) collective-permute-start(f32[128,512]{1,0:T(8,128)S(1)} %get-tuple-element.6), channel_id=1, source_target_pairs={{0,2},{1,3},{2,4},{3,5},{4,6},{5,7},{6,8},{7,9},{8,10},{9,11},{10,... | collective-permute-start | bytes 786440 | tf_op jit(solution)/shard_map/ppermute | solution.py:15
  77.4 1.9 collective-permute-start
  79.3 0.6 fusion.10
  79.9 21.7 %collective-permute-done.2 = f32[128,512]{1,0:T(8,128)S(1)} collective-permute-done((f32[128,512]{1,0:T(8,128)S(1)}, f32[128,512]{1,0:T(8,128)S(1)}, u32[]{:S(2)}, u32[]{:S(2)}) %collective-permute-start.2) | collective-permute-done | bytes 262176 | tf_op jit(solution)/shard_map/ppermute | solution.py:15
  101.6 8.0 %collective-permute-done.1 = f32[128,512]{1,0:T(8,128)S(1)} collective-permute-done((f32[128,512]{1,0:T(8,128)S(1)}, f32[128,512]{1,0:T(8,128)S(1)}, u32[]{:S(2)}, u32[]{:S(2)}) %collective-permute-start.1) | collective-permute-done | bytes 262176 | tf_op jit(solution)/shard_map/ppermute | solution.py:15
  109.6 0.0 collective-permute-done
  109.6 0.0 copy-done.4
  109.6 0.0 copy-done.5
  109.6 0.0 copy-done.6
  109.6 1.3 multiply_convert_fusion
  110.9 1.9 collective-permute-start.5
  112.8 5.5 %collective-permute-start.4 = (bf16[128,512]{1,0:T(8,128)(2,1)S(1)}, bf16[128,512]{1,0:T(8,128)(2,1)S(1)}, u32[]{:S(2)}, u32[]{:S(2)}) collective-permute-start(bf16[128,512]{1,0:T(8,128)(2,1)S(1)} %get-tuple-element.2), channel_id=1, source_target_pairs={{0,62},{1,63},{2,0},{3,1},{4,2},{5,3},{6,4},{7,5},{8,6},{9,7},{10,... | collective-permute-start | bytes 393224 | tf_op jit(solution)/shard_map/ppermute | solution.py:15
  118.3 5.2 %collective-permute-start.3 = (bf16[128,512]{1,0:T(8,128)(2,1)S(1)}, bf16[128,512]{1,0:T(8,128)(2,1)S(1)}, u32[]{:S(2)}, u32[]{:S(2)}) collective-permute-start(bf16[128,512]{1,0:T(8,128)(2,1)S(1)} %get-tuple-element.2), channel_id=1, source_target_pairs={{0,63},{1,0},{2,1},{3,2},{4,3},{5,4},{6,5},{7,6},{8,7},{9,8},{10,9... | collective-permute-start | bytes 393224 | tf_op jit(solution)/shard_map/ppermute | solution.py:15
  123.6 1.3 convolution_bitcast_fusion.1
  124.9 0.0 collective-permute-done.5
  124.9 1.6 collective-permute-done.4
  126.5 1.6 collective-permute-done.3
  128.1 0.1 pad_maximum_fusion.1
  128.2 1.6 gather_fusion.1
  129.8 2.1 fusion.2
  131.9 0.0 copy-done.1
  131.9 0.0 copy-start
  131.9 0.8 fusion.3
  132.7 0.4 copy-done
  133.1 0.2 pad_maximum_fusion
  133.3 5.1 %all_to_all.35 = f32[2,512,512]{2,1,0:T(8,128)S(1)} all-to-all(f32[2,512,512]{2,1,0:T(8,128)S(1)} %bitcast.67), channel_id=1, replica_groups=mesh['zlo'=2,'x'=8,'zhi'=4,'y'=8,'core'=2] {'core'}, dimensions={0} | all-to-all | bytes 4194304 | tf_op jit(solution)/shard_map/all_to_all | solution.py:21
  138.4 0.3 reduce_sum.27
  138.6 30.8 %all_to_all.36 = f32[16,32,512]{2,1,0:T(8,128)S(1)} all-to-all(f32[16,32,512]{2,1,0:T(8,128)S(1)} %bitcast.68), channel_id=1, replica_groups=mesh['zlo'=2,'x'=8,'zhi'=4,'y'=8,'core'=2] {'zlo','x'}, dimensions={0} | all-to-all | bytes 2097152 | tf_op jit(solution)/shard_map/all_to_all | solution.py:21
  169.4 0.1 reduce_sum.28
  169.5 0.1 copy.17
  169.6 20.2 %all_to_all.37 = f32[32,1,512]{2,1,0:T(1,128)S(1)} all-to-all(f32[32,1,512]{2,1,0:T(1,128)S(1)} %copy.17), channel_id=1, replica_groups=mesh['zlo'=2,'x'=8,'zhi'=4,'y'=8,'core'=2] {'zhi','y'}, dimensions={0} | all-to-all | bytes 131072 | tf_op jit(solution)/shard_map/all_to_all | solution.py:21
  189.8 0.1 reduce_sum.29
  189.9 0.5 broadcast.211
  190.4 0.8 reduce.1
  191.3 14.1 %all_to_all.38 = bf16[32,2,256]{2,1,0:T(2,128)(2,1)S(1)} all-to-all(bf16[32,2,256]{2,1,0:T(2,128)(2,1)S(1)} %reshape.225), channel_id=1, replica_groups=mesh['zlo'=2,'x'=8,'zhi'=4,'y'=8,'core'=2] {'zhi','y'}, dimensions={0} | all-to-all | bytes 65536 | tf_op jit(solution)/shard_map/all_to_all | solution.py:28
  205.4 0.8 broadcast_in_dim.115
  206.2 7.0 %all-to-all-start.5 = ((bf16[16,32,512]{2,1,0:T(8,128)(2,1)}), bf16[16,32,512]{2,1,0:T(8,128)(2,1)S(1)}, u32[]{:S(2)}, u32[]{:S(2)}) async-start(bf16[16,32,512]{2,1,0:T(8,128)(2,1)} %broadcast_in_dim.115), calls=%async_computation.5 | async-start | bytes 1048576 | tf_op jit(solution)/shard_map/all_to_all | solution.py:28
  213.2 0.7 multiply_convert_fusion.1
  214.0 10.8 %all-to-all-done.5 = bf16[16,32,512]{2,1,0:T(8,128)(2,1)S(1)} async-done(((bf16[16,32,512]{2,1,0:T(8,128)(2,1)}), bf16[16,32,512]{2,1,0:T(8,128)(2,1)S(1)}, u32[]{:S(2)}, u32[]{:S(2)}) %all-to-all-start.5) | async-done | bytes 524320 | tf_op jit(solution)/shard_map/all_to_all | solution.py:28
  224.8 0.1 broadcast_in_dim.117
  224.8 9.3 %all_to_all.39 = bf16[2,512,512]{2,1,0:T(8,128)(2,1)S(1)} all-to-all(bf16[2,512,512]{2,1,0:T(8,128)(2,1)S(1)} %broadcast_in_dim.117), channel_id=1, replica_groups=mesh['zlo'=2,'x'=8,'zhi'=4,'y'=8,'core'=2] {'core'}, dimensions={0} | all-to-all | bytes 2097152 | tf_op jit(solution)/shard_map/all_to_all | solution.py:28
  234.1 1.7 bitcast_convert_fusion.4
  (15 shorter events, 0.2 us)
Async XLA Ops:
  3.1 10.9 %copy-start.2 = (bf16[1,8,128,128]{3,2,1,0:T(8,128)(2,1)S(1)}, bf16[1,8,128,128]{3,2,1,0:T(8,128)(2,1)}, u32[]{:S(2)}) copy-start(bf16[1,8,128,128]{3,2,1,0:T(8,128)(2,1)} %param.8) | copy-start | bytes 786436
  3.1 11.1 %copy-start.7 = (s32[1,8]{1,0:T(1,128)S(1)}, s32[1,8]{1,0:T(1,128)}, u32[]{:S(2)}) copy-start(s32[1,8]{1,0:T(1,128)} %param.10) | copy-start | bytes 100
  3.1 11.2 %copy-start.8 = (s32[1,8]{1,0:T(1,128)S(1)}, s32[1,8]{1,0:T(1,128)}, u32[]{:S(2)}) copy-start(s32[1,8]{1,0:T(1,128)} %param.9) | copy-start | bytes 100
  3.1 51.1 %all-to-all-start = ((bf16[16,128,512]{2,1,0:T(8,128)(2,1)}), bf16[16,128,512]{2,1,0:T(8,128)(2,1)S(1)}, u32[]{:S(2)}, u32[]{:S(2)}) async-start(bf16[16,128,512]{2,1,0:T(8,128)(2,1)} %broadcast_in_dim.106), calls=%async_computation | async-start | bytes 4194304 | tf_op jit(solution)/shard_map/all_to_all | solution.py:28
  54.8 1.2 copy-start.3
  60.4 49.1 %copy-start.4 = (bf16[128,512]{1,0:T(8,128)(2,1)S(1)}, bf16[128,512]{1,0:T(8,128)(2,1)}, u32[]{:S(2)}) copy-start(bf16[128,512]{1,0:T(8,128)(2,1)} %param.7) | copy-start | bytes 393220
  60.5 49.1 %copy-start.5 = (bf16[1024,512]{1,0:T(8,128)(2,1)S(1)}, bf16[1024,512]{1,0:T(8,128)(2,1)}, u32[]{:S(2)}) copy-start(bf16[1024,512]{1,0:T(8,128)(2,1)} %param.12) | copy-start | bytes 3145732
  60.5 49.1 %copy-start.6 = (bf16[128,512]{1,0:T(8,128)(2,1)S(1)}, bf16[128,512]{1,0:T(8,128)(2,1)}, u32[]{:S(2)}) copy-start(bf16[128,512]{1,0:T(8,128)(2,1)} %param.13) | copy-start | bytes 393220
  60.5 41.1 %collective-permute-start.2 = (f32[128,512]{1,0:T(8,128)S(1)}, f32[128,512]{1,0:T(8,128)S(1)}, u32[]{:S(2)}, u32[]{:S(2)}) collective-permute-start(f32[128,512]{1,0:T(8,128)S(1)} %get-tuple-element.5), channel_id=1, source_target_pairs={{0,3},{1,4},{2,5},{3,6},{4,7},{5,8},{6,9},{7,10},{8,11},{9,12},{10... | collective-permute-start | bytes 786440 | tf_op jit(solution)/shard_map/ppermute | solution.py:15
  74.0 35.5 %collective-permute-start.1 = (f32[128,512]{1,0:T(8,128)S(1)}, f32[128,512]{1,0:T(8,128)S(1)}, u32[]{:S(2)}, u32[]{:S(2)}) collective-permute-start(f32[128,512]{1,0:T(8,128)S(1)} %get-tuple-element.6), channel_id=1, source_target_pairs={{0,2},{1,3},{2,4},{3,5},{4,6},{5,7},{6,8},{7,9},{8,10},{9,11},{10,... | collective-permute-start | bytes 786440 | tf_op jit(solution)/shard_map/ppermute | solution.py:15
  77.4 32.2 %collective-permute-start = (f32[128,512]{1,0:T(8,128)S(1)}, f32[128,512]{1,0:T(8,128)S(1)}, u32[]{:S(2)}, u32[]{:S(2)}) collective-permute-start(f32[128,512]{1,0:T(8,128)S(1)} %get-tuple-element.4), channel_id=1, source_target_pairs={{0,1},{1,2},{2,3},{3,4},{4,5},{5,6},{6,7},{7,8},{8,9},{9,10},{10,1... | collective-permute-start | bytes 786440 | tf_op jit(solution)/shard_map/ppermute | solution.py:15
  110.9 14.0 %collective-permute-start.5 = (bf16[128,512]{1,0:T(8,128)(2,1)S(1)}, bf16[128,512]{1,0:T(8,128)(2,1)S(1)}, u32[]{:S(2)}, u32[]{:S(2)}) collective-permute-start(bf16[128,512]{1,0:T(8,128)(2,1)S(1)} %get-tuple-element.2), channel_id=1, source_target_pairs={{0,61},{1,62},{2,63},{3,0},{4,1},{5,2},{6,3},{7,4},{8,5},{9,6},{10... | collective-permute-start | bytes 393224 | tf_op jit(solution)/shard_map/ppermute | solution.py:15
  112.8 13.7 %collective-permute-start.4 = (bf16[128,512]{1,0:T(8,128)(2,1)S(1)}, bf16[128,512]{1,0:T(8,128)(2,1)S(1)}, u32[]{:S(2)}, u32[]{:S(2)}) collective-permute-start(bf16[128,512]{1,0:T(8,128)(2,1)S(1)} %get-tuple-element.2), channel_id=1, source_target_pairs={{0,62},{1,63},{2,0},{3,1},{4,2},{5,3},{6,4},{7,5},{8,6},{9,7},{10,... | collective-permute-start | bytes 393224 | tf_op jit(solution)/shard_map/ppermute | solution.py:15
  118.3 9.8 %collective-permute-start.3 = (bf16[128,512]{1,0:T(8,128)(2,1)S(1)}, bf16[128,512]{1,0:T(8,128)(2,1)S(1)}, u32[]{:S(2)}, u32[]{:S(2)}) collective-permute-start(bf16[128,512]{1,0:T(8,128)(2,1)S(1)} %get-tuple-element.2), channel_id=1, source_target_pairs={{0,63},{1,0},{2,1},{3,2},{4,3},{5,4},{6,5},{7,6},{8,7},{9,8},{10,9... | collective-permute-start | bytes 393224 | tf_op jit(solution)/shard_map/ppermute | solution.py:15
  129.8 2.1 copy-start.1
  131.9 1.2 copy-start
  206.2 18.5 %all-to-all-start.5 = ((bf16[16,32,512]{2,1,0:T(8,128)(2,1)}), bf16[16,32,512]{2,1,0:T(8,128)(2,1)S(1)}, u32[]{:S(2)}, u32[]{:S(2)}) async-start(bf16[16,32,512]{2,1,0:T(8,128)(2,1)} %broadcast_in_dim.115), calls=%async_computation.5 | async-start | bytes 1048576 | tf_op jit(solution)/shard_map/all_to_all | solution.py:28

commit v6 on v5

--- a/solution.py
+++ b/solution.py
@@ -31,11 +31,9 @@
 
 def reduce_all(stacked, scale):
     part = exchange_sum(stacked, "core")
-    part = exchange_sum(part, ROW)
-    part = exchange_sum(part, ("zhi", "y"))
+    part = exchange_sum(part, ROW + ("zhi", "y"))
     part = (part * scale).astype(jnp.bfloat16)
-    part = exchange_gather(part, ("zhi", "y"))
-    part = exchange_gather(part, ROW)
+    part = exchange_gather(part, ROW + ("zhi", "y"))
     return exchange_gather(part, "core").astype(jnp.float32)
 
 

time: 237 us -> 240 us (1.013)
  blocking collectives: 79.4 us -> 65.1 us
  starting transfers between devices: 48.7 us -> 57 us
  waiting for transfers between devices: 82.4 us -> 87 us
  other arithmetic: 5.28 us -> 8.77 us
    all_to_all x2 -> x1, blocking collectives: 23.4 us -> 9.1 us  [exchange_gather(): copies = lax.all_to_all(copies, axes, 0, 0, tiled=True)]
    all_to_all x2, starting transfers between devices: 17.3 us -> 25.6 us  [exchange_gather(): copies = lax.all_to_all(copies, axes, 0, 0, tiled=True)]
    all_to_all x2, waiting for transfers between devices: 49.4 us -> 54 us  [exchange_gather(): copies = lax.all_to_all(copies, axes, 0, 0, tiled=True)]
    broadcast_in_dim x1, other arithmetic: 0.82 us -> 3.82 us  [exchange_gather(): copies = jnp.broadcast_to(part[None], (peers,) + part.shape)]
    all_to_all x3 -> x2, blocking collectives: 56.1 us -> 56 us  [exchange_sum(): pieces = lax.all_to_all(pieces, axes, 0, 0, tiled=True)]
where the time goes in v6:
time: 240 us
  waiting for transfers between devices  87 us (36%)
  blocking collectives  65.1 us (27%)
  starting transfers between devices  57 us (24%)
  local copies, waits for them, and re-layouts  10.8 us (4%)
  matrix products  9.31 us (4%)
  other arithmetic  8.77 us (4%)
    all_to_all x2, blocking collectives, exchange_sum(): pieces = lax.all_to_all(pieces, axes, 0, 0, tiled=True)  56 us
    all_to_all x2, waiting for transfers between devices, exchange_gather(): copies = lax.all_to_all(copies, axes, 0, 0, tiled=True)  54 us
    ppermute x6, waiting for transfers between devices, from_behind(): return lax.ppermute(value, COL, pairs)  33 us
    ppermute x6, starting transfers between devices, from_behind(): return lax.ppermute(value, COL, pairs)  31.5 us
    all_to_all x2, starting transfers between devices, exchange_gather(): copies = lax.all_to_all(copies, axes, 0, 0, tiled=True)  25.6 us
    all_to_all x1, blocking collectives, exchange_gather(): copies = lax.all_to_all(copies, axes, 0, 0, tiled=True)  9.1 us
  transfers between devices with their start and end apart: 8, of which 6 were waited for; matrix products, arithmetic and copies ran while one was open for 2% of the time, Pallas kernels for 0%

profile of v6, /device:TPU:1, one launch (start us, length us, event | category | flops | bytes accessed | tf_op | source)
XLA Modules:
  0.0 239.6 jit_solution(7217943812733851759)
XLA Ops:
  0.6 2.4 %broadcast_in_dim.99 = bf16[16,128,512]{2,1,0:T(8,128)(2,1)} broadcast(bf16[128,512]{1,0:T(8,128)(2,1)} %param.7), dimensions={1,2} | broadcast | bytes 2228224 | tf_op jit(solution)/shard_map/broadcast_in_dim | solution.py:27
  3.1 0.0 copy-start.2
  3.1 0.0 copy-start.7
  3.1 0.0 copy-start.8
  3.1 10.3 %all-to-all-start = ((bf16[16,128,512]{2,1,0:T(8,128)(2,1)}), bf16[16,128,512]{2,1,0:T(8,128)(2,1)S(1)}, u32[]{:S(2)}, u32[]{:S(2)}) async-start(bf16[16,128,512]{2,1,0:T(8,128)(2,1)} %broadcast_in_dim.99), calls=%async_computation | async-start | bytes 4194304 | tf_op jit(solution)/shard_map/all_to_all | solution.py:28
  14.0 0.0 copy-done.2
  14.0 0.2 copy.13
  14.2 0.0 copy-done.7
  14.2 0.0 copy-done.8
  14.3 0.1 broadcast_bitcast_fusion
  14.4 1.1 broadcast_select_fusion.1
  15.5 38.6 %all-to-all-done = bf16[16,128,512]{2,1,0:T(8,128)(2,1)S(1)} async-done(((bf16[16,128,512]{2,1,0:T(8,128)(2,1)}), bf16[16,128,512]{2,1,0:T(8,128)(2,1)S(1)}, u32[]{:S(2)}, u32[]{:S(2)}) %all-to-all-start) | async-done | bytes 2097184 | tf_op jit(solution)/shard_map/all_to_all | solution.py:28
  54.2 0.6 gather_fusion
  54.8 0.0 copy-start.3
  54.8 0.2 bitcast_select_fusion
  55.0 1.0 copy-done.3
  56.0 3.3 %fusion.4 = f32[512,512]{1,0:T(8,128)} fusion(bf16[1024,512]{1,0:T(8,128)(2,1)S(1)} %bitcast_select_fusion, bf16[64,8,8,128]{3,2,1,0:T(8,128)(2,1)S(1)} %bitcast.67, bf16[1024,512]{1,0:T(8,128)(2,1)} %param.12), kind=kOutput, calls=%fused_computation.12 | convolution fusion | flops 1074266112 | bytes 3670016 | tf_op jit(solution)/shard_map/dot_general | solution.py:65
  59.3 1.2 fusion.37
  60.4 0.0 copy-start.4
  60.4 0.0 copy-start.5
  60.5 0.0 copy-start.6
  60.5 13.6 %collective-permute-start.2 = (f32[128,512]{1,0:T(8,128)S(1)}, f32[128,512]{1,0:T(8,128)S(1)}, u32[]{:S(2)}, u32[]{:S(2)}) collective-permute-start(f32[128,512]{1,0:T(8,128)S(1)} %get-tuple-element.5), channel_id=1, source_target_pairs={{0,3},{1,4},{2,5},{3,6},{4,7},{5,8},{6,9},{7,10},{8,11},{9,12},{10... | collective-permute-start | bytes 786440 | tf_op jit(solution)/shard_map/ppermute | solution.py:15
  74.0 3.3 %collective-permute-start.1 = (f32[128,512]{1,0:T(8,128)S(1)}, f32[128,512]{1,0:T(8,128)S(1)}, u32[]{:S(2)}, u32[]{:S(2)}) collective-permute-start(f32[128,512]{1,0:T(8,128)S(1)} %get-tuple-element.6), channel_id=1, source_target_pairs={{0,2},{1,3},{2,4},{3,5},{4,6},{5,7},{6,8},{7,9},{8,10},{9,11},{10,... | collective-permute-start | bytes 786440 | tf_op jit(solution)/shard_map/ppermute | solution.py:15
  77.4 1.9 collective-permute-start
  79.3 0.6 fusion.10
  79.9 21.7 %collective-permute-done.2 = f32[128,512]{1,0:T(8,128)S(1)} collective-permute-done((f32[128,512]{1,0:T(8,128)S(1)}, f32[128,512]{1,0:T(8,128)S(1)}, u32[]{:S(2)}, u32[]{:S(2)}) %collective-permute-start.2) | collective-permute-done | bytes 262176 | tf_op jit(solution)/shard_map/ppermute | solution.py:15
  101.6 8.0 %collective-permute-done.1 = f32[128,512]{1,0:T(8,128)S(1)} collective-permute-done((f32[128,512]{1,0:T(8,128)S(1)}, f32[128,512]{1,0:T(8,128)S(1)}, u32[]{:S(2)}, u32[]{:S(2)}) %collective-permute-start.1) | collective-permute-done | bytes 262176 | tf_op jit(solution)/shard_map/ppermute | solution.py:15
  109.6 0.0 collective-permute-done
  109.6 0.0 copy-done.4
  109.6 0.0 copy-done.5
  109.6 0.0 copy-done.6
  109.6 1.3 multiply_convert_fusion
  110.9 1.9 collective-permute-start.5
  112.8 5.5 %collective-permute-start.4 = (bf16[128,512]{1,0:T(8,128)(2,1)S(1)}, bf16[128,512]{1,0:T(8,128)(2,1)S(1)}, u32[]{:S(2)}, u32[]{:S(2)}) collective-permute-start(bf16[128,512]{1,0:T(8,128)(2,1)S(1)} %get-tuple-element.2), channel_id=1, source_target_pairs={{0,62},{1,63},{2,0},{3,1},{4,2},{5,3},{6,4},{7,5},{8,6},{9,7},{10,... | collective-permute-start | bytes 393224 | tf_op jit(solution)/shard_map/ppermute | solution.py:15
  118.3 5.2 %collective-permute-start.3 = (bf16[128,512]{1,0:T(8,128)(2,1)S(1)}, bf16[128,512]{1,0:T(8,128)(2,1)S(1)}, u32[]{:S(2)}, u32[]{:S(2)}) collective-permute-start(bf16[128,512]{1,0:T(8,128)(2,1)S(1)} %get-tuple-element.2), channel_id=1, source_target_pairs={{0,63},{1,0},{2,1},{3,2},{4,3},{5,4},{6,5},{7,6},{8,7},{9,8},{10,9... | collective-permute-start | bytes 393224 | tf_op jit(solution)/shard_map/ppermute | solution.py:15
  123.6 1.3 convolution_bitcast_fusion.1
  124.9 0.0 collective-permute-done.5
  124.9 1.6 collective-permute-done.4
  126.5 1.6 collective-permute-done.3
  128.1 0.1 pad_maximum_fusion.1
  128.2 1.6 gather_fusion.1
  129.8 2.1 fusion.2
  131.9 0.0 copy-done.1
  131.9 0.0 copy-start
  131.9 0.8 fusion.3
  132.7 0.4 copy-done
  133.1 0.2 pad_maximum_fusion
  133.3 5.1 %all_to_all.25 = f32[2,512,512]{2,1,0:T(8,128)S(1)} all-to-all(f32[2,512,512]{2,1,0:T(8,128)S(1)} %bitcast.64), channel_id=1, replica_groups=mesh['zlo'=2,'x'=8,'zhi'=4,'y'=8,'core'=2] {'core'}, dimensions={0} | all-to-all | bytes 4194304 | tf_op jit(solution)/shard_map/all_to_all | solution.py:21
  138.4 0.3 reduce_sum.18
  138.6 0.7 reshape.200
  139.3 51.0 %all_to_all.26 = f32[512,1,512]{2,1,0:T(1,128)S(1)} all-to-all(f32[512,1,512]{2,1,0:T(1,128)S(1)} %reshape.200), channel_id=1, replica_groups=mesh['zlo'=2,'x'=8,'zhi'=4,'y'=8,'core'=2] {'zlo','x','zhi','y'}, dimensions={0} | all-to-all | bytes 2097152 | tf_op jit(solution)/shard_map/all_to_all | solution.py:21
  190.3 0.6 reduce_sum.19
  190.9 0.5 broadcast_in_dim.106
  191.5 0.5 broadcast.211
  192.0 3.8 %reduce.1 = bf16[512,512]{1,0:T(8,128)(2,1)S(1)} reduce(bf16[512,1,512]{2,1,0:T(2,128)(2,1)S(1)} %broadcast_in_dim.106, bf16[]{:T(256)} %broadcast.211), dimensions={1}, to_apply=%broadcast_in_dim.106.reduce_sub_computation | reduce | bytes 1048578 | tf_op jit(solution)/shard_map/broadcast_in_dim | solution.py:27
  195.8 0.9 reshape.220
  196.8 15.3 %all-to-all-start.3 = ((bf16[512,2,256]{2,1,0:T(2,128)(2,1)}), bf16[512,2,256]{2,1,0:T(2,128)(2,1)S(1)}, u32[]{:S(2)}, u32[]{:S(2)}) async-start(bf16[512,2,256]{2,1,0:T(2,128)(2,1)} %reshape.220), calls=%async_computation.3 | async-start | bytes 1048576 | tf_op jit(solution)/shard_map/all_to_all | solution.py:28
  212.0 0.7 multiply_convert_fusion.1
  212.8 15.4 %all-to-all-done.3 = bf16[512,2,256]{2,1,0:T(2,128)(2,1)S(1)} async-done(((bf16[512,2,256]{2,1,0:T(2,128)(2,1)}), bf16[512,2,256]{2,1,0:T(2,128)(2,1)S(1)}, u32[]{:S(2)}, u32[]{:S(2)}) %all-to-all-start.3) | async-done | bytes 524320 | tf_op jit(solution)/shard_map/all_to_all | solution.py:28
  228.2 0.4 reshape.221
  228.6 0.1 copy.23
  228.8 0.1 broadcast_in_dim.108
  228.8 9.1 %all_to_all.27 = bf16[2,512,512]{2,1,0:T(8,128)(2,1)S(1)} all-to-all(bf16[2,512,512]{2,1,0:T(8,128)(2,1)S(1)} %broadcast_in_dim.108), channel_id=1, replica_groups=mesh['zlo'=2,'x'=8,'zhi'=4,'y'=8,'core'=2] {'core'}, dimensions={0} | all-to-all | bytes 2097152 | tf_op jit(solution)/shard_map/all_to_all | solution.py:28
  237.9 1.7 bitcast_convert_fusion.4
  (11 shorter events, 0.1 us)
Async XLA Ops:
  3.1 10.9 %copy-start.2 = (bf16[1,8,128,128]{3,2,1,0:T(8,128)(2,1)S(1)}, bf16[1,8,128,128]{3,2,1,0:T(8,128)(2,1)}, u32[]{:S(2)}) copy-start(bf16[1,8,128,128]{3,2,1,0:T(8,128)(2,1)} %param.8) | copy-start | bytes 786436
  3.1 11.1 %copy-start.7 = (s32[1,8]{1,0:T(1,128)S(1)}, s32[1,8]{1,0:T(1,128)}, u32[]{:S(2)}) copy-start(s32[1,8]{1,0:T(1,128)} %param.10) | copy-start | bytes 100
  3.1 11.2 %copy-start.8 = (s32[1,8]{1,0:T(1,128)S(1)}, s32[1,8]{1,0:T(1,128)}, u32[]{:S(2)}) copy-start(s32[1,8]{1,0:T(1,128)} %param.9) | copy-start | bytes 100
  3.1 51.1 %all-to-all-start = ((bf16[16,128,512]{2,1,0:T(8,128)(2,1)}), bf16[16,128,512]{2,1,0:T(8,128)(2,1)S(1)}, u32[]{:S(2)}, u32[]{:S(2)}) async-start(bf16[16,128,512]{2,1,0:T(8,128)(2,1)} %broadcast_in_dim.99), calls=%async_computation | async-start | bytes 4194304 | tf_op jit(solution)/shard_map/all_to_all | solution.py:28
  54.8 1.2 copy-start.3
  60.4 49.2 %copy-start.4 = (bf16[128,512]{1,0:T(8,128)(2,1)S(1)}, bf16[128,512]{1,0:T(8,128)(2,1)}, u32[]{:S(2)}) copy-start(bf16[128,512]{1,0:T(8,128)(2,1)} %param.7) | copy-start | bytes 393220
  60.4 49.1 %copy-start.5 = (bf16[1024,512]{1,0:T(8,128)(2,1)S(1)}, bf16[1024,512]{1,0:T(8,128)(2,1)}, u32[]{:S(2)}) copy-start(bf16[1024,512]{1,0:T(8,128)(2,1)} %param.12) | copy-start | bytes 3145732
  60.5 49.1 %copy-start.6 = (bf16[128,512]{1,0:T(8,128)(2,1)S(1)}, bf16[128,512]{1,0:T(8,128)(2,1)}, u32[]{:S(2)}) copy-start(bf16[128,512]{1,0:T(8,128)(2,1)} %param.13) | copy-start | bytes 393220
  60.5 41.1 %collective-permute-start.2 = (f32[128,512]{1,0:T(8,128)S(1)}, f32[128,512]{1,0:T(8,128)S(1)}, u32[]{:S(2)}, u32[]{:S(2)}) collective-permute-start(f32[128,512]{1,0:T(8,128)S(1)} %get-tuple-element.5), channel_id=1, source_target_pairs={{0,3},{1,4},{2,5},{3,6},{4,7},{5,8},{6,9},{7,10},{8,11},{9,12},{10... | collective-permute-start | bytes 786440 | tf_op jit(solution)/shard_map/ppermute | solution.py:15
  74.0 35.6 %collective-permute-start.1 = (f32[128,512]{1,0:T(8,128)S(1)}, f32[128,512]{1,0:T(8,128)S(1)}, u32[]{:S(2)}, u32[]{:S(2)}) collective-permute-start(f32[128,512]{1,0:T(8,128)S(1)} %get-tuple-element.6), channel_id=1, source_target_pairs={{0,2},{1,3},{2,4},{3,5},{4,6},{5,7},{6,8},{7,9},{8,10},{9,11},{10,... | collective-permute-start | bytes 786440 | tf_op jit(solution)/shard_map/ppermute | solution.py:15
  77.4 32.2 %collective-permute-start = (f32[128,512]{1,0:T(8,128)S(1)}, f32[128,512]{1,0:T(8,128)S(1)}, u32[]{:S(2)}, u32[]{:S(2)}) collective-permute-start(f32[128,512]{1,0:T(8,128)S(1)} %get-tuple-element.4), channel_id=1, source_target_pairs={{0,1},{1,2},{2,3},{3,4},{4,5},{5,6},{6,7},{7,8},{8,9},{9,10},{10,1... | collective-permute-start | bytes 786440 | tf_op jit(solution)/shard_map/ppermute | solution.py:15
  110.9 14.0 %collective-permute-start.5 = (bf16[128,512]{1,0:T(8,128)(2,1)S(1)}, bf16[128,512]{1,0:T(8,128)(2,1)S(1)}, u32[]{:S(2)}, u32[]{:S(2)}) collective-permute-start(bf16[128,512]{1,0:T(8,128)(2,1)S(1)} %get-tuple-element.2), channel_id=1, source_target_pairs={{0,61},{1,62},{2,63},{3,0},{4,1},{5,2},{6,3},{7,4},{8,5},{9,6},{10... | collective-permute-start | bytes 393224 | tf_op jit(solution)/shard_map/ppermute | solution.py:15
  112.8 13.7 %collective-permute-start.4 = (bf16[128,512]{1,0:T(8,128)(2,1)S(1)}, bf16[128,512]{1,0:T(8,128)(2,1)S(1)}, u32[]{:S(2)}, u32[]{:S(2)}) collective-permute-start(bf16[128,512]{1,0:T(8,128)(2,1)S(1)} %get-tuple-element.2), channel_id=1, source_target_pairs={{0,62},{1,63},{2,0},{3,1},{4,2},{5,3},{6,4},{7,5},{8,6},{9,7},{10,... | collective-permute-start | bytes 393224 | tf_op jit(solution)/shard_map/ppermute | solution.py:15
  118.3 9.8 %collective-permute-start.3 = (bf16[128,512]{1,0:T(8,128)(2,1)S(1)}, bf16[128,512]{1,0:T(8,128)(2,1)S(1)}, u32[]{:S(2)}, u32[]{:S(2)}) collective-permute-start(bf16[128,512]{1,0:T(8,128)(2,1)S(1)} %get-tuple-element.2), channel_id=1, source_target_pairs={{0,63},{1,0},{2,1},{3,2},{4,3},{5,4},{6,5},{7,6},{8,7},{9,8},{10,9... | collective-permute-start | bytes 393224 | tf_op jit(solution)/shard_map/ppermute | solution.py:15
  129.8 2.1 copy-start.1
  131.9 1.2 copy-start
  196.8 31.4 %all-to-all-start.3 = ((bf16[512,2,256]{2,1,0:T(2,128)(2,1)}), bf16[512,2,256]{2,1,0:T(2,128)(2,1)S(1)}, u32[]{:S(2)}, u32[]{:S(2)}) async-start(bf16[512,2,256]{2,1,0:T(2,128)(2,1)} %reshape.220), calls=%async_computation.3 | async-start | bytes 1048576 | tf_op jit(solution)/shard_map/all_to_all | solution.py:28

commit v7 on v5

--- a/solution.py
+++ b/solution.py
@@ -40,7 +40,8 @@
 
 
 def gather_row(features):
-    return exchange_gather(features, ROW)
+    part = exchange_gather(features, "x")
+    return exchange_gather(part, "zlo")
 
 
 def body(features, adj_tiles, tile_rows, tile_cols, tile_count, weight, cotangent):

time: 237 us -> 244 us (1.030)
  waiting for transfers between devices: 82.4 us -> 87 us
  starting transfers between devices: 48.7 us -> 52.6 us
    all_to_all x2 -> x3, starting transfers between devices: 17.3 us -> 29.9 us  [exchange_gather(): copies = lax.all_to_all(copies, axes, 0, 0, tiled=True)]
    ppermute x6, starting transfers between devices: 31.5 us -> 22.7 us  [from_behind(): return lax.ppermute(value, COL, pairs)]
    ppermute x6, waiting for transfers between devices: 32.9 us -> 35.7 us  [from_behind(): return lax.ppermute(value, COL, pairs)]
    all_to_all x2 -> x3, waiting for transfers between devices: 49.4 us -> 51.3 us  [exchange_gather(): copies = lax.all_to_all(copies, axes, 0, 0, tiled=True)]
    broadcast_in_dim x5 -> x6, local copies, waits for them, and re-layouts: 3.89 us -> 4.89 us  [exchange_gather(): copies = jnp.broadcast_to(part[None], (peers,) + part.shape)]
  transfers between devices with their start and end apart: 8 -> 9, of which waited for: 6 -> 7; matrix products, arithmetic and copies ran while one was open for 2% -> 2% of each run, Pallas kernels for 0% -> 0%
where the time goes in v7:
time: 244 us; the launch traced here: 243 us
  waiting for transfers between devices  87 us (36%)
  blocking collectives  77 us (32%)
  starting transfers between devices  52.6 us (22%)
  local copies, waits for them, and re-layouts  10.1 us (4%)
  matrix products  9.33 us (4%)
  other arithmetic  5.32 us (2%)
    all_to_all x3, blocking collectives, exchange_sum(): pieces = lax.all_to_all(pieces, axes, 0, 0, tiled=True)  53.7 us
    all_to_all x3, waiting for transfers between devices, exchange_gather(): copies = lax.all_to_all(copies, axes, 0, 0, tiled=True)  51.3 us
    ppermute x6, waiting for transfers between devices, from_behind(): return lax.ppermute(value, COL, pairs)  35.7 us
    all_to_all x3, starting transfers between devices, exchange_gather(): copies = lax.all_to_all(copies, axes, 0, 0, tiled=True)  29.9 us
    all_to_all x2, blocking collectives, exchange_gather(): copies = lax.all_to_all(copies, axes, 0, 0, tiled=True)  23.4 us
    ppermute x6, starting transfers between devices, from_behind(): return lax.ppermute(value, COL, pairs)  22.7 us
    broadcast_in_dim x6, local copies, waits for them, and re-layouts, exchange_gather(): copies = jnp.broadcast_to(part[None], (peers,) + part.shape)  4.89 us
  transfers between devices with their start and end apart: 9, of which 7 were waited for; matrix products, arithmetic and copies ran while one was open for 2% of the time, Pallas kernels for 0%

profile of v7, /device:TPU:1, one launch (start us, length us, event | category | flops | bytes accessed | tf_op | source)
XLA Modules:
  0.0 242.9 jit_solution(16556294481157677787)
XLA Ops:
  0.6 2.0 broadcast_in_dim.113
  2.6 7.3 %all-to-all-start = ((bf16[8,128,512]{2,1,0:T(8,128)(2,1)}), bf16[8,128,512]{2,1,0:T(8,128)(2,1)S(1)}, u32[]{:S(2)}, u32[]{:S(2)}) async-start(bf16[8,128,512]{2,1,0:T(8,128)(2,1)} %broadcast_in_dim.113), calls=%async_computation | async-start | bytes 2097152 | tf_op jit(solution)/shard_map/all_to_all | solution.py:28
  10.6 16.2 %all-to-all-done = bf16[8,128,512]{2,1,0:T(8,128)(2,1)S(1)} async-done(((bf16[8,128,512]{2,1,0:T(8,128)(2,1)}), bf16[8,128,512]{2,1,0:T(8,128)(2,1)S(1)}, u32[]{:S(2)}, u32[]{:S(2)}) %all-to-all-start) | async-done | bytes 1048608 | tf_op jit(solution)/shard_map/all_to_all | solution.py:28
  26.8 1.5 broadcast_in_dim.115
  28.2 16.7 %all-to-all-start.1 = ((bf16[2,1024,512]{2,1,0:T(8,128)(2,1)}), bf16[2,1024,512]{2,1,0:T(8,128)(2,1)S(1)}, u32[]{:S(2)}, u32[]{:S(2)}) async-start(bf16[2,1024,512]{2,1,0:T(8,128)(2,1)} %broadcast_in_dim.115), calls=%async_computation.1 | async-start | bytes 4194304 | tf_op jit(solution)/shard_map/all_to_all | solution.py:28
  45.0 0.0 copy-done.2
  45.0 0.2 copy.15
  45.2 0.0 copy-done.7
  45.2 0.0 copy-done.8
  45.3 0.1 broadcast_bitcast_fusion
  45.4 1.1 broadcast_select_fusion.1
  46.5 24.3 %all-to-all-done.1 = bf16[2,1024,512]{2,1,0:T(8,128)(2,1)S(1)} async-done(((bf16[2,1024,512]{2,1,0:T(8,128)(2,1)}), bf16[2,1024,512]{2,1,0:T(8,128)(2,1)S(1)}, u32[]{:S(2)}, u32[]{:S(2)}) %all-to-all-start.1) | async-done | bytes 2097184 | tf_op jit(solution)/shard_map/all_to_all | solution.py:28
  70.8 0.6 gather_fusion
  71.4 0.0 copy-start.3
  71.4 0.2 bitcast_select_fusion
  71.6 1.0 copy-done.3
  72.6 3.3 %fusion.4 = f32[512,512]{1,0:T(8,128)} fusion(bf16[1024,512]{1,0:T(8,128)(2,1)S(1)} %bitcast_select_fusion, bf16[64,8,8,128]{3,2,1,0:T(8,128)(2,1)S(1)} %bitcast.75, bf16[1024,512]{1,0:T(8,128)(2,1)} %param.12), kind=kOutput, calls=%fused_computation.12 | convolution fusion | flops 1074266112 | bytes 3670016 | tf_op jit(solution)/shard_map/dot_general | solution.py:68
  75.9 1.2 fusion.37
  77.0 0.0 copy-start.4
  77.0 0.0 copy-start.5
  77.1 0.0 copy-start.6
  77.1 5.5 %collective-permute-start.2 = (f32[128,512]{1,0:T(8,128)S(1)}, f32[128,512]{1,0:T(8,128)S(1)}, u32[]{:S(2)}, u32[]{:S(2)}) collective-permute-start(f32[128,512]{1,0:T(8,128)S(1)} %get-tuple-element.5), channel_id=1, source_target_pairs={{0,3},{1,4},{2,5},{3,6},{4,7},{5,8},{6,9},{7,10},{8,11},{9,12},{10... | collective-permute-start | bytes 786440 | tf_op jit(solution)/shard_map/ppermute | solution.py:15
  82.5 3.3 %collective-permute-start.1 = (f32[128,512]{1,0:T(8,128)S(1)}, f32[128,512]{1,0:T(8,128)S(1)}, u32[]{:S(2)}, u32[]{:S(2)}) collective-permute-start(f32[128,512]{1,0:T(8,128)S(1)} %get-tuple-element.6), channel_id=1, source_target_pairs={{0,2},{1,3},{2,4},{3,5},{4,6},{5,7},{6,8},{7,9},{8,10},{9,11},{10,... | collective-permute-start | bytes 786440 | tf_op jit(solution)/shard_map/ppermute | solution.py:15
  85.9 1.9 collective-permute-start
  87.8 0.6 fusion.10
  88.4 25.0 %collective-permute-done.2 = f32[128,512]{1,0:T(8,128)S(1)} collective-permute-done((f32[128,512]{1,0:T(8,128)S(1)}, f32[128,512]{1,0:T(8,128)S(1)}, u32[]{:S(2)}, u32[]{:S(2)}) %collective-permute-start.2) | collective-permute-done | bytes 262176 | tf_op jit(solution)/shard_map/ppermute | solution.py:15
  113.4 7.5 %collective-permute-done.1 = f32[128,512]{1,0:T(8,128)S(1)} collective-permute-done((f32[128,512]{1,0:T(8,128)S(1)}, f32[128,512]{1,0:T(8,128)S(1)}, u32[]{:S(2)}, u32[]{:S(2)}) %collective-permute-start.1) | collective-permute-done | bytes 262176 | tf_op jit(solution)/shard_map/ppermute | solution.py:15
  120.9 0.0 collective-permute-done
  120.9 0.0 copy-done.4
  120.9 0.0 copy-done.5
  120.9 0.0 copy-done.6
  120.9 1.3 multiply_convert_fusion
  122.2 2.3 collective-permute-start.5
  124.5 5.4 %collective-permute-start.4 = (bf16[128,512]{1,0:T(8,128)(2,1)S(1)}, bf16[128,512]{1,0:T(8,128)(2,1)S(1)}, u32[]{:S(2)}, u32[]{:S(2)}) collective-permute-start(bf16[128,512]{1,0:T(8,128)(2,1)S(1)} %get-tuple-element.2), channel_id=1, source_target_pairs={{0,62},{1,63},{2,0},{3,1},{4,2},{5,3},{6,4},{7,5},{8,6},{9,7},{10,... | collective-permute-start | bytes 393224 | tf_op jit(solution)/shard_map/ppermute | solution.py:15
  129.9 4.2 %collective-permute-start.3 = (bf16[128,512]{1,0:T(8,128)(2,1)S(1)}, bf16[128,512]{1,0:T(8,128)(2,1)S(1)}, u32[]{:S(2)}, u32[]{:S(2)}) collective-permute-start(bf16[128,512]{1,0:T(8,128)(2,1)S(1)} %get-tuple-element.2), channel_id=1, source_target_pairs={{0,63},{1,0},{2,1},{3,2},{4,3},{5,4},{6,5},{7,6},{8,7},{9,8},{10,9... | collective-permute-start | bytes 393224 | tf_op jit(solution)/shard_map/ppermute | solution.py:15
  134.1 1.3 convolution_bitcast_fusion.1
  135.4 0.0 collective-permute-done.5
  135.5 1.6 collective-permute-done.4
  137.1 1.6 collective-permute-done.3
  138.7 0.1 pad_maximum_fusion.1
  138.8 1.6 gather_fusion.1
  140.4 2.1 fusion.2
  142.5 0.0 copy-done.1
  142.5 0.0 copy-start
  142.5 0.8 fusion.3
  143.3 0.4 copy-done
  143.7 0.2 pad_maximum_fusion
  143.9 5.6 %all_to_all.40 = f32[2,512,512]{2,1,0:T(8,128)S(1)} all-to-all(f32[2,512,512]{2,1,0:T(8,128)S(1)} %bitcast.69), channel_id=1, replica_groups=mesh['zlo'=2,'x'=8,'zhi'=4,'y'=8,'core'=2] {'core'}, dimensions={0} | all-to-all | bytes 4194304 | tf_op jit(solution)/shard_map/all_to_all | solution.py:21
  149.5 0.3 reduce_sum.27
  149.8 28.3 %all_to_all.41 = f32[16,32,512]{2,1,0:T(8,128)S(1)} all-to-all(f32[16,32,512]{2,1,0:T(8,128)S(1)} %bitcast.72), channel_id=1, replica_groups=mesh['zlo'=2,'x'=8,'zhi'=4,'y'=8,'core'=2] {'zlo','x'}, dimensions={0} | all-to-all | bytes 2097152 | tf_op jit(solution)/shard_map/all_to_all | solution.py:21
  178.1 0.1 reduce_sum.28
  178.2 0.1 copy.17
  178.3 19.7 %all_to_all.42 = f32[32,1,512]{2,1,0:T(1,128)S(1)} all-to-all(f32[32,1,512]{2,1,0:T(1,128)S(1)} %copy.17), channel_id=1, replica_groups=mesh['zlo'=2,'x'=8,'zhi'=4,'y'=8,'core'=2] {'zhi','y'}, dimensions={0} | all-to-all | bytes 131072 | tf_op jit(solution)/shard_map/all_to_all | solution.py:21
  198.0 0.1 reduce_sum.29
  198.1 0.5 broadcast.211
  198.6 0.8 reduce.1
  199.5 14.1 %all_to_all.43 = bf16[32,2,256]{2,1,0:T(2,128)(2,1)S(1)} all-to-all(bf16[32,2,256]{2,1,0:T(2,128)(2,1)S(1)} %reshape.226), channel_id=1, replica_groups=mesh['zlo'=2,'x'=8,'zhi'=4,'y'=8,'core'=2] {'zhi','y'}, dimensions={0} | all-to-all | bytes 65536 | tf_op jit(solution)/shard_map/all_to_all | solution.py:28
  213.6 0.8 broadcast_in_dim.124
  214.4 5.9 %all-to-all-start.6 = ((bf16[16,32,512]{2,1,0:T(8,128)(2,1)}), bf16[16,32,512]{2,1,0:T(8,128)(2,1)S(1)}, u32[]{:S(2)}, u32[]{:S(2)}) async-start(bf16[16,32,512]{2,1,0:T(8,128)(2,1)} %broadcast_in_dim.124), calls=%async_computation.6 | async-start | bytes 1048576 | tf_op jit(solution)/shard_map/all_to_all | solution.py:28
  220.3 0.7 multiply_convert_fusion.1
  221.1 10.8 %all-to-all-done.6 = bf16[16,32,512]{2,1,0:T(8,128)(2,1)S(1)} async-done(((bf16[16,32,512]{2,1,0:T(8,128)(2,1)}), bf16[16,32,512]{2,1,0:T(8,128)(2,1)S(1)}, u32[]{:S(2)}, u32[]{:S(2)}) %all-to-all-start.6) | async-done | bytes 524320 | tf_op jit(solution)/shard_map/all_to_all | solution.py:28
  231.8 0.1 broadcast_in_dim.126
  231.9 9.3 %all_to_all.44 = bf16[2,512,512]{2,1,0:T(8,128)(2,1)S(1)} all-to-all(bf16[2,512,512]{2,1,0:T(8,128)(2,1)S(1)} %broadcast_in_dim.126), channel_id=1, replica_groups=mesh['zlo'=2,'x'=8,'zhi'=4,'y'=8,'core'=2] {'core'}, dimensions={0} | all-to-all | bytes 2097152 | tf_op jit(solution)/shard_map/all_to_all | solution.py:28
  241.2 1.7 bitcast_convert_fusion.4
  (18 shorter events, 0.2 us)
Async XLA Ops:
  2.6 24.2 %all-to-all-start = ((bf16[8,128,512]{2,1,0:T(8,128)(2,1)}), bf16[8,128,512]{2,1,0:T(8,128)(2,1)S(1)}, u32[]{:S(2)}, u32[]{:S(2)}) async-start(bf16[8,128,512]{2,1,0:T(8,128)(2,1)} %broadcast_in_dim.113), calls=%async_computation | async-start | bytes 2097152 | tf_op jit(solution)/shard_map/all_to_all | solution.py:28
  28.2 16.7 %copy-start.2 = (bf16[1,8,128,128]{3,2,1,0:T(8,128)(2,1)S(1)}, bf16[1,8,128,128]{3,2,1,0:T(8,128)(2,1)}, u32[]{:S(2)}) copy-start(bf16[1,8,128,128]{3,2,1,0:T(8,128)(2,1)} %param.8) | copy-start | bytes 786436
  28.2 16.9 %copy-start.7 = (s32[1,8]{1,0:T(1,128)S(1)}, s32[1,8]{1,0:T(1,128)}, u32[]{:S(2)}) copy-start(s32[1,8]{1,0:T(1,128)} %param.10) | copy-start | bytes 100
  28.2 17.0 %copy-start.8 = (s32[1,8]{1,0:T(1,128)S(1)}, s32[1,8]{1,0:T(1,128)}, u32[]{:S(2)}) copy-start(s32[1,8]{1,0:T(1,128)} %param.9) | copy-start | bytes 100
  28.2 42.5 %all-to-all-start.1 = ((bf16[2,1024,512]{2,1,0:T(8,128)(2,1)}), bf16[2,1024,512]{2,1,0:T(8,128)(2,1)S(1)}, u32[]{:S(2)}, u32[]{:S(2)}) async-start(bf16[2,1024,512]{2,1,0:T(8,128)(2,1)} %broadcast_in_dim.115), calls=%async_computation.1 | async-start | bytes 4194304 | tf_op jit(solution)/shard_map/all_to_all | solution.py:28
  71.4 1.2 copy-start.3
  77.0 43.9 %copy-start.4 = (bf16[128,512]{1,0:T(8,128)(2,1)S(1)}, bf16[128,512]{1,0:T(8,128)(2,1)}, u32[]{:S(2)}) copy-start(bf16[128,512]{1,0:T(8,128)(2,1)} %param.7) | copy-start | bytes 393220
  77.0 43.8 %copy-start.5 = (bf16[1024,512]{1,0:T(8,128)(2,1)S(1)}, bf16[1024,512]{1,0:T(8,128)(2,1)}, u32[]{:S(2)}) copy-start(bf16[1024,512]{1,0:T(8,128)(2,1)} %param.12) | copy-start | bytes 3145732
  77.1 43.8 %copy-start.6 = (bf16[128,512]{1,0:T(8,128)(2,1)S(1)}, bf16[128,512]{1,0:T(8,128)(2,1)}, u32[]{:S(2)}) copy-start(bf16[128,512]{1,0:T(8,128)(2,1)} %param.13) | copy-start | bytes 393220
  77.1 36.3 %collective-permute-start.2 = (f32[128,512]{1,0:T(8,128)S(1)}, f32[128,512]{1,0:T(8,128)S(1)}, u32[]{:S(2)}, u32[]{:S(2)}) collective-permute-start(f32[128,512]{1,0:T(8,128)S(1)} %get-tuple-element.5), channel_id=1, source_target_pairs={{0,3},{1,4},{2,5},{3,6},{4,7},{5,8},{6,9},{7,10},{8,11},{9,12},{10... | collective-permute-start | bytes 786440 | tf_op jit(solution)/shard_map/ppermute | solution.py:15
  82.5 38.3 %collective-permute-start.1 = (f32[128,512]{1,0:T(8,128)S(1)}, f32[128,512]{1,0:T(8,128)S(1)}, u32[]{:S(2)}, u32[]{:S(2)}) collective-permute-start(f32[128,512]{1,0:T(8,128)S(1)} %get-tuple-element.6), channel_id=1, source_target_pairs={{0,2},{1,3},{2,4},{3,5},{4,6},{5,7},{6,8},{7,9},{8,10},{9,11},{10,... | collective-permute-start | bytes 786440 | tf_op jit(solution)/shard_map/ppermute | solution.py:15
  85.9 35.0 %collective-permute-start = (f32[128,512]{1,0:T(8,128)S(1)}, f32[128,512]{1,0:T(8,128)S(1)}, u32[]{:S(2)}, u32[]{:S(2)}) collective-permute-start(f32[128,512]{1,0:T(8,128)S(1)} %get-tuple-element.4), channel_id=1, source_target_pairs={{0,1},{1,2},{2,3},{3,4},{4,5},{5,6},{6,7},{7,8},{8,9},{9,10},{10,1... | collective-permute-start | bytes 786440 | tf_op jit(solution)/shard_map/ppermute | solution.py:15
  122.2 13.3 %collective-permute-start.5 = (bf16[128,512]{1,0:T(8,128)(2,1)S(1)}, bf16[128,512]{1,0:T(8,128)(2,1)S(1)}, u32[]{:S(2)}, u32[]{:S(2)}) collective-permute-start(bf16[128,512]{1,0:T(8,128)(2,1)S(1)} %get-tuple-element.2), channel_id=1, source_target_pairs={{0,61},{1,62},{2,63},{3,0},{4,1},{5,2},{6,3},{7,4},{8,5},{9,6},{10... | collective-permute-start | bytes 393224 | tf_op jit(solution)/shard_map/ppermute | solution.py:15
  124.5 12.6 %collective-permute-start.4 = (bf16[128,512]{1,0:T(8,128)(2,1)S(1)}, bf16[128,512]{1,0:T(8,128)(2,1)S(1)}, u32[]{:S(2)}, u32[]{:S(2)}) collective-permute-start(bf16[128,512]{1,0:T(8,128)(2,1)S(1)} %get-tuple-element.2), channel_id=1, source_target_pairs={{0,62},{1,63},{2,0},{3,1},{4,2},{5,3},{6,4},{7,5},{8,6},{9,7},{10,... | collective-permute-start | bytes 393224 | tf_op jit(solution)/shard_map/ppermute | solution.py:15
  129.9 8.8 %collective-permute-start.3 = (bf16[128,512]{1,0:T(8,128)(2,1)S(1)}, bf16[128,512]{1,0:T(8,128)(2,1)S(1)}, u32[]{:S(2)}, u32[]{:S(2)}) collective-permute-start(bf16[128,512]{1,0:T(8,128)(2,1)S(1)} %get-tuple-element.2), channel_id=1, source_target_pairs={{0,63},{1,0},{2,1},{3,2},{4,3},{5,4},{6,5},{7,6},{8,7},{9,8},{10,9... | collective-permute-start | bytes 393224 | tf_op jit(solution)/shard_map/ppermute | solution.py:15
  140.4 2.1 copy-start.1
  142.5 1.2 copy-start
  214.4 17.4 %all-to-all-start.6 = ((bf16[16,32,512]{2,1,0:T(8,128)(2,1)}), bf16[16,32,512]{2,1,0:T(8,128)(2,1)S(1)}, u32[]{:S(2)}, u32[]{:S(2)}) async-start(bf16[16,32,512]{2,1,0:T(8,128)(2,1)} %broadcast_in_dim.124), calls=%async_computation.6 | async-start | bytes 1048576 | tf_op jit(solution)/shard_map/all_to_all | solution.py:28

commit v8 on v5

--- a/solution.py
+++ b/solution.py
@@ -66,9 +66,9 @@
     placed = placed.transpose(0, 2, 1, 3).reshape(REACH * tile_size, slots * tile_size)
     stacked_sums = jnp.dot(placed, projected, preferred_element_type=jnp.float32)
     stacked_sums = stacked_sums.reshape(REACH, tile_size, width)
-    neighbour = stacked_sums[0]
-    for step in range(1, REACH):
-        neighbour = neighbour + from_behind(stacked_sums[step], step)
+    first = from_behind(jnp.stack([stacked_sums[1], stacked_sums[3]]), 1)
+    second = from_behind(first[1] + stacked_sums[2], 2)
+    neighbour = stacked_sums[0] + first[0] + second
 
     pre_act = jnp.dot(features, w_self, preferred_element_type=jnp.float32) + neighbour
     hidden = jax.nn.silu(pre_act).astype(jnp.bfloat16)

time: 237 us -> 231 us (0.975)
  waiting for transfers between devices: 82.4 us -> 79.3 us
    ppermute x6 -> x5, waiting for transfers between devices: 32.9 us -> 29.8 us  [from_behind(): return lax.ppermute(value, COL, pairs)]
    ppermute x6 -> x5, starting transfers between devices: 31.5 us -> 31.2 us  [from_behind(): return lax.ppermute(value, COL, pairs)]
  transfers between devices with their start and end apart: 8 -> 7, of which waited for: 6 -> 6; matrix products, arithmetic and copies ran while one was open for 2% -> 2% of each run, Pallas kernels for 0% -> 0%
where the time goes in v8:
time: 231 us; the launch traced here: 230 us
  waiting for transfers between devices  79.3 us (34%)
  blocking collectives  78.9 us (34%)
  starting transfers between devices  48.5 us (21%)
  matrix products  7.59 us (3%)
  other arithmetic  7.44 us (3%)
  local copies, waits for them, and re-layouts  7.14 us (3%)
    all_to_all x3, blocking collectives, exchange_sum(): pieces = lax.all_to_all(pieces, axes, 0, 0, tiled=True)  55.5 us
    all_to_all x2, waiting for transfers between devices, exchange_gather(): copies = lax.all_to_all(copies, axes, 0, 0, tiled=True)  49.5 us
    ppermute x5, starting transfers between devices, from_behind(): return lax.ppermute(value, COL, pairs)  31.2 us
    ppermute x5, waiting for transfers between devices, from_behind(): return lax.ppermute(value, COL, pairs)  29.8 us
    all_to_all x2, blocking collectives, exchange_gather(): copies = lax.all_to_all(copies, axes, 0, 0, tiled=True)  23.4 us
    all_to_all x2, starting transfers between devices, exchange_gather(): copies = lax.all_to_all(copies, axes, 0, 0, tiled=True)  17.3 us
  transfers between devices with their start and end apart: 7, of which 6 were waited for; matrix products, arithmetic and copies ran while one was open for 2% of the time, Pallas kernels for 0%

profile of v8, /device:TPU:1, one launch (start us, length us, event | category | flops | bytes accessed | tf_op | source)
XLA Modules:
  0.0 230.5 jit_solution(11398098628866917130)
XLA Ops:
  0.6 2.4 %broadcast_in_dim.106 = bf16[16,128,512]{2,1,0:T(8,128)(2,1)} broadcast(bf16[128,512]{1,0:T(8,128)(2,1)} %param.7), dimensions={1,2} | broadcast | bytes 2228224 | tf_op jit(solution)/shard_map/broadcast_in_dim | solution.py:27
  3.1 0.0 copy-start.3
  3.1 0.0 copy-start.8
  3.1 0.0 copy-start.9
  3.1 10.3 %all-to-all-start = ((bf16[16,128,512]{2,1,0:T(8,128)(2,1)}), bf16[16,128,512]{2,1,0:T(8,128)(2,1)S(1)}, u32[]{:S(2)}, u32[]{:S(2)}) async-start(bf16[16,128,512]{2,1,0:T(8,128)(2,1)} %broadcast_in_dim.106), calls=%async_computation | async-start | bytes 4194304 | tf_op jit(solution)/shard_map/all_to_all | solution.py:28
  14.0 0.0 copy-done.3
  14.0 0.2 copy.15
  14.2 0.0 copy-done.8
  14.3 0.0 copy-done.9
  14.3 0.1 broadcast_bitcast_fusion
  14.4 1.1 broadcast_select_fusion.1
  15.5 38.7 %all-to-all-done = bf16[16,128,512]{2,1,0:T(8,128)(2,1)S(1)} async-done(((bf16[16,128,512]{2,1,0:T(8,128)(2,1)}), bf16[16,128,512]{2,1,0:T(8,128)(2,1)S(1)}, u32[]{:S(2)}, u32[]{:S(2)}) %all-to-all-start) | async-done | bytes 2097184 | tf_op jit(solution)/shard_map/all_to_all | solution.py:28
  54.2 0.6 gather_fusion
  54.8 0.0 copy-start.4
  54.8 1.2 bitcast_select_fusion
  56.0 0.2 copy-done.4
  56.2 2.6 %fusion.4 = f32[512,512]{1,0:T(8,128)S(1)} fusion(bf16[1024,512]{1,0:T(8,128)(2,1)} %bitcast_select_fusion, bf16[64,8,8,128]{3,2,1,0:T(8,128)(2,1)S(1)} %bitcast.89, bf16[1024,512]{1,0:T(8,128)(2,1)} %param.12), kind=kOutput, calls=%fused_computation.12 | convolution fusion | flops 1074266112 | bytes 3670016 | tf_op jit(solution)/shard_map/dot_general | solution.py:67
  58.8 0.0 copy-start.5
  58.8 0.0 copy-start.2
  58.8 0.0 copy-start.6
  58.9 12.4 %collective-permute-start = (f32[2,128,512]{2,1,0:T(8,128)S(1)}, f32[2,128,512]{2,1,0:T(8,128)S(1)}, u32[]{:S(2)}, u32[]{:S(2)}) collective-permute-start(f32[2,128,512]{2,1,0:T(8,128)S(1)} %pad_maximum_fusion.1), channel_id=1, source_target_pairs={{0,1},{1,2},{2,3},{3,4},{4,5},{5,6},{6,7},{7,8},{8,9},{9,10},{10,1... | collective-permute-start | bytes 1572872 | tf_op jit(solution)/shard_map/ppermute | solution.py:15
  71.4 0.0 copy-done.2
  71.4 0.0 copy-done.6
  71.4 0.2 fusion.18
  71.6 0.0 copy-start.7
  71.6 5.8 %collective-permute-done = f32[2,128,512]{2,1,0:T(8,128)S(1)} collective-permute-done((f32[2,128,512]{2,1,0:T(8,128)S(1)}, f32[2,128,512]{2,1,0:T(8,128)S(1)}, u32[]{:S(2)}, u32[]{:S(2)}) %collective-permute-start) | collective-permute-done | bytes 524320 | tf_op jit(solution)/shard_map/ppermute | solution.py:15
  77.5 0.0 copy-done.5
  77.5 3.3 %collective-permute-start.1 = (f32[128,512]{1,0:T(8,128)S(1)}, f32[128,512]{1,0:T(8,128)S(1)}, u32[]{:S(2)}, u32[]{:S(2)}) collective-permute-start(f32[128,512]{1,0:T(8,128)S(1)} %slice_add_fusion), channel_id=1, source_target_pairs={{0,2},{1,3},{2,4},{3,5},{4,6},{5,7},{6,8},{7,9},{8,10},{9,11},{10,... | collective-permute-start | bytes 786440 | tf_op jit(solution)/shard_map/ppermute | solution.py:15
  80.8 0.6 fusion.10
  81.4 20.7 %collective-permute-done.1 = f32[128,512]{1,0:T(8,128)S(1)} collective-permute-done((f32[128,512]{1,0:T(8,128)S(1)}, f32[128,512]{1,0:T(8,128)S(1)}, u32[]{:S(2)}, u32[]{:S(2)}) %collective-permute-start.1) | collective-permute-done | bytes 262176 | tf_op jit(solution)/shard_map/ppermute | solution.py:15
  102.2 0.0 copy-done.7
  102.2 1.1 multiply_convert_fusion
  103.3 8.7 %collective-permute-start.4 = (bf16[128,512]{1,0:T(8,128)(2,1)S(1)}, bf16[128,512]{1,0:T(8,128)(2,1)S(1)}, u32[]{:S(2)}, u32[]{:S(2)}) collective-permute-start(bf16[128,512]{1,0:T(8,128)(2,1)S(1)} %get-tuple-element.2), channel_id=1, source_target_pairs={{0,61},{1,62},{2,63},{3,0},{4,1},{5,2},{6,3},{7,4},{8,5},{9,6},{10... | collective-permute-start | bytes 393224 | tf_op jit(solution)/shard_map/ppermute | solution.py:15
  112.0 1.9 collective-permute-start.3
  113.9 4.9 %collective-permute-start.2 = (bf16[128,512]{1,0:T(8,128)(2,1)S(1)}, bf16[128,512]{1,0:T(8,128)(2,1)S(1)}, u32[]{:S(2)}, u32[]{:S(2)}) collective-permute-start(bf16[128,512]{1,0:T(8,128)(2,1)S(1)} %get-tuple-element.2), channel_id=1, source_target_pairs={{0,63},{1,0},{2,1},{3,2},{4,3},{5,4},{6,5},{7,6},{8,7},{9,8},{10,9... | collective-permute-start | bytes 393224 | tf_op jit(solution)/shard_map/ppermute | solution.py:15
  118.8 1.3 convolution_bitcast_fusion.1
  120.1 0.0 collective-permute-done.4
  120.1 1.6 collective-permute-done.3
  121.7 1.6 collective-permute-done.2
  123.3 0.1 pad_maximum_fusion.2
  123.4 1.6 gather_fusion.1
  125.0 2.1 fusion.2
  127.1 0.0 copy-done.1
  127.1 0.0 copy-start
  127.1 0.8 fusion.3
  127.9 0.4 copy-done
  128.3 0.2 pad_maximum_fusion
  128.5 5.1 %all_to_all.35 = f32[2,512,512]{2,1,0:T(8,128)S(1)} all-to-all(f32[2,512,512]{2,1,0:T(8,128)S(1)} %bitcast.84), channel_id=1, replica_groups=mesh['zlo'=2,'x'=8,'zhi'=4,'y'=8,'core'=2] {'core'}, dimensions={0} | all-to-all | bytes 4194304 | tf_op jit(solution)/shard_map/all_to_all | solution.py:21
  133.5 0.3 reduce_sum.27
  133.8 30.9 %all_to_all.36 = f32[16,32,512]{2,1,0:T(8,128)S(1)} all-to-all(f32[16,32,512]{2,1,0:T(8,128)S(1)} %bitcast.85), channel_id=1, replica_groups=mesh['zlo'=2,'x'=8,'zhi'=4,'y'=8,'core'=2] {'zlo','x'}, dimensions={0} | all-to-all | bytes 2097152 | tf_op jit(solution)/shard_map/all_to_all | solution.py:21
  164.7 0.1 reduce_sum.28
  164.8 0.1 copy.17
  164.9 19.5 %all_to_all.37 = f32[32,1,512]{2,1,0:T(1,128)S(1)} all-to-all(f32[32,1,512]{2,1,0:T(1,128)S(1)} %copy.17), channel_id=1, replica_groups=mesh['zlo'=2,'x'=8,'zhi'=4,'y'=8,'core'=2] {'zhi','y'}, dimensions={0} | all-to-all | bytes 131072 | tf_op jit(solution)/shard_map/all_to_all | solution.py:21
  184.4 0.1 reduce_sum.29
  184.6 0.5 broadcast.211
  185.1 0.8 reduce.1
  185.9 14.1 %all_to_all.38 = bf16[32,2,256]{2,1,0:T(2,128)(2,1)S(1)} all-to-all(bf16[32,2,256]{2,1,0:T(2,128)(2,1)S(1)} %reshape.223), channel_id=1, replica_groups=mesh['zlo'=2,'x'=8,'zhi'=4,'y'=8,'core'=2] {'zhi','y'}, dimensions={0} | all-to-all | bytes 65536 | tf_op jit(solution)/shard_map/all_to_all | solution.py:28
  200.0 0.8 broadcast_in_dim.115
  200.9 7.0 %all-to-all-start.5 = ((bf16[16,32,512]{2,1,0:T(8,128)(2,1)}), bf16[16,32,512]{2,1,0:T(8,128)(2,1)S(1)}, u32[]{:S(2)}, u32[]{:S(2)}) async-start(bf16[16,32,512]{2,1,0:T(8,128)(2,1)} %broadcast_in_dim.115), calls=%async_computation.5 | async-start | bytes 1048576 | tf_op jit(solution)/shard_map/all_to_all | solution.py:28
  207.9 0.7 multiply_convert_fusion.1
  208.6 10.8 %all-to-all-done.5 = bf16[16,32,512]{2,1,0:T(8,128)(2,1)S(1)} async-done(((bf16[16,32,512]{2,1,0:T(8,128)(2,1)}), bf16[16,32,512]{2,1,0:T(8,128)(2,1)S(1)}, u32[]{:S(2)}, u32[]{:S(2)}) %all-to-all-start.5) | async-done | bytes 524320 | tf_op jit(solution)/shard_map/all_to_all | solution.py:28
  219.4 0.1 broadcast_in_dim.117
  219.5 9.3 %all_to_all.39 = bf16[2,512,512]{2,1,0:T(8,128)(2,1)S(1)} all-to-all(bf16[2,512,512]{2,1,0:T(8,128)(2,1)S(1)} %broadcast_in_dim.117), channel_id=1, replica_groups=mesh['zlo'=2,'x'=8,'zhi'=4,'y'=8,'core'=2] {'core'}, dimensions={0} | all-to-all | bytes 2097152 | tf_op jit(solution)/shard_map/all_to_all | solution.py:28
  228.8 1.7 bitcast_convert_fusion.4
  (18 shorter events, 0.3 us)
Async XLA Ops:
  3.1 10.9 %copy-start.3 = (bf16[1,8,128,128]{3,2,1,0:T(8,128)(2,1)S(1)}, bf16[1,8,128,128]{3,2,1,0:T(8,128)(2,1)}, u32[]{:S(2)}) copy-start(bf16[1,8,128,128]{3,2,1,0:T(8,128)(2,1)} %param.8) | copy-start | bytes 786436
  3.1 11.1 %copy-start.8 = (s32[1,8]{1,0:T(1,128)S(1)}, s32[1,8]{1,0:T(1,128)}, u32[]{:S(2)}) copy-start(s32[1,8]{1,0:T(1,128)} %param.10) | copy-start | bytes 100
  3.1 11.2 %copy-start.9 = (s32[1,8]{1,0:T(1,128)S(1)}, s32[1,8]{1,0:T(1,128)}, u32[]{:S(2)}) copy-start(s32[1,8]{1,0:T(1,128)} %param.9) | copy-start | bytes 100
  3.1 51.1 %all-to-all-start = ((bf16[16,128,512]{2,1,0:T(8,128)(2,1)}), bf16[16,128,512]{2,1,0:T(8,128)(2,1)S(1)}, u32[]{:S(2)}, u32[]{:S(2)}) async-start(bf16[16,128,512]{2,1,0:T(8,128)(2,1)} %broadcast_in_dim.106), calls=%async_computation | async-start | bytes 4194304 | tf_op jit(solution)/shard_map/all_to_all | solution.py:28
  54.8 1.4 copy-start.4
  58.8 18.7 %copy-start.5 = (f32[512,512]{1,0:T(8,128)}, f32[512,512]{1,0:T(8,128)S(1)}, u32[]{:S(2)}) copy-start(f32[512,512]{1,0:T(8,128)S(1)} %fusion.4) | copy-start | bytes 3145732
  58.8 12.6 %copy-start.2 = (bf16[128,512]{1,0:T(8,128)(2,1)S(1)}, bf16[128,512]{1,0:T(8,128)(2,1)}, u32[]{:S(2)}) copy-start(bf16[128,512]{1,0:T(8,128)(2,1)} %param.7) | copy-start | bytes 393220
  58.8 12.6 %copy-start.6 = (bf16[1024,512]{1,0:T(8,128)(2,1)S(1)}, bf16[1024,512]{1,0:T(8,128)(2,1)}, u32[]{:S(2)}) copy-start(bf16[1024,512]{1,0:T(8,128)(2,1)} %param.12) | copy-start | bytes 3145732
  58.9 18.5 %collective-permute-start = (f32[2,128,512]{2,1,0:T(8,128)S(1)}, f32[2,128,512]{2,1,0:T(8,128)S(1)}, u32[]{:S(2)}, u32[]{:S(2)}) collective-permute-start(f32[2,128,512]{2,1,0:T(8,128)S(1)} %pad_maximum_fusion.1), channel_id=1, source_target_pairs={{0,1},{1,2},{2,3},{3,4},{4,5},{5,6},{6,7},{7,8},{8,9},{9,10},{10,1... | collective-permute-start | bytes 1572872 | tf_op jit(solution)/shard_map/ppermute | solution.py:15
  71.6 30.5 %copy-start.7 = (bf16[128,512]{1,0:T(8,128)(2,1)S(1)}, bf16[128,512]{1,0:T(8,128)(2,1)}, u32[]{:S(2)}) copy-start(bf16[128,512]{1,0:T(8,128)(2,1)} %param.13) | copy-start | bytes 393220
  77.5 24.7 %collective-permute-start.1 = (f32[128,512]{1,0:T(8,128)S(1)}, f32[128,512]{1,0:T(8,128)S(1)}, u32[]{:S(2)}, u32[]{:S(2)}) collective-permute-start(f32[128,512]{1,0:T(8,128)S(1)} %slice_add_fusion), channel_id=1, source_target_pairs={{0,2},{1,3},{2,4},{3,5},{4,6},{5,7},{6,8},{7,9},{8,10},{9,11},{10,... | collective-permute-start | bytes 786440 | tf_op jit(solution)/shard_map/ppermute | solution.py:15
  103.3 16.8 %collective-permute-start.4 = (bf16[128,512]{1,0:T(8,128)(2,1)S(1)}, bf16[128,512]{1,0:T(8,128)(2,1)S(1)}, u32[]{:S(2)}, u32[]{:S(2)}) collective-permute-start(bf16[128,512]{1,0:T(8,128)(2,1)S(1)} %get-tuple-element.2), channel_id=1, source_target_pairs={{0,61},{1,62},{2,63},{3,0},{4,1},{5,2},{6,3},{7,4},{8,5},{9,6},{10... | collective-permute-start | bytes 393224 | tf_op jit(solution)/shard_map/ppermute | solution.py:15
  112.0 9.7 %collective-permute-start.3 = (bf16[128,512]{1,0:T(8,128)(2,1)S(1)}, bf16[128,512]{1,0:T(8,128)(2,1)S(1)}, u32[]{:S(2)}, u32[]{:S(2)}) collective-permute-start(bf16[128,512]{1,0:T(8,128)(2,1)S(1)} %get-tuple-element.2), channel_id=1, source_target_pairs={{0,62},{1,63},{2,0},{3,1},{4,2},{5,3},{6,4},{7,5},{8,6},{9,7},{10,... | collective-permute-start | bytes 393224 | tf_op jit(solution)/shard_map/ppermute | solution.py:15
  113.9 9.4 %collective-permute-start.2 = (bf16[128,512]{1,0:T(8,128)(2,1)S(1)}, bf16[128,512]{1,0:T(8,128)(2,1)S(1)}, u32[]{:S(2)}, u32[]{:S(2)}) collective-permute-start(bf16[128,512]{1,0:T(8,128)(2,1)S(1)} %get-tuple-element.2), channel_id=1, source_target_pairs={{0,63},{1,0},{2,1},{3,2},{4,3},{5,4},{6,5},{7,6},{8,7},{9,8},{10,9... | collective-permute-start | bytes 393224 | tf_op jit(solution)/shard_map/ppermute | solution.py:15
  125.0 2.1 copy-start.1
  127.1 1.2 copy-start
  200.9 18.5 %all-to-all-start.5 = ((bf16[16,32,512]{2,1,0:T(8,128)(2,1)}), bf16[16,32,512]{2,1,0:T(8,128)(2,1)S(1)}, u32[]{:S(2)}, u32[]{:S(2)}) async-start(bf16[16,32,512]{2,1,0:T(8,128)(2,1)} %broadcast_in_dim.115), calls=%async_computation.5 | async-start | bytes 1048576 | tf_op jit(solution)/shard_map/all_to_all | solution.py:28

commit v9 on v8

--- a/solution.py
+++ b/solution.py
@@ -31,11 +31,11 @@
 
 def reduce_all(stacked, scale):
     part = exchange_sum(stacked, "core")
+    part = exchange_sum(part, ("zhi", "y"))
     part = exchange_sum(part, ROW)
-    part = exchange_sum(part, ("zhi", "y"))
     part = (part * scale).astype(jnp.bfloat16)
+    part = exchange_gather(part, ROW)
     part = exchange_gather(part, ("zhi", "y"))
-    part = exchange_gather(part, ROW)
     return exchange_gather(part, "core").astype(jnp.float32)
 
 

time: 231 us -> 232 us (level)
  blocking collectives: 78.9 us -> 74 us
  waiting for transfers between devices: 79.3 us -> 82.3 us
  starting transfers between devices: 48.5 us -> 51.3 us
    all_to_all x2, blocking collectives: 23.4 us -> 19.8 us  [exchange_gather(): copies = lax.all_to_all(copies, axes, 0, 0, tiled=True)]
    all_to_all x2, waiting for transfers between devices: 49.5 us -> 52.5 us  [exchange_gather(): copies = lax.all_to_all(copies, axes, 0, 0, tiled=True)]
    all_to_all x2, starting transfers between devices: 17.3 us -> 20.1 us  [exchange_gather(): copies = lax.all_to_all(copies, axes, 0, 0, tiled=True)]
where the time goes in v9:
time: 232 us; the launch traced here: 231 us
  waiting for transfers between devices  82.3 us (35%)
  blocking collectives  74 us (32%)
  starting transfers between devices  51.3 us (22%)
  matrix products  7.59 us (3%)
  other arithmetic  7.33 us (3%)
  local copies, waits for them, and re-layouts  7.09 us (3%)
    all_to_all x3, blocking collectives, exchange_sum(): pieces = lax.all_to_all(pieces, axes, 0, 0, tiled=True)  54.3 us
    all_to_all x2, waiting for transfers between devices, exchange_gather(): copies = lax.all_to_all(copies, axes, 0, 0, tiled=True)  52.5 us
    ppermute x5, starting transfers between devices, from_behind(): return lax.ppermute(value, COL, pairs)  31.2 us
    ppermute x5, waiting for transfers between devices, from_behind(): return lax.ppermute(value, COL, pairs)  29.8 us
    all_to_all x2, starting transfers between devices, exchange_gather(): copies = lax.all_to_all(copies, axes, 0, 0, tiled=True)  20.1 us
    all_to_all x2, blocking collectives, exchange_gather(): copies = lax.all_to_all(copies, axes, 0, 0, tiled=True)  19.8 us
  transfers between devices with their start and end apart: 7, of which 6 were waited for; matrix products, arithmetic and copies ran while one was open for 2% of the time, Pallas kernels for 0%

profile of v9, /device:TPU:1, one launch (start us, length us, event | category | flops | bytes accessed | tf_op | source)
XLA Modules:
  0.0 231.3 jit_solution(10479725146854861726)
XLA Ops:
  0.6 2.4 %broadcast_in_dim.106 = bf16[16,128,512]{2,1,0:T(8,128)(2,1)} broadcast(bf16[128,512]{1,0:T(8,128)(2,1)} %param.7), dimensions={1,2} | broadcast | bytes 2228224 | tf_op jit(solution)/shard_map/broadcast_in_dim | solution.py:27
  3.1 0.0 copy-start.3
  3.1 0.0 copy-start.8
  3.1 0.0 copy-start.9
  3.1 10.3 %all-to-all-start = ((bf16[16,128,512]{2,1,0:T(8,128)(2,1)}), bf16[16,128,512]{2,1,0:T(8,128)(2,1)S(1)}, u32[]{:S(2)}, u32[]{:S(2)}) async-start(bf16[16,128,512]{2,1,0:T(8,128)(2,1)} %broadcast_in_dim.106), calls=%async_computation | async-start | bytes 4194304 | tf_op jit(solution)/shard_map/all_to_all | solution.py:28
  14.0 0.0 copy-done.3
  14.0 0.2 copy.15
  14.2 0.0 copy-done.8
  14.3 0.0 copy-done.9
  14.3 0.1 broadcast_bitcast_fusion
  14.4 1.1 broadcast_select_fusion.1
  15.5 38.7 %all-to-all-done = bf16[16,128,512]{2,1,0:T(8,128)(2,1)S(1)} async-done(((bf16[16,128,512]{2,1,0:T(8,128)(2,1)}), bf16[16,128,512]{2,1,0:T(8,128)(2,1)S(1)}, u32[]{:S(2)}, u32[]{:S(2)}) %all-to-all-start) | async-done | bytes 2097184 | tf_op jit(solution)/shard_map/all_to_all | solution.py:28
  54.2 0.6 gather_fusion
  54.8 0.0 copy-start.4
  54.8 1.2 bitcast_select_fusion
  56.0 0.2 copy-done.4
  56.2 2.6 %fusion.4 = f32[512,512]{1,0:T(8,128)S(1)} fusion(bf16[1024,512]{1,0:T(8,128)(2,1)} %bitcast_select_fusion, bf16[64,8,8,128]{3,2,1,0:T(8,128)(2,1)S(1)} %bitcast.89, bf16[1024,512]{1,0:T(8,128)(2,1)} %param.12), kind=kOutput, calls=%fused_computation.12 | convolution fusion | flops 1074266112 | bytes 3670016 | tf_op jit(solution)/shard_map/dot_general | solution.py:67
  58.8 0.0 copy-start.5
  58.8 0.0 copy-start.2
  58.8 0.0 copy-start.6
  58.9 12.4 %collective-permute-start = (f32[2,128,512]{2,1,0:T(8,128)S(1)}, f32[2,128,512]{2,1,0:T(8,128)S(1)}, u32[]{:S(2)}, u32[]{:S(2)}) collective-permute-start(f32[2,128,512]{2,1,0:T(8,128)S(1)} %pad_maximum_fusion.1), channel_id=1, source_target_pairs={{0,1},{1,2},{2,3},{3,4},{4,5},{5,6},{6,7},{7,8},{8,9},{9,10},{10,1... | collective-permute-start | bytes 1572872 | tf_op jit(solution)/shard_map/ppermute | solution.py:15
  71.4 0.0 copy-done.2
  71.4 0.0 copy-done.6
  71.4 0.2 fusion.18
  71.6 0.0 copy-start.7
  71.6 5.8 %collective-permute-done = f32[2,128,512]{2,1,0:T(8,128)S(1)} collective-permute-done((f32[2,128,512]{2,1,0:T(8,128)S(1)}, f32[2,128,512]{2,1,0:T(8,128)S(1)}, u32[]{:S(2)}, u32[]{:S(2)}) %collective-permute-start) | collective-permute-done | bytes 524320 | tf_op jit(solution)/shard_map/ppermute | solution.py:15
  77.5 0.0 copy-done.5
  77.5 3.3 %collective-permute-start.1 = (f32[128,512]{1,0:T(8,128)S(1)}, f32[128,512]{1,0:T(8,128)S(1)}, u32[]{:S(2)}, u32[]{:S(2)}) collective-permute-start(f32[128,512]{1,0:T(8,128)S(1)} %slice_add_fusion), channel_id=1, source_target_pairs={{0,2},{1,3},{2,4},{3,5},{4,6},{5,7},{6,8},{7,9},{8,10},{9,11},{10,... | collective-permute-start | bytes 786440 | tf_op jit(solution)/shard_map/ppermute | solution.py:15
  80.8 0.6 fusion.10
  81.4 20.7 %collective-permute-done.1 = f32[128,512]{1,0:T(8,128)S(1)} collective-permute-done((f32[128,512]{1,0:T(8,128)S(1)}, f32[128,512]{1,0:T(8,128)S(1)}, u32[]{:S(2)}, u32[]{:S(2)}) %collective-permute-start.1) | collective-permute-done | bytes 262176 | tf_op jit(solution)/shard_map/ppermute | solution.py:15
  102.2 0.0 copy-done.7
  102.2 1.1 multiply_convert_fusion
  103.3 8.7 %collective-permute-start.4 = (bf16[128,512]{1,0:T(8,128)(2,1)S(1)}, bf16[128,512]{1,0:T(8,128)(2,1)S(1)}, u32[]{:S(2)}, u32[]{:S(2)}) collective-permute-start(bf16[128,512]{1,0:T(8,128)(2,1)S(1)} %get-tuple-element.2), channel_id=1, source_target_pairs={{0,61},{1,62},{2,63},{3,0},{4,1},{5,2},{6,3},{7,4},{8,5},{9,6},{10... | collective-permute-start | bytes 393224 | tf_op jit(solution)/shard_map/ppermute | solution.py:15
  112.0 1.9 collective-permute-start.3
  113.9 4.9 %collective-permute-start.2 = (bf16[128,512]{1,0:T(8,128)(2,1)S(1)}, bf16[128,512]{1,0:T(8,128)(2,1)S(1)}, u32[]{:S(2)}, u32[]{:S(2)}) collective-permute-start(bf16[128,512]{1,0:T(8,128)(2,1)S(1)} %get-tuple-element.2), channel_id=1, source_target_pairs={{0,63},{1,0},{2,1},{3,2},{4,3},{5,4},{6,5},{7,6},{8,7},{9,8},{10,9... | collective-permute-start | bytes 393224 | tf_op jit(solution)/shard_map/ppermute | solution.py:15
  118.8 1.3 convolution_bitcast_fusion.1
  120.1 0.0 collective-permute-done.4
  120.1 1.6 collective-permute-done.3
  121.7 1.6 collective-permute-done.2
  123.3 0.1 pad_maximum_fusion.2
  123.4 1.6 gather_fusion.1
  125.0 0.0 copy-start.1
  125.0 2.1 fusion.2
  127.1 0.0 copy-done.1
  127.1 0.0 copy-start
  127.1 0.8 fusion.3
  127.9 0.4 copy-done
  128.3 0.2 pad_maximum_fusion
  128.5 5.1 %all_to_all.35 = f32[2,512,512]{2,1,0:T(8,128)S(1)} all-to-all(f32[2,512,512]{2,1,0:T(8,128)S(1)} %bitcast.84), channel_id=1, replica_groups=mesh['zlo'=2,'x'=8,'zhi'=4,'y'=8,'core'=2] {'core'}, dimensions={0} | all-to-all | bytes 4194304 | tf_op jit(solution)/shard_map/all_to_all | solution.py:21
  133.5 0.3 reduce_sum.27
  133.8 36.0 %all_to_all.36 = f32[32,16,512]{2,1,0:T(8,128)S(1)} all-to-all(f32[32,16,512]{2,1,0:T(8,128)S(1)} %bitcast.85), channel_id=1, replica_groups=mesh['zlo'=2,'x'=8,'zhi'=4,'y'=8,'core'=2] {'zhi','y'}, dimensions={0} | all-to-all | bytes 2097152 | tf_op jit(solution)/shard_map/all_to_all | solution.py:21
  169.8 0.1 reduce_sum.28
  169.9 13.2 %all_to_all.37 = f32[16,1,512]{2,1,0:T(1,128)S(1)} all-to-all(f32[16,1,512]{2,1,0:T(1,128)S(1)} %copy.17), channel_id=1, replica_groups=mesh['zlo'=2,'x'=8,'zhi'=4,'y'=8,'core'=2] {'zlo','x'}, dimensions={0} | all-to-all | bytes 65536 | tf_op jit(solution)/shard_map/all_to_all | solution.py:21
  183.2 0.5 broadcast.211
  183.7 0.7 reduce.1
  184.5 9.9 %all_to_all.38 = bf16[16,2,256]{2,1,0:T(2,128)(2,1)S(1)} all-to-all(bf16[16,2,256]{2,1,0:T(2,128)(2,1)S(1)} %reshape.223), channel_id=1, replica_groups=mesh['zlo'=2,'x'=8,'zhi'=4,'y'=8,'core'=2] {'zlo','x'}, dimensions={0} | all-to-all | bytes 32768 | tf_op jit(solution)/shard_map/all_to_all | solution.py:28
  194.4 0.9 broadcast_in_dim.115
  195.3 9.8 %all-to-all-start.5 = ((bf16[32,16,512]{2,1,0:T(8,128)(2,1)}), bf16[32,16,512]{2,1,0:T(8,128)(2,1)S(1)}, u32[]{:S(2)}, u32[]{:S(2)}) async-start(bf16[32,16,512]{2,1,0:T(8,128)(2,1)} %broadcast_in_dim.115), calls=%async_computation.5 | async-start | bytes 1048576 | tf_op jit(solution)/shard_map/all_to_all | solution.py:28
  205.1 0.7 multiply_convert_fusion.1
  205.8 13.8 %all-to-all-done.5 = bf16[32,16,512]{2,1,0:T(8,128)(2,1)S(1)} async-done(((bf16[32,16,512]{2,1,0:T(8,128)(2,1)}), bf16[32,16,512]{2,1,0:T(8,128)(2,1)S(1)}, u32[]{:S(2)}, u32[]{:S(2)}) %all-to-all-start.5) | async-done | bytes 524320 | tf_op jit(solution)/shard_map/all_to_all | solution.py:28
  219.6 0.1 broadcast_in_dim.117
  219.7 9.9 %all_to_all.39 = bf16[2,512,512]{2,1,0:T(8,128)(2,1)S(1)} all-to-all(bf16[2,512,512]{2,1,0:T(8,128)(2,1)S(1)} %broadcast_in_dim.117), channel_id=1, replica_groups=mesh['zlo'=2,'x'=8,'zhi'=4,'y'=8,'core'=2] {'core'}, dimensions={0} | all-to-all | bytes 2097152 | tf_op jit(solution)/shard_map/all_to_all | solution.py:28
  229.6 1.7 bitcast_convert_fusion.4
  (19 shorter events, 0.3 us)
Async XLA Ops:
  3.1 10.9 %copy-start.3 = (bf16[1,8,128,128]{3,2,1,0:T(8,128)(2,1)S(1)}, bf16[1,8,128,128]{3,2,1,0:T(8,128)(2,1)}, u32[]{:S(2)}) copy-start(bf16[1,8,128,128]{3,2,1,0:T(8,128)(2,1)} %param.8) | copy-start | bytes 786436
  3.1 11.1 %copy-start.8 = (s32[1,8]{1,0:T(1,128)S(1)}, s32[1,8]{1,0:T(1,128)}, u32[]{:S(2)}) copy-start(s32[1,8]{1,0:T(1,128)} %param.10) | copy-start | bytes 100
  3.1 11.2 %copy-start.9 = (s32[1,8]{1,0:T(1,128)S(1)}, s32[1,8]{1,0:T(1,128)}, u32[]{:S(2)}) copy-start(s32[1,8]{1,0:T(1,128)} %param.9) | copy-start | bytes 100
  3.1 51.1 %all-to-all-start = ((bf16[16,128,512]{2,1,0:T(8,128)(2,1)}), bf16[16,128,512]{2,1,0:T(8,128)(2,1)S(1)}, u32[]{:S(2)}, u32[]{:S(2)}) async-start(bf16[16,128,512]{2,1,0:T(8,128)(2,1)} %broadcast_in_dim.106), calls=%async_computation | async-start | bytes 4194304 | tf_op jit(solution)/shard_map/all_to_all | solution.py:28
  54.8 1.4 copy-start.4
  58.8 18.7 %copy-start.5 = (f32[512,512]{1,0:T(8,128)}, f32[512,512]{1,0:T(8,128)S(1)}, u32[]{:S(2)}) copy-start(f32[512,512]{1,0:T(8,128)S(1)} %fusion.4) | copy-start | bytes 3145732
  58.8 12.6 %copy-start.2 = (bf16[128,512]{1,0:T(8,128)(2,1)S(1)}, bf16[128,512]{1,0:T(8,128)(2,1)}, u32[]{:S(2)}) copy-start(bf16[128,512]{1,0:T(8,128)(2,1)} %param.7) | copy-start | bytes 393220
  58.8 12.6 %copy-start.6 = (bf16[1024,512]{1,0:T(8,128)(2,1)S(1)}, bf16[1024,512]{1,0:T(8,128)(2,1)}, u32[]{:S(2)}) copy-start(bf16[1024,512]{1,0:T(8,128)(2,1)} %param.12) | copy-start | bytes 3145732
  58.9 18.5 %collective-permute-start = (f32[2,128,512]{2,1,0:T(8,128)S(1)}, f32[2,128,512]{2,1,0:T(8,128)S(1)}, u32[]{:S(2)}, u32[]{:S(2)}) collective-permute-start(f32[2,128,512]{2,1,0:T(8,128)S(1)} %pad_maximum_fusion.1), channel_id=1, source_target_pairs={{0,1},{1,2},{2,3},{3,4},{4,5},{5,6},{6,7},{7,8},{8,9},{9,10},{10,1... | collective-permute-start | bytes 1572872 | tf_op jit(solution)/shard_map/ppermute | solution.py:15
  71.6 30.5 %copy-start.7 = (bf16[128,512]{1,0:T(8,128)(2,1)S(1)}, bf16[128,512]{1,0:T(8,128)(2,1)}, u32[]{:S(2)}) copy-start(bf16[128,512]{1,0:T(8,128)(2,1)} %param.13) | copy-start | bytes 393220
  77.5 24.7 %collective-permute-start.1 = (f32[128,512]{1,0:T(8,128)S(1)}, f32[128,512]{1,0:T(8,128)S(1)}, u32[]{:S(2)}, u32[]{:S(2)}) collective-permute-start(f32[128,512]{1,0:T(8,128)S(1)} %slice_add_fusion), channel_id=1, source_target_pairs={{0,2},{1,3},{2,4},{3,5},{4,6},{5,7},{6,8},{7,9},{8,10},{9,11},{10,... | collective-permute-start | bytes 786440 | tf_op jit(solution)/shard_map/ppermute | solution.py:15
  103.3 16.8 %collective-permute-start.4 = (bf16[128,512]{1,0:T(8,128)(2,1)S(1)}, bf16[128,512]{1,0:T(8,128)(2,1)S(1)}, u32[]{:S(2)}, u32[]{:S(2)}) collective-permute-start(bf16[128,512]{1,0:T(8,128)(2,1)S(1)} %get-tuple-element.2), channel_id=1, source_target_pairs={{0,61},{1,62},{2,63},{3,0},{4,1},{5,2},{6,3},{7,4},{8,5},{9,6},{10... | collective-permute-start | bytes 393224 | tf_op jit(solution)/shard_map/ppermute | solution.py:15
  112.0 9.7 %collective-permute-start.3 = (bf16[128,512]{1,0:T(8,128)(2,1)S(1)}, bf16[128,512]{1,0:T(8,128)(2,1)S(1)}, u32[]{:S(2)}, u32[]{:S(2)}) collective-permute-start(bf16[128,512]{1,0:T(8,128)(2,1)S(1)} %get-tuple-element.2), channel_id=1, source_target_pairs={{0,62},{1,63},{2,0},{3,1},{4,2},{5,3},{6,4},{7,5},{8,6},{9,7},{10,... | collective-permute-start | bytes 393224 | tf_op jit(solution)/shard_map/ppermute | solution.py:15
  113.9 9.4 %collective-permute-start.2 = (bf16[128,512]{1,0:T(8,128)(2,1)S(1)}, bf16[128,512]{1,0:T(8,128)(2,1)S(1)}, u32[]{:S(2)}, u32[]{:S(2)}) collective-permute-start(bf16[128,512]{1,0:T(8,128)(2,1)S(1)} %get-tuple-element.2), channel_id=1, source_target_pairs={{0,63},{1,0},{2,1},{3,2},{4,3},{5,4},{6,5},{7,6},{8,7},{9,8},{10,9... | collective-permute-start | bytes 393224 | tf_op jit(solution)/shard_map/ppermute | solution.py:15
  125.0 2.1 copy-start.1
  127.1 1.2 copy-start
  195.3 24.4 %all-to-all-start.5 = ((bf16[32,16,512]{2,1,0:T(8,128)(2,1)}), bf16[32,16,512]{2,1,0:T(8,128)(2,1)S(1)}, u32[]{:S(2)}, u32[]{:S(2)}) async-start(bf16[32,16,512]{2,1,0:T(8,128)(2,1)} %broadcast_in_dim.115), calls=%async_computation.5 | async-start | bytes 1048576 | tf_op jit(solution)/shard_map/all_to_all | solution.py:28

commit v10 on v8

--- a/solution.py
+++ b/solution.py
@@ -66,9 +66,10 @@
     placed = placed.transpose(0, 2, 1, 3).reshape(REACH * tile_size, slots * tile_size)
     stacked_sums = jnp.dot(placed, projected, preferred_element_type=jnp.float32)
     stacked_sums = stacked_sums.reshape(REACH, tile_size, width)
-    first = from_behind(jnp.stack([stacked_sums[1], stacked_sums[3]]), 1)
-    second = from_behind(first[1] + stacked_sums[2], 2)
-    neighbour = stacked_sums[0] + first[0] + second
+    carry = from_behind(stacked_sums[REACH - 1], 1)
+    for step in range(REACH - 2, 0, -1):
+        carry = from_behind(carry + stacked_sums[step], 1)
+    neighbour = stacked_sums[0] + carry
 
     pre_act = jnp.dot(features, w_self, preferred_element_type=jnp.float32) + neighbour
     hidden = jax.nn.silu(pre_act).astype(jnp.bfloat16)

time: 231 us -> 240 us (1.039)
  blocking collectives: 78.9 us -> 98 us
  waiting for transfers between devices: 79.3 us -> 70.9 us
  starting transfers between devices: 48.5 us -> 46 us
    all_to_all x2 -> x3, blocking collectives: 23.4 us -> 41.7 us  [exchange_gather(): copies = lax.all_to_all(copies, axes, 0, 0, tiled=True)]
    all_to_all x2 -> x1, waiting for transfers between devices: 49.5 us -> 38.7 us  [exchange_gather(): copies = lax.all_to_all(copies, axes, 0, 0, tiled=True)]
    all_to_all x2 -> x1, starting transfers between devices: 17.3 us -> 10.3 us  [exchange_gather(): copies = lax.all_to_all(copies, axes, 0, 0, tiled=True)]
    ppermute x5 -> x6, starting transfers between devices: 31.2 us -> 35.8 us  [from_behind(): return lax.ppermute(value, COL, pairs)]
    ppermute x5 -> x6, waiting for transfers between devices: 29.8 us -> 32.2 us  [from_behind(): return lax.ppermute(value, COL, pairs)]
where the time goes in v10:
time: 240 us; the launch traced here: 239 us
  blocking collectives  98 us (41%)
  waiting for transfers between devices  70.9 us (30%)
  starting transfers between devices  46 us (19%)
  matrix products  8.67 us (4%)
  other arithmetic  7.34 us (3%)
  local copies, waits for them, and re-layouts  6.32 us (3%)
    all_to_all x3, blocking collectives, exchange_sum(): pieces = lax.all_to_all(pieces, axes, 0, 0, tiled=True)  56.3 us
    all_to_all x3, blocking collectives, exchange_gather(): copies = lax.all_to_all(copies, axes, 0, 0, tiled=True)  41.7 us
    all_to_all x1, waiting for transfers between devices, exchange_gather(): copies = lax.all_to_all(copies, axes, 0, 0, tiled=True)  38.7 us
    ppermute x6, starting transfers between devices, from_behind(): return lax.ppermute(value, COL, pairs)  35.8 us
    ppermute x6, waiting for transfers between devices, from_behind(): return lax.ppermute(value, COL, pairs)  32.2 us
    all_to_all x1, starting transfers between devices, exchange_gather(): copies = lax.all_to_all(copies, axes, 0, 0, tiled=True)  10.3 us
  transfers between devices with their start and end apart: 7, of which 6 were waited for; matrix products, arithmetic and copies ran while one was open for 2% of the time, Pallas kernels for 0%

profile of v10, /device:TPU:1, one launch (start us, length us, event | category | flops | bytes accessed | tf_op | source)
XLA Modules:
  0.0 238.8 jit_solution(6780407160399506738)
XLA Ops:
  0.6 2.4 %broadcast_in_dim.106 = bf16[16,128,512]{2,1,0:T(8,128)(2,1)} broadcast(bf16[128,512]{1,0:T(8,128)(2,1)} %param.7), dimensions={1,2} | broadcast | bytes 2228224 | tf_op jit(solution)/shard_map/broadcast_in_dim | solution.py:27
  3.1 0.0 copy-start.3
  3.1 0.0 copy-start.7
  3.1 0.0 copy-start.8
  3.1 10.3 %all-to-all-start = ((bf16[16,128,512]{2,1,0:T(8,128)(2,1)}), bf16[16,128,512]{2,1,0:T(8,128)(2,1)S(1)}, u32[]{:S(2)}, u32[]{:S(2)}) async-start(bf16[16,128,512]{2,1,0:T(8,128)(2,1)} %broadcast_in_dim.106), calls=%async_computation | async-start | bytes 4194304 | tf_op jit(solution)/shard_map/all_to_all | solution.py:28
  14.0 0.0 copy-done.3
  14.0 0.2 copy.15
  14.2 0.0 copy-done.7
  14.3 0.0 copy-done.8
  14.3 0.1 broadcast_bitcast_fusion
  14.4 1.1 broadcast_select_fusion.1
  15.5 38.7 %all-to-all-done = bf16[16,128,512]{2,1,0:T(8,128)(2,1)S(1)} async-done(((bf16[16,128,512]{2,1,0:T(8,128)(2,1)}), bf16[16,128,512]{2,1,0:T(8,128)(2,1)S(1)}, u32[]{:S(2)}, u32[]{:S(2)}) %all-to-all-start) | async-done | bytes 2097184 | tf_op jit(solution)/shard_map/all_to_all | solution.py:28
  54.2 0.6 gather_fusion
  54.8 0.0 copy-start.5
  54.8 1.2 bitcast_select_fusion
  56.0 0.2 copy-done.5
  56.2 0.0 copy-start.9
  56.2 0.0 copy-start.2
  56.2 2.6 %fusion.4 = f32[512,512]{1,0:T(8,128)S(1)} fusion(bf16[1024,512]{1,0:T(8,128)(2,1)} %bitcast_select_fusion, bf16[64,8,8,128]{3,2,1,0:T(8,128)(2,1)S(1)} %bitcast.72, bf16[1024,512]{1,0:T(8,128)(2,1)} %param.12), kind=kOutput, calls=%fused_computation.12 | convolution fusion | flops 1074266112 | bytes 3670016 | tf_op jit(solution)/shard_map/dot_general | solution.py:67
  58.8 0.0 copy-start.4
  58.9 12.3 %collective-permute-start = (f32[128,512]{1,0:T(8,128)S(1)}, f32[128,512]{1,0:T(8,128)S(1)}, u32[]{:S(2)}, u32[]{:S(2)}) collective-permute-start(f32[128,512]{1,0:T(8,128)S(1)} %slice.33), channel_id=1, source_target_pairs={{0,1},{1,2},{2,3},{3,4},{4,5},{5,6},{6,7},{7,8},{8,9},{9,10},{10,1... | collective-permute-start | bytes 786440 | tf_op jit(solution)/shard_map/ppermute | solution.py:15
  71.2 0.0 copy-done.9
  71.2 3.2 %collective-permute-done = f32[128,512]{1,0:T(8,128)S(1)} collective-permute-done((f32[128,512]{1,0:T(8,128)S(1)}, f32[128,512]{1,0:T(8,128)S(1)}, u32[]{:S(2)}, u32[]{:S(2)}) %collective-permute-start) | collective-permute-done | bytes 262176 | tf_op jit(solution)/shard_map/ppermute | solution.py:15
  74.5 4.4 %collective-permute-start.1 = (f32[128,512]{1,0:T(8,128)S(1)}, f32[128,512]{1,0:T(8,128)S(1)}, u32[]{:S(2)}, u32[]{:S(2)}) collective-permute-start(f32[128,512]{1,0:T(8,128)S(1)} %slice_add_fusion.1), channel_id=1, source_target_pairs={{0,1},{1,2},{2,3},{3,4},{4,5},{5,6},{6,7},{7,8},{8,9},{9,10},{10,1... | collective-permute-start | bytes 786440 | tf_op jit(solution)/shard_map/ppermute | solution.py:15
  78.9 0.0 copy-done.2
  78.9 1.3 fusion.18
  80.2 0.0 copy-start.6
  80.2 14.2 %collective-permute-done.1 = f32[128,512]{1,0:T(8,128)S(1)} collective-permute-done((f32[128,512]{1,0:T(8,128)S(1)}, f32[128,512]{1,0:T(8,128)S(1)}, u32[]{:S(2)}, u32[]{:S(2)}) %collective-permute-start.1) | collective-permute-done | bytes 262176 | tf_op jit(solution)/shard_map/ppermute | solution.py:15
  94.4 0.0 copy-done.4
  94.5 1.9 collective-permute-start.2
  96.4 0.6 fusion.10
  97.0 11.5 %collective-permute-done.2 = f32[128,512]{1,0:T(8,128)S(1)} collective-permute-done((f32[128,512]{1,0:T(8,128)S(1)}, f32[128,512]{1,0:T(8,128)S(1)}, u32[]{:S(2)}, u32[]{:S(2)}) %collective-permute-start.2) | collective-permute-done | bytes 262176 | tf_op jit(solution)/shard_map/ppermute | solution.py:15
  108.4 0.0 copy-done.6
  108.4 1.7 multiply_convert_fusion
  110.2 1.9 collective-permute-start.5
  112.1 10.3 %collective-permute-start.4 = (bf16[128,512]{1,0:T(8,128)(2,1)S(1)}, bf16[128,512]{1,0:T(8,128)(2,1)S(1)}, u32[]{:S(2)}, u32[]{:S(2)}) collective-permute-start(bf16[128,512]{1,0:T(8,128)(2,1)S(1)} %get-tuple-element.2), channel_id=1, source_target_pairs={{0,62},{1,63},{2,0},{3,1},{4,2},{5,3},{6,4},{7,5},{8,6},{9,7},{10,... | collective-permute-start | bytes 393224 | tf_op jit(solution)/shard_map/ppermute | solution.py:15
  122.4 4.9 %collective-permute-start.3 = (bf16[128,512]{1,0:T(8,128)(2,1)S(1)}, bf16[128,512]{1,0:T(8,128)(2,1)S(1)}, u32[]{:S(2)}, u32[]{:S(2)}) collective-permute-start(bf16[128,512]{1,0:T(8,128)(2,1)S(1)} %get-tuple-element.2), channel_id=1, source_target_pairs={{0,63},{1,0},{2,1},{3,2},{4,3},{5,4},{6,5},{7,6},{8,7},{9,8},{10,9... | collective-permute-start | bytes 393224 | tf_op jit(solution)/shard_map/ppermute | solution.py:15
  127.4 1.3 convolution_bitcast_fusion.1
  128.7 0.0 collective-permute-done.5
  128.7 1.6 collective-permute-done.4
  130.3 1.6 collective-permute-done.3
  131.9 0.1 pad_maximum_fusion.1
  132.0 1.6 gather_fusion.1
  133.6 0.0 copy-start.1
  133.6 2.1 fusion.2
  135.7 0.0 copy-done.1
  135.7 0.0 copy-start
  135.7 0.8 fusion.3
  136.5 0.4 copy-done
  136.9 0.2 pad_maximum_fusion
  137.1 5.1 %all_to_all.35 = f32[2,512,512]{2,1,0:T(8,128)S(1)} all-to-all(f32[2,512,512]{2,1,0:T(8,128)S(1)} %bitcast.67), channel_id=1, replica_groups=mesh['zlo'=2,'x'=8,'zhi'=4,'y'=8,'core'=2] {'core'}, dimensions={0} | all-to-all | bytes 4194304 | tf_op jit(solution)/shard_map/all_to_all | solution.py:21
  142.2 0.3 reduce_sum.27
  142.4 30.8 %all_to_all.36 = f32[16,32,512]{2,1,0:T(8,128)S(1)} all-to-all(f32[16,32,512]{2,1,0:T(8,128)S(1)} %bitcast.68), channel_id=1, replica_groups=mesh['zlo'=2,'x'=8,'zhi'=4,'y'=8,'core'=2] {'zlo','x'}, dimensions={0} | all-to-all | bytes 2097152 | tf_op jit(solution)/shard_map/all_to_all | solution.py:21
  173.2 0.1 reduce_sum.28
  173.3 0.1 copy.17
  173.3 20.4 %all_to_all.37 = f32[32,1,512]{2,1,0:T(1,128)S(1)} all-to-all(f32[32,1,512]{2,1,0:T(1,128)S(1)} %copy.17), channel_id=1, replica_groups=mesh['zlo'=2,'x'=8,'zhi'=4,'y'=8,'core'=2] {'zhi','y'}, dimensions={0} | all-to-all | bytes 131072 | tf_op jit(solution)/shard_map/all_to_all | solution.py:21
  193.8 0.1 reduce_sum.29
  193.9 0.5 broadcast.211
  194.4 0.8 reduce.1
  195.3 14.1 %all_to_all.38 = bf16[32,2,256]{2,1,0:T(2,128)(2,1)S(1)} all-to-all(bf16[32,2,256]{2,1,0:T(2,128)(2,1)S(1)} %reshape.225), channel_id=1, replica_groups=mesh['zlo'=2,'x'=8,'zhi'=4,'y'=8,'core'=2] {'zhi','y'}, dimensions={0} | all-to-all | bytes 65536 | tf_op jit(solution)/shard_map/all_to_all | solution.py:28
  209.4 18.3 %all_to_all.39 = bf16[16,32,512]{2,1,0:T(8,128)(2,1)S(1)} all-to-all(bf16[16,32,512]{2,1,0:T(8,128)(2,1)S(1)} %broadcast_in_dim.115), channel_id=1, replica_groups=mesh['zlo'=2,'x'=8,'zhi'=4,'y'=8,'core'=2] {'zlo','x'}, dimensions={0} | all-to-all | bytes 1048576 | tf_op jit(solution)/shard_map/all_to_all | solution.py:28
  227.8 0.1 broadcast_in_dim.117
  227.8 9.3 %all_to_all.40 = bf16[2,512,512]{2,1,0:T(8,128)(2,1)S(1)} all-to-all(bf16[2,512,512]{2,1,0:T(8,128)(2,1)S(1)} %broadcast_in_dim.117), channel_id=1, replica_groups=mesh['zlo'=2,'x'=8,'zhi'=4,'y'=8,'core'=2] {'core'}, dimensions={0} | all-to-all | bytes 2097152 | tf_op jit(solution)/shard_map/all_to_all | solution.py:28
  237.1 1.7 bitcast_convert_fusion.4
  (18 shorter events, 0.3 us)
Async XLA Ops:
  3.1 10.9 %copy-start.3 = (bf16[1,8,128,128]{3,2,1,0:T(8,128)(2,1)S(1)}, bf16[1,8,128,128]{3,2,1,0:T(8,128)(2,1)}, u32[]{:S(2)}) copy-start(bf16[1,8,128,128]{3,2,1,0:T(8,128)(2,1)} %param.8) | copy-start | bytes 786436
  3.1 11.1 %copy-start.7 = (s32[1,8]{1,0:T(1,128)S(1)}, s32[1,8]{1,0:T(1,128)}, u32[]{:S(2)}) copy-start(s32[1,8]{1,0:T(1,128)} %param.10) | copy-start | bytes 100
  3.1 11.2 %copy-start.8 = (s32[1,8]{1,0:T(1,128)S(1)}, s32[1,8]{1,0:T(1,128)}, u32[]{:S(2)}) copy-start(s32[1,8]{1,0:T(1,128)} %param.9) | copy-start | bytes 100
  3.1 51.1 %all-to-all-start = ((bf16[16,128,512]{2,1,0:T(8,128)(2,1)}), bf16[16,128,512]{2,1,0:T(8,128)(2,1)S(1)}, u32[]{:S(2)}, u32[]{:S(2)}) async-start(bf16[16,128,512]{2,1,0:T(8,128)(2,1)} %broadcast_in_dim.106), calls=%async_computation | async-start | bytes 4194304 | tf_op jit(solution)/shard_map/all_to_all | solution.py:28
  54.8 1.4 copy-start.5
  56.2 15.0 %copy-start.9 = (s32[1,8]{1,0:T(1,128)S(1)}, s32[1,8]{1,0:T(1,128)}, u32[]{:S(2)}) copy-start(s32[1,8]{1,0:T(1,128)} %param.9) | copy-start | bytes 100
  56.2 22.7 %copy-start.2 = (bf16[128,512]{1,0:T(8,128)(2,1)S(1)}, bf16[128,512]{1,0:T(8,128)(2,1)}, u32[]{:S(2)}) copy-start(bf16[128,512]{1,0:T(8,128)(2,1)} %param.7) | copy-start | bytes 393220
  58.8 35.6 %copy-start.4 = (f32[512,512]{1,0:T(8,128)}, f32[512,512]{1,0:T(8,128)S(1)}, u32[]{:S(2)}) copy-start(f32[512,512]{1,0:T(8,128)S(1)} %fusion.4) | copy-start | bytes 3145732
  58.9 15.6 %collective-permute-start = (f32[128,512]{1,0:T(8,128)S(1)}, f32[128,512]{1,0:T(8,128)S(1)}, u32[]{:S(2)}, u32[]{:S(2)}) collective-permute-start(f32[128,512]{1,0:T(8,128)S(1)} %slice.33), channel_id=1, source_target_pairs={{0,1},{1,2},{2,3},{3,4},{4,5},{5,6},{6,7},{7,8},{8,9},{9,10},{10,1... | collective-permute-start | bytes 786440 | tf_op jit(solution)/shard_map/ppermute | solution.py:15
  74.5 19.9 %collective-permute-start.1 = (f32[128,512]{1,0:T(8,128)S(1)}, f32[128,512]{1,0:T(8,128)S(1)}, u32[]{:S(2)}, u32[]{:S(2)}) collective-permute-start(f32[128,512]{1,0:T(8,128)S(1)} %slice_add_fusion.1), channel_id=1, source_target_pairs={{0,1},{1,2},{2,3},{3,4},{4,5},{5,6},{6,7},{7,8},{8,9},{9,10},{10,1... | collective-permute-start | bytes 786440 | tf_op jit(solution)/shard_map/ppermute | solution.py:15
  80.2 28.2 %copy-start.6 = (bf16[128,512]{1,0:T(8,128)(2,1)S(1)}, bf16[128,512]{1,0:T(8,128)(2,1)}, u32[]{:S(2)}) copy-start(bf16[128,512]{1,0:T(8,128)(2,1)} %param.13) | copy-start | bytes 393220
  94.5 14.0 %collective-permute-start.2 = (f32[128,512]{1,0:T(8,128)S(1)}, f32[128,512]{1,0:T(8,128)S(1)}, u32[]{:S(2)}, u32[]{:S(2)}) collective-permute-start(f32[128,512]{1,0:T(8,128)S(1)} %slice_add_fusion), channel_id=1, source_target_pairs={{0,1},{1,2},{2,3},{3,4},{4,5},{5,6},{6,7},{7,8},{8,9},{9,10},{10,1... | collective-permute-start | bytes 786440 | tf_op jit(solution)/shard_map/ppermute | solution.py:15
  110.2 18.5 %collective-permute-start.5 = (bf16[128,512]{1,0:T(8,128)(2,1)S(1)}, bf16[128,512]{1,0:T(8,128)(2,1)S(1)}, u32[]{:S(2)}, u32[]{:S(2)}) collective-permute-start(bf16[128,512]{1,0:T(8,128)(2,1)S(1)} %get-tuple-element.2), channel_id=1, source_target_pairs={{0,61},{1,62},{2,63},{3,0},{4,1},{5,2},{6,3},{7,4},{8,5},{9,6},{10... | collective-permute-start | bytes 393224 | tf_op jit(solution)/shard_map/ppermute | solution.py:15
  112.1 18.2 %collective-permute-start.4 = (bf16[128,512]{1,0:T(8,128)(2,1)S(1)}, bf16[128,512]{1,0:T(8,128)(2,1)S(1)}, u32[]{:S(2)}, u32[]{:S(2)}) collective-permute-start(bf16[128,512]{1,0:T(8,128)(2,1)S(1)} %get-tuple-element.2), channel_id=1, source_target_pairs={{0,62},{1,63},{2,0},{3,1},{4,2},{5,3},{6,4},{7,5},{8,6},{9,7},{10,... | collective-permute-start | bytes 393224 | tf_op jit(solution)/shard_map/ppermute | solution.py:15
  122.4 9.5 %collective-permute-start.3 = (bf16[128,512]{1,0:T(8,128)(2,1)S(1)}, bf16[128,512]{1,0:T(8,128)(2,1)S(1)}, u32[]{:S(2)}, u32[]{:S(2)}) collective-permute-start(bf16[128,512]{1,0:T(8,128)(2,1)S(1)} %get-tuple-element.2), channel_id=1, source_target_pairs={{0,63},{1,0},{2,1},{3,2},{4,3},{5,4},{6,5},{7,6},{8,7},{9,8},{10,9... | collective-permute-start | bytes 393224 | tf_op jit(solution)/shard_map/ppermute | solution.py:15
  133.6 2.1 copy-start.1
  135.7 1.2 copy-start

commit v11 on v8

--- a/solution.py
+++ b/solution.py
@@ -66,9 +66,10 @@
     placed = placed.transpose(0, 2, 1, 3).reshape(REACH * tile_size, slots * tile_size)
     stacked_sums = jnp.dot(placed, projected, preferred_element_type=jnp.float32)
     stacked_sums = stacked_sums.reshape(REACH, tile_size, width)
-    first = from_behind(jnp.stack([stacked_sums[1], stacked_sums[3]]), 1)
-    second = from_behind(first[1] + stacked_sums[2], 2)
-    neighbour = stacked_sums[0] + first[0] + second
+    nearest = from_behind(stacked_sums[1], 1)
+    carried = from_behind(stacked_sums[3], 1)
+    second = from_behind(carried + stacked_sums[2], 2)
+    neighbour = stacked_sums[0] + nearest + second
 
     pre_act = jnp.dot(features, w_self, preferred_element_type=jnp.float32) + neighbour
     hidden = jax.nn.silu(pre_act).astype(jnp.bfloat16)

time: 231 us -> 232 us (level)
  waiting for transfers between devices: 79.3 us -> 66.8 us
  starting transfers between devices: 48.5 us -> 59.4 us
    ppermute x5 -> x6, waiting for transfers between devices: 29.8 us -> 17.9 us  [from_behind(): return lax.ppermute(value, COL, pairs)]
    ppermute x5 -> x6, starting transfers between devices: 31.2 us -> 42.1 us  [from_behind(): return lax.ppermute(value, COL, pairs)]
  transfers between devices with their start and end apart: 7 -> 8, of which waited for: 6 -> 6; matrix products, arithmetic and copies ran while one was open for 2% -> 3% of each run, Pallas kernels for 0% -> 0%
where the time goes in v11:
time: 232 us; the launch traced here: 231 us
  blocking collectives  79.2 us (34%)
  waiting for transfers between devices  66.8 us (29%)
  starting transfers between devices  59.4 us (26%)
  matrix products  8.67 us (4%)
  other arithmetic  8.52 us (4%)
  local copies, waits for them, and re-layouts  7.13 us (3%)
    all_to_all x3, blocking collectives, exchange_sum(): pieces = lax.all_to_all(pieces, axes, 0, 0, tiled=True)  55.8 us
    all_to_all x2, waiting for transfers between devices, exchange_gather(): copies = lax.all_to_all(copies, axes, 0, 0, tiled=True)  48.9 us
    ppermute x6, starting transfers between devices, from_behind(): return lax.ppermute(value, COL, pairs)  42.1 us
    all_to_all x2, blocking collectives, exchange_gather(): copies = lax.all_to_all(copies, axes, 0, 0, tiled=True)  23.4 us
    ppermute x6, waiting for transfers between devices, from_behind(): return lax.ppermute(value, COL, pairs)  17.9 us
    all_to_all x2, starting transfers between devices, exchange_gather(): copies = lax.all_to_all(copies, axes, 0, 0, tiled=True)  17.3 us
  transfers between devices with their start and end apart: 8, of which 6 were waited for; matrix products, arithmetic and copies ran while one was open for 3% of the time, Pallas kernels for 0%

profile of v11, /device:TPU:1, one launch (start us, length us, event | category | flops | bytes accessed | tf_op | source)
XLA Modules:
  0.0 231.3 jit_solution(5239083131772765306)
XLA Ops:
  0.6 2.4 %broadcast_in_dim.106 = bf16[16,128,512]{2,1,0:T(8,128)(2,1)} broadcast(bf16[128,512]{1,0:T(8,128)(2,1)} %param.7), dimensions={1,2} | broadcast | bytes 2228224 | tf_op jit(solution)/shard_map/broadcast_in_dim | solution.py:27
  3.1 10.3 %all-to-all-start = ((bf16[16,128,512]{2,1,0:T(8,128)(2,1)}), bf16[16,128,512]{2,1,0:T(8,128)(2,1)S(1)}, u32[]{:S(2)}, u32[]{:S(2)}) async-start(bf16[16,128,512]{2,1,0:T(8,128)(2,1)} %broadcast_in_dim.106), calls=%async_computation | async-start | bytes 4194304 | tf_op jit(solution)/shard_map/all_to_all | solution.py:28
  14.0 0.0 copy-done.3
  14.0 0.2 copy.15
  14.2 0.0 copy-done.9
  14.3 0.0 copy-done.10
  14.3 0.0 copy-start.7
  14.3 0.5 fusion.29
  14.8 0.1 broadcast_bitcast_fusion
  14.9 1.1 broadcast_select_fusion.1
  16.0 0.0 copy-done.7
  16.0 38.2 %all-to-all-done = bf16[16,128,512]{2,1,0:T(8,128)(2,1)S(1)} async-done(((bf16[16,128,512]{2,1,0:T(8,128)(2,1)}), bf16[16,128,512]{2,1,0:T(8,128)(2,1)S(1)}, u32[]{:S(2)}, u32[]{:S(2)}) %all-to-all-start) | async-done | bytes 2097184 | tf_op jit(solution)/shard_map/all_to_all | solution.py:28
  54.2 0.6 gather_fusion
  54.8 0.0 copy-start.4
  54.8 1.2 bitcast_select_fusion
  56.0 0.2 copy-done.4
  56.2 2.6 %fusion.4 = f32[512,512]{1,0:T(8,128)S(1)} fusion(bf16[1024,512]{1,0:T(8,128)(2,1)} %bitcast_select_fusion, bf16[64,8,8,128]{3,2,1,0:T(8,128)(2,1)S(1)} %bitcast.72, bf16[1024,512]{1,0:T(8,128)(2,1)} %param.12), kind=kOutput, calls=%fused_computation.12 | convolution fusion | flops 1074266112 | bytes 3670016 | tf_op jit(solution)/shard_map/dot_general | solution.py:67
  58.8 0.0 copy-start.5
  58.8 0.0 copy-start.8
  58.9 12.3 %collective-permute-start.1 = (f32[128,512]{1,0:T(8,128)S(1)}, f32[128,512]{1,0:T(8,128)S(1)}, u32[]{:S(2)}, u32[]{:S(2)}) collective-permute-start(f32[128,512]{1,0:T(8,128)S(1)} %slice.34), channel_id=1, source_target_pairs={{0,1},{1,2},{2,3},{3,4},{4,5},{5,6},{6,7},{7,8},{8,9},{9,10},{10,1... | collective-permute-start | bytes 786440 | tf_op jit(solution)/shard_map/ppermute | solution.py:15
  71.2 0.6 pad_clamp_fusion
  71.8 0.0 copy-done.2
  71.8 1.3 fusion.18
  73.0 0.0 copy-start.6
  73.1 1.4 collective-permute-done.1
  74.5 0.1 fusion.36
  74.5 3.3 %collective-permute-start.2 = (f32[128,512]{1,0:T(8,128)S(1)}, f32[128,512]{1,0:T(8,128)S(1)}, u32[]{:S(2)}, u32[]{:S(2)}) collective-permute-start(f32[128,512]{1,0:T(8,128)S(1)} %get-tuple-element.5), channel_id=1, source_target_pairs={{0,2},{1,3},{2,4},{3,5},{4,6},{5,7},{6,8},{7,9},{8,10},{9,11},{10,... | collective-permute-start | bytes 786440 | tf_op jit(solution)/shard_map/ppermute | solution.py:15
  77.9 4.7 %collective-permute-start = (f32[128,512]{1,0:T(8,128)S(1)}, f32[128,512]{1,0:T(8,128)S(1)}, u32[]{:S(2)}, u32[]{:S(2)}) collective-permute-start(f32[128,512]{1,0:T(8,128)S(1)} %get-tuple-element.4), channel_id=1, source_target_pairs={{0,1},{1,2},{2,3},{3,4},{4,5},{5,6},{6,7},{7,8},{8,9},{9,10},{10,1... | collective-permute-start | bytes 786440 | tf_op jit(solution)/shard_map/ppermute | solution.py:15
  82.6 0.6 fusion.10
  83.1 13.2 %collective-permute-done.2 = f32[128,512]{1,0:T(8,128)S(1)} collective-permute-done((f32[128,512]{1,0:T(8,128)S(1)}, f32[128,512]{1,0:T(8,128)S(1)}, u32[]{:S(2)}, u32[]{:S(2)}) %collective-permute-start.2) | collective-permute-done | bytes 262176 | tf_op jit(solution)/shard_map/ppermute | solution.py:15
  96.4 0.0 collective-permute-done
  96.4 1.1 multiply_convert_fusion
  97.5 12.5 %collective-permute-start.5 = (bf16[128,512]{1,0:T(8,128)(2,1)S(1)}, bf16[128,512]{1,0:T(8,128)(2,1)S(1)}, u32[]{:S(2)}, u32[]{:S(2)}) collective-permute-start(bf16[128,512]{1,0:T(8,128)(2,1)S(1)} %get-tuple-element.2), channel_id=1, source_target_pairs={{0,61},{1,62},{2,63},{3,0},{4,1},{5,2},{6,3},{7,4},{8,5},{9,6},{10... | collective-permute-start | bytes 393224 | tf_op jit(solution)/shard_map/ppermute | solution.py:15
  110.0 3.3 %collective-permute-start.4 = (bf16[128,512]{1,0:T(8,128)(2,1)S(1)}, bf16[128,512]{1,0:T(8,128)(2,1)S(1)}, u32[]{:S(2)}, u32[]{:S(2)}) collective-permute-start(bf16[128,512]{1,0:T(8,128)(2,1)S(1)} %get-tuple-element.2), channel_id=1, source_target_pairs={{0,62},{1,63},{2,0},{3,1},{4,2},{5,3},{6,4},{7,5},{8,6},{9,7},{10,... | collective-permute-start | bytes 393224 | tf_op jit(solution)/shard_map/ppermute | solution.py:15
  113.3 6.0 %collective-permute-start.3 = (bf16[128,512]{1,0:T(8,128)(2,1)S(1)}, bf16[128,512]{1,0:T(8,128)(2,1)S(1)}, u32[]{:S(2)}, u32[]{:S(2)}) collective-permute-start(bf16[128,512]{1,0:T(8,128)(2,1)S(1)} %get-tuple-element.2), channel_id=1, source_target_pairs={{0,63},{1,0},{2,1},{3,2},{4,3},{5,4},{6,5},{7,6},{8,7},{9,8},{10,9... | collective-permute-start | bytes 393224 | tf_op jit(solution)/shard_map/ppermute | solution.py:15
  119.3 1.3 convolution_bitcast_fusion.1
  120.6 0.0 collective-permute-done.5
  120.6 1.6 collective-permute-done.4
  122.2 1.6 collective-permute-done.3
  123.9 0.1 pad_maximum_fusion.1
  123.9 1.6 gather_fusion.1
  125.5 2.1 fusion.2
  127.6 0.0 copy-done.1
  127.6 0.0 copy-start
  127.6 0.8 fusion.3
  128.4 0.4 copy-done
  128.8 0.2 pad_maximum_fusion
  129.0 5.1 %all_to_all.35 = f32[2,512,512]{2,1,0:T(8,128)S(1)} all-to-all(f32[2,512,512]{2,1,0:T(8,128)S(1)} %bitcast.67), channel_id=1, replica_groups=mesh['zlo'=2,'x'=8,'zhi'=4,'y'=8,'core'=2] {'core'}, dimensions={0} | all-to-all | bytes 4194304 | tf_op jit(solution)/shard_map/all_to_all | solution.py:21
  134.1 0.3 reduce_sum.27
  134.3 30.3 %all_to_all.36 = f32[16,32,512]{2,1,0:T(8,128)S(1)} all-to-all(f32[16,32,512]{2,1,0:T(8,128)S(1)} %bitcast.68), channel_id=1, replica_groups=mesh['zlo'=2,'x'=8,'zhi'=4,'y'=8,'core'=2] {'zlo','x'}, dimensions={0} | all-to-all | bytes 2097152 | tf_op jit(solution)/shard_map/all_to_all | solution.py:21
  164.6 0.1 reduce_sum.28
  164.7 0.1 copy.17
  164.8 20.5 %all_to_all.37 = f32[32,1,512]{2,1,0:T(1,128)S(1)} all-to-all(f32[32,1,512]{2,1,0:T(1,128)S(1)} %copy.17), channel_id=1, replica_groups=mesh['zlo'=2,'x'=8,'zhi'=4,'y'=8,'core'=2] {'zhi','y'}, dimensions={0} | all-to-all | bytes 131072 | tf_op jit(solution)/shard_map/all_to_all | solution.py:21
  185.2 0.1 reduce_sum.29
  185.4 0.5 broadcast.211
  185.9 0.8 reduce.1
  186.7 14.1 %all_to_all.38 = bf16[32,2,256]{2,1,0:T(2,128)(2,1)S(1)} all-to-all(bf16[32,2,256]{2,1,0:T(2,128)(2,1)S(1)} %reshape.225), channel_id=1, replica_groups=mesh['zlo'=2,'x'=8,'zhi'=4,'y'=8,'core'=2] {'zhi','y'}, dimensions={0} | all-to-all | bytes 65536 | tf_op jit(solution)/shard_map/all_to_all | solution.py:28
  200.8 0.8 broadcast_in_dim.115
  201.7 7.0 %all-to-all-start.5 = ((bf16[16,32,512]{2,1,0:T(8,128)(2,1)}), bf16[16,32,512]{2,1,0:T(8,128)(2,1)S(1)}, u32[]{:S(2)}, u32[]{:S(2)}) async-start(bf16[16,32,512]{2,1,0:T(8,128)(2,1)} %broadcast_in_dim.115), calls=%async_computation.5 | async-start | bytes 1048576 | tf_op jit(solution)/shard_map/all_to_all | solution.py:28
  208.7 0.7 multiply_convert_fusion.1
  209.4 10.8 %all-to-all-done.5 = bf16[16,32,512]{2,1,0:T(8,128)(2,1)S(1)} async-done(((bf16[16,32,512]{2,1,0:T(8,128)(2,1)}), bf16[16,32,512]{2,1,0:T(8,128)(2,1)S(1)}, u32[]{:S(2)}, u32[]{:S(2)}) %all-to-all-start.5) | async-done | bytes 524320 | tf_op jit(solution)/shard_map/all_to_all | solution.py:28
  220.2 0.1 broadcast_in_dim.117
  220.3 9.3 %all_to_all.39 = bf16[2,512,512]{2,1,0:T(8,128)(2,1)S(1)} all-to-all(bf16[2,512,512]{2,1,0:T(8,128)(2,1)S(1)} %broadcast_in_dim.117), channel_id=1, replica_groups=mesh['zlo'=2,'x'=8,'zhi'=4,'y'=8,'core'=2] {'core'}, dimensions={0} | all-to-all | bytes 2097152 | tf_op jit(solution)/shard_map/all_to_all | solution.py:28
  229.6 1.7 bitcast_convert_fusion.4
  (21 shorter events, 0.2 us)
Async XLA Ops:
  3.1 10.9 %copy-start.3 = (bf16[1,8,128,128]{3,2,1,0:T(8,128)(2,1)S(1)}, bf16[1,8,128,128]{3,2,1,0:T(8,128)(2,1)}, u32[]{:S(2)}) copy-start(bf16[1,8,128,128]{3,2,1,0:T(8,128)(2,1)} %param.8) | copy-start | bytes 786436
  3.1 11.1 %copy-start.9 = (s32[1,8]{1,0:T(1,128)S(1)}, s32[1,8]{1,0:T(1,128)}, u32[]{:S(2)}) copy-start(s32[1,8]{1,0:T(1,128)} %param.10) | copy-start | bytes 100
  3.1 11.2 %copy-start.10 = (s32[1,8]{1,0:T(1,128)S(1)}, s32[1,8]{1,0:T(1,128)}, u32[]{:S(2)}) copy-start(s32[1,8]{1,0:T(1,128)} %param.9) | copy-start | bytes 100
  3.1 51.1 %all-to-all-start = ((bf16[16,128,512]{2,1,0:T(8,128)(2,1)}), bf16[16,128,512]{2,1,0:T(8,128)(2,1)S(1)}, u32[]{:S(2)}, u32[]{:S(2)}) async-start(bf16[16,128,512]{2,1,0:T(8,128)(2,1)} %broadcast_in_dim.106), calls=%async_computation | async-start | bytes 4194304 | tf_op jit(solution)/shard_map/all_to_all | solution.py:28
  14.3 1.8 copy-start.7
  54.8 1.4 copy-start.4
  56.2 15.6 %copy-start.2 = (bf16[128,512]{1,0:T(8,128)(2,1)S(1)}, bf16[128,512]{1,0:T(8,128)(2,1)}, u32[]{:S(2)}) copy-start(bf16[128,512]{1,0:T(8,128)(2,1)} %param.7) | copy-start | bytes 393220
  58.8 19.0 %copy-start.5 = (f32[512,512]{1,0:T(8,128)}, f32[512,512]{1,0:T(8,128)S(1)}, u32[]{:S(2)}) copy-start(f32[512,512]{1,0:T(8,128)S(1)} %fusion.4) | copy-start | bytes 3145732
  58.8 23.7 %copy-start.8 = (pred[8]{0:T(512)(128)(4,1)S(1)}, pred[8]{0:T(512)(128)(4,1)}, u32[]{:S(2)}) copy-start(pred[8]{0:T(512)(128)(4,1)} %copy-done.7) | copy-start | bytes 28
  58.9 15.6 %collective-permute-start.1 = (f32[128,512]{1,0:T(8,128)S(1)}, f32[128,512]{1,0:T(8,128)S(1)}, u32[]{:S(2)}, u32[]{:S(2)}) collective-permute-start(f32[128,512]{1,0:T(8,128)S(1)} %slice.34), channel_id=1, source_target_pairs={{0,1},{1,2},{2,3},{3,4},{4,5},{5,6},{6,7},{7,8},{8,9},{9,10},{10,1... | collective-permute-start | bytes 786440 | tf_op jit(solution)/shard_map/ppermute | solution.py:15
  73.0 23.3 %copy-start.6 = (bf16[128,512]{1,0:T(8,128)(2,1)S(1)}, bf16[128,512]{1,0:T(8,128)(2,1)}, u32[]{:S(2)}) copy-start(bf16[128,512]{1,0:T(8,128)(2,1)} %param.13) | copy-start | bytes 393220
  74.5 21.8 %collective-permute-start.2 = (f32[128,512]{1,0:T(8,128)S(1)}, f32[128,512]{1,0:T(8,128)S(1)}, u32[]{:S(2)}, u32[]{:S(2)}) collective-permute-start(f32[128,512]{1,0:T(8,128)S(1)} %get-tuple-element.5), channel_id=1, source_target_pairs={{0,2},{1,3},{2,4},{3,5},{4,6},{5,7},{6,8},{7,9},{8,10},{9,11},{10,... | collective-permute-start | bytes 786440 | tf_op jit(solution)/shard_map/ppermute | solution.py:15
  77.9 18.5 %collective-permute-start = (f32[128,512]{1,0:T(8,128)S(1)}, f32[128,512]{1,0:T(8,128)S(1)}, u32[]{:S(2)}, u32[]{:S(2)}) collective-permute-start(f32[128,512]{1,0:T(8,128)S(1)} %get-tuple-element.4), channel_id=1, source_target_pairs={{0,1},{1,2},{2,3},{3,4},{4,5},{5,6},{6,7},{7,8},{8,9},{9,10},{10,1... | collective-permute-start | bytes 786440 | tf_op jit(solution)/shard_map/ppermute | solution.py:15
  97.5 23.1 %collective-permute-start.5 = (bf16[128,512]{1,0:T(8,128)(2,1)S(1)}, bf16[128,512]{1,0:T(8,128)(2,1)S(1)}, u32[]{:S(2)}, u32[]{:S(2)}) collective-permute-start(bf16[128,512]{1,0:T(8,128)(2,1)S(1)} %get-tuple-element.2), channel_id=1, source_target_pairs={{0,61},{1,62},{2,63},{3,0},{4,1},{5,2},{6,3},{7,4},{8,5},{9,6},{10... | collective-permute-start | bytes 393224 | tf_op jit(solution)/shard_map/ppermute | solution.py:15
  110.0 12.2 %collective-permute-start.4 = (bf16[128,512]{1,0:T(8,128)(2,1)S(1)}, bf16[128,512]{1,0:T(8,128)(2,1)S(1)}, u32[]{:S(2)}, u32[]{:S(2)}) collective-permute-start(bf16[128,512]{1,0:T(8,128)(2,1)S(1)} %get-tuple-element.2), channel_id=1, source_target_pairs={{0,62},{1,63},{2,0},{3,1},{4,2},{5,3},{6,4},{7,5},{8,6},{9,7},{10,... | collective-permute-start | bytes 393224 | tf_op jit(solution)/shard_map/ppermute | solution.py:15
  113.3 10.6 %collective-permute-start.3 = (bf16[128,512]{1,0:T(8,128)(2,1)S(1)}, bf16[128,512]{1,0:T(8,128)(2,1)S(1)}, u32[]{:S(2)}, u32[]{:S(2)}) collective-permute-start(bf16[128,512]{1,0:T(8,128)(2,1)S(1)} %get-tuple-element.2), channel_id=1, source_target_pairs={{0,63},{1,0},{2,1},{3,2},{4,3},{5,4},{6,5},{7,6},{8,7},{9,8},{10,9... | collective-permute-start | bytes 393224 | tf_op jit(solution)/shard_map/ppermute | solution.py:15
  125.5 2.1 copy-start.1
  127.6 1.2 copy-start
  201.7 18.5 %all-to-all-start.5 = ((bf16[16,32,512]{2,1,0:T(8,128)(2,1)}), bf16[16,32,512]{2,1,0:T(8,128)(2,1)S(1)}, u32[]{:S(2)}, u32[]{:S(2)}) async-start(bf16[16,32,512]{2,1,0:T(8,128)(2,1)} %broadcast_in_dim.115), calls=%async_computation.5 | async-start | bytes 1048576 | tf_op jit(solution)/shard_map/all_to_all | solution.py:28

commit v12 on v8

--- a/solution.py
+++ b/solution.py
@@ -29,14 +29,23 @@
     return copies.reshape(peers * part.shape[0], *part.shape[1:])
 
 
+def swap_core(value):
+    return lax.ppermute(value, "core", [(0, 1), (1, 0)])
+
+
 def reduce_all(stacked, scale):
-    part = exchange_sum(stacked, "core")
+    first = lax.axis_index("core") == 0
+    halves = stacked.reshape(2, stacked.shape[0] // 2, stacked.shape[1])
+    kept = jnp.where(first, halves[0], halves[1])
+    part = kept + swap_core(jnp.where(first, halves[1], halves[0]))
     part = exchange_sum(part, ROW)
     part = exchange_sum(part, ("zhi", "y"))
     part = (part * scale).astype(jnp.bfloat16)
     part = exchange_gather(part, ("zhi", "y"))
     part = exchange_gather(part, ROW)
-    return exchange_gather(part, "core").astype(jnp.float32)
+    other = swap_core(part)
+    whole = jnp.where(first, jnp.concatenate([part, other]), jnp.concatenate([other, part]))
+    return whole.astype(jnp.float32)
 
 
 def gather_row(features):

time: 231 us -> 232 us (level)
  waiting for transfers between devices: 79.3 us -> 70.2 us
  blocking collectives: 78.9 us -> 82.9 us
  other arithmetic: 7.44 us -> 10 us
  starting transfers between devices: 48.5 us -> 50.9 us
    all_to_all x2 -> x1, waiting for transfers between devices: 49.5 us -> 38.2 us  [exchange_gather(): copies = lax.all_to_all(copies, axes, 0, 0, tiled=True)]
    ppermute x0 -> x2, starting transfers between devices: none -> 8.9 us  [swap_core(): return lax.ppermute(value, 'core', [(0, 1), (1, 0)])]
    all_to_all x2, blocking collectives: 23.4 us -> 31.9 us  [exchange_gather(): copies = lax.all_to_all(copies, axes, 0, 0, tiled=True)]
    all_to_all x2 -> x1, starting transfers between devices: 17.3 us -> 10.3 us  [exchange_gather(): copies = lax.all_to_all(copies, axes, 0, 0, tiled=True)]
    all_to_all x3 -> x2, blocking collectives: 55.5 us -> 51 us  [exchange_sum(): pieces = lax.all_to_all(pieces, axes, 0, 0, tiled=True)]
    ppermute x0 -> x2, waiting for transfers between devices: none -> 3.4 us  [swap_core(): return lax.ppermute(value, 'core', [(0, 1), (1, 0)])]
  transfers between devices with their start and end apart: 7 -> 8, of which waited for: 6 -> 7; matrix products, arithmetic and copies ran while one was open for 2% -> 2% of each run, Pallas kernels for 0% -> 0%
where the time goes in v12:
time: 232 us; the launch traced here: 231 us
  blocking collectives  82.9 us (36%)
  waiting for transfers between devices  70.2 us (30%)
  starting transfers between devices  50.9 us (22%)
  other arithmetic  10 us (4%)
  matrix products  7.7 us (3%)
  local copies, waits for them, and re-layouts  7.62 us (3%)
    all_to_all x2, blocking collectives, exchange_sum(): pieces = lax.all_to_all(pieces, axes, 0, 0, tiled=True)  51 us
    all_to_all x1, waiting for transfers between devices, exchange_gather(): copies = lax.all_to_all(copies, axes, 0, 0, tiled=True)  38.2 us
    all_to_all x2, blocking collectives, exchange_gather(): copies = lax.all_to_all(copies, axes, 0, 0, tiled=True)  31.9 us
    ppermute x5, starting transfers between devices, from_behind(): return lax.ppermute(value, COL, pairs)  31.7 us
    ppermute x5, waiting for transfers between devices, from_behind(): return lax.ppermute(value, COL, pairs)  28.6 us
    all_to_all x1, starting transfers between devices, exchange_gather(): copies = lax.all_to_all(copies, axes, 0, 0, tiled=True)  10.3 us
    ppermute x2, starting transfers between devices, swap_core(): return lax.ppermute(value, 'core', [(0, 1), (1, 0)])  8.9 us
  transfers between devices with their start and end apart: 8, of which 7 were waited for; matrix products, arithmetic and copies ran while one was open for 2% of the time, Pallas kernels for 0%

profile of v12, /device:TPU:1, one launch (start us, length us, event | category | flops | bytes accessed | tf_op | source)
XLA Modules:
  0.0 230.9 jit_solution(15589625821306890641)
XLA Ops:
  0.6 2.4 %broadcast_in_dim.99 = bf16[16,128,512]{2,1,0:T(8,128)(2,1)} broadcast(bf16[128,512]{1,0:T(8,128)(2,1)} %param.7), dimensions={1,2} | broadcast | bytes 2228224 | tf_op jit(solution)/shard_map/broadcast_in_dim | solution.py:27
  3.1 0.0 copy-start.2
  3.1 0.0 copy-start.10
  3.1 10.3 %all-to-all-start = ((bf16[16,128,512]{2,1,0:T(8,128)(2,1)}), bf16[16,128,512]{2,1,0:T(8,128)(2,1)S(1)}, u32[]{:S(2)}, u32[]{:S(2)}) async-start(bf16[16,128,512]{2,1,0:T(8,128)(2,1)} %broadcast_in_dim.99), calls=%async_computation | async-start | bytes 4194304 | tf_op jit(solution)/shard_map/all_to_all | solution.py:28
  14.0 0.0 copy-done.2
  14.0 0.2 copy.13
  14.2 0.0 copy-done.10
  14.3 0.0 copy-done.11
  14.3 0.5 fusion.31
  14.8 0.1 broadcast_bitcast_fusion
  14.9 1.1 broadcast_select_fusion.1
  16.0 38.2 %all-to-all-done = bf16[16,128,512]{2,1,0:T(8,128)(2,1)S(1)} async-done(((bf16[16,128,512]{2,1,0:T(8,128)(2,1)}), bf16[16,128,512]{2,1,0:T(8,128)(2,1)S(1)}, u32[]{:S(2)}, u32[]{:S(2)}) %all-to-all-start) | async-done | bytes 2097184 | tf_op jit(solution)/shard_map/all_to_all | solution.py:28
  54.2 0.6 gather_fusion
  54.8 0.0 copy-start.3
  54.8 1.2 bitcast_select_fusion
  56.0 0.2 copy-done.3
  56.2 2.6 %fusion.4 = f32[512,512]{1,0:T(8,128)S(1)} fusion(bf16[1024,512]{1,0:T(8,128)(2,1)} %bitcast_select_fusion, bf16[64,8,8,128]{3,2,1,0:T(8,128)(2,1)S(1)} %bitcast.86, bf16[1024,512]{1,0:T(8,128)(2,1)} %param.12), kind=kOutput, calls=%fused_computation.11 | convolution fusion | flops 1074266112 | bytes 3670016 | tf_op jit(solution)/shard_map/dot_general | solution.py:76
  58.8 0.0 copy-start.4
  58.8 0.0 copy-start.9
  58.8 0.0 copy-start.1
  58.9 12.4 %collective-permute-start = (f32[2,128,512]{2,1,0:T(8,128)S(1)}, f32[2,128,512]{2,1,0:T(8,128)S(1)}, u32[]{:S(2)}, u32[]{:S(2)}) collective-permute-start(f32[2,128,512]{2,1,0:T(8,128)S(1)} %pad_maximum_fusion), channel_id=1, source_target_pairs={{0,1},{1,2},{2,3},{3,4},{4,5},{5,6},{6,7},{7,8},{8,9},{9,10},{10,1... | collective-permute-start | bytes 1572872 | tf_op jit(solution)/shard_map/ppermute | solution.py:15
  71.3 0.0 copy-done.9
  71.4 0.7 compare_and_fusion
  72.1 0.0 copy-done.1
  72.1 1.3 fusion.19
  73.3 0.0 copy-start.8
  73.3 4.1 %collective-permute-done = f32[2,128,512]{2,1,0:T(8,128)S(1)} collective-permute-done((f32[2,128,512]{2,1,0:T(8,128)S(1)}, f32[2,128,512]{2,1,0:T(8,128)S(1)}, u32[]{:S(2)}, u32[]{:S(2)}) %collective-permute-start) | collective-permute-done | bytes 524320 | tf_op jit(solution)/shard_map/ppermute | solution.py:15
  77.5 0.0 copy-done.4
  77.5 0.7 copy-done.6
  78.2 3.3 %collective-permute-start.1 = (f32[128,512]{1,0:T(8,128)S(1)}, f32[128,512]{1,0:T(8,128)S(1)}, u32[]{:S(2)}, u32[]{:S(2)}) collective-permute-start(f32[128,512]{1,0:T(8,128)S(1)} %slice_add_fusion), channel_id=1, source_target_pairs={{0,2},{1,3},{2,4},{3,5},{4,6},{5,7},{6,8},{7,9},{8,10},{9,11},{10,... | collective-permute-start | bytes 786440 | tf_op jit(solution)/shard_map/ppermute | solution.py:15
  81.6 0.0 copy-start.7
  81.6 0.6 fusion.11
  82.1 20.3 %collective-permute-done.1 = f32[128,512]{1,0:T(8,128)S(1)} collective-permute-done((f32[128,512]{1,0:T(8,128)S(1)}, f32[128,512]{1,0:T(8,128)S(1)}, u32[]{:S(2)}, u32[]{:S(2)}) %collective-permute-start.1) | collective-permute-done | bytes 262176 | tf_op jit(solution)/shard_map/ppermute | solution.py:15
  102.5 0.0 copy-done.8
  102.5 0.0 copy-done.7
  102.5 1.8 multiply_convert_fusion
  104.3 9.1 %collective-permute-start.4 = (bf16[128,512]{1,0:T(8,128)(2,1)S(1)}, bf16[128,512]{1,0:T(8,128)(2,1)S(1)}, u32[]{:S(2)}, u32[]{:S(2)}) collective-permute-start(bf16[128,512]{1,0:T(8,128)(2,1)S(1)} %get-tuple-element.2), channel_id=1, source_target_pairs={{0,61},{1,62},{2,63},{3,0},{4,1},{5,2},{6,3},{7,4},{8,5},{9,6},{10... | collective-permute-start | bytes 393224 | tf_op jit(solution)/shard_map/ppermute | solution.py:15
  113.4 1.9 collective-permute-start.3
  115.3 5.0 %collective-permute-start.2 = (bf16[128,512]{1,0:T(8,128)(2,1)S(1)}, bf16[128,512]{1,0:T(8,128)(2,1)S(1)}, u32[]{:S(2)}, u32[]{:S(2)}) collective-permute-start(bf16[128,512]{1,0:T(8,128)(2,1)S(1)} %get-tuple-element.2), channel_id=1, source_target_pairs={{0,63},{1,0},{2,1},{3,2},{4,3},{5,4},{6,5},{7,6},{8,7},{9,8},{10,9... | collective-permute-start | bytes 393224 | tf_op jit(solution)/shard_map/ppermute | solution.py:15
  120.3 0.3 convolution_bitcast_fusion.1
  120.6 0.0 collective-permute-done.4
  120.6 2.6 %collective-permute-done.3 = bf16[128,512]{1,0:T(8,128)(2,1)S(1)} collective-permute-done((bf16[128,512]{1,0:T(8,128)(2,1)S(1)}, bf16[128,512]{1,0:T(8,128)(2,1)S(1)}, u32[]{:S(2)}, u32[]{:S(2)}) %collective-permute-start.3) | collective-permute-done | bytes 131104 | tf_op jit(solution)/shard_map/ppermute | solution.py:15
  123.2 1.6 collective-permute-done.2
  124.8 0.9 pad_maximum_fusion.1
  125.7 2.6 %gather_fusion.1 = bf16[8,128,512]{2,1,0:T(8,128)(2,1)} fusion(bf16[4,128,512]{2,1,0:T(8,128)(2,1)} %pad_maximum_fusion.1, s32[1024]{0:T(1024)S(1)} %pad_clamp_fusion), kind=kCustom, calls=%fused_computation.1 | custom fusion | bytes 2097184 | tf_op jit(solution)/shard_map/jit(_take)/gather | solution.py:91
  128.3 2.1 fusion.2
  130.4 0.0 copy-done
  130.4 0.8 broadcast_select_fusion.2
  131.3 1.9 collective-permute-start.5
  133.2 2.6 %collective-permute-done.5 = f32[512,512]{1,0:T(8,128)S(1)} collective-permute-done((f32[512,512]{1,0:T(8,128)S(1)}, f32[512,512]{1,0:T(8,128)S(1)}, u32[]{:S(2)}, u32[]{:S(2)}) %collective-permute-start.5) | collective-permute-done | bytes 1048608 | tf_op jit(solution)/shard_map/ppermute | solution.py:33
  135.8 0.3 select_add_fusion
  136.2 31.4 %all_to_all.25 = f32[16,32,512]{2,1,0:T(8,128)S(1)} all-to-all(f32[16,32,512]{2,1,0:T(8,128)S(1)} %bitcast.81), channel_id=1, replica_groups=mesh['zlo'=2,'x'=8,'zhi'=4,'y'=8,'core'=2] {'zlo','x'}, dimensions={0} | all-to-all | bytes 2097152 | tf_op jit(solution)/shard_map/all_to_all | solution.py:21
  167.6 0.1 reduce_sum.18
  167.7 19.5 %all_to_all.26 = f32[32,1,512]{2,1,0:T(1,128)S(1)} all-to-all(f32[32,1,512]{2,1,0:T(1,128)S(1)} %reshape.203), channel_id=1, replica_groups=mesh['zlo'=2,'x'=8,'zhi'=4,'y'=8,'core'=2] {'zhi','y'}, dimensions={0} | all-to-all | bytes 131072 | tf_op jit(solution)/shard_map/all_to_all | solution.py:21
  187.2 0.1 reduce_sum.19
  187.4 0.5 broadcast.211
  187.9 0.8 reduce.1
  188.7 14.1 %all_to_all.27 = bf16[32,2,256]{2,1,0:T(2,128)(2,1)S(1)} all-to-all(bf16[32,2,256]{2,1,0:T(2,128)(2,1)S(1)} %reshape.223), channel_id=1, replica_groups=mesh['zlo'=2,'x'=8,'zhi'=4,'y'=8,'core'=2] {'zhi','y'}, dimensions={0} | all-to-all | bytes 65536 | tf_op jit(solution)/shard_map/all_to_all | solution.py:28
  202.9 17.9 %all_to_all.28 = bf16[16,32,512]{2,1,0:T(8,128)(2,1)S(1)} all-to-all(bf16[16,32,512]{2,1,0:T(8,128)(2,1)S(1)} %broadcast_in_dim.108), channel_id=1, replica_groups=mesh['zlo'=2,'x'=8,'zhi'=4,'y'=8,'core'=2] {'zlo','x'}, dimensions={0} | all-to-all | bytes 1048576 | tf_op jit(solution)/shard_map/all_to_all | solution.py:28
  220.8 7.0 %collective-permute-start.6 = (bf16[512,512]{1,0:T(8,128)(2,1)S(1)}, bf16[512,512]{1,0:T(8,128)(2,1)S(1)}, u32[]{:S(2)}, u32[]{:S(2)}) collective-permute-start(bf16[512,512]{1,0:T(8,128)(2,1)S(1)} %bitcast.82), channel_id=1, source_target_pairs={{0,1},{1,0},{2,3},{3,2},{4,5},{5,4},{6,7},{7,6},{8,9},{9,8},{10,11... | collective-permute-start | bytes 1572872 | tf_op jit(solution)/shard_map/ppermute | solution.py:33
  227.8 0.0 copy-done.5
  227.8 0.7 multiply_convert_fusion.1
  228.5 0.8 collective-permute-done.6
  229.3 1.7 fusion.8
  (21 shorter events, 0.4 us)
Async XLA Ops:
  3.1 10.9 %copy-start.2 = (bf16[1,8,128,128]{3,2,1,0:T(8,128)(2,1)S(1)}, bf16[1,8,128,128]{3,2,1,0:T(8,128)(2,1)}, u32[]{:S(2)}) copy-start(bf16[1,8,128,128]{3,2,1,0:T(8,128)(2,1)} %param.8) | copy-start | bytes 786436
  3.1 11.1 %copy-start.10 = (s32[1,8]{1,0:T(1,128)S(1)}, s32[1,8]{1,0:T(1,128)}, u32[]{:S(2)}) copy-start(s32[1,8]{1,0:T(1,128)} %param.10) | copy-start | bytes 100
  3.1 11.2 %copy-start.11 = (s32[1,8]{1,0:T(1,128)S(1)}, s32[1,8]{1,0:T(1,128)}, u32[]{:S(2)}) copy-start(s32[1,8]{1,0:T(1,128)} %param.9) | copy-start | bytes 100
  3.1 51.1 %all-to-all-start = ((bf16[16,128,512]{2,1,0:T(8,128)(2,1)}), bf16[16,128,512]{2,1,0:T(8,128)(2,1)S(1)}, u32[]{:S(2)}, u32[]{:S(2)}) async-start(bf16[16,128,512]{2,1,0:T(8,128)(2,1)} %broadcast_in_dim.99), calls=%async_computation | async-start | bytes 4194304 | tf_op jit(solution)/shard_map/all_to_all | solution.py:28
  54.8 1.4 copy-start.3
  58.8 18.7 %copy-start.4 = (f32[512,512]{1,0:T(8,128)}, f32[512,512]{1,0:T(8,128)S(1)}, u32[]{:S(2)}) copy-start(f32[512,512]{1,0:T(8,128)S(1)} %fusion.4) | copy-start | bytes 3145732
  58.8 12.5 %copy-start.9 = (s32[8]{0:T(128)S(1)}, s32[8]{0:T(128)}, u32[]{:S(2)}) copy-start(s32[8]{0:T(128)} %fusion.31) | copy-start | bytes 100
  58.8 13.2 %copy-start.1 = (bf16[128,512]{1,0:T(8,128)(2,1)S(1)}, bf16[128,512]{1,0:T(8,128)(2,1)}, u32[]{:S(2)}) copy-start(bf16[128,512]{1,0:T(8,128)(2,1)} %param.7) | copy-start | bytes 393220
  58.9 18.5 %collective-permute-start = (f32[2,128,512]{2,1,0:T(8,128)S(1)}, f32[2,128,512]{2,1,0:T(8,128)S(1)}, u32[]{:S(2)}, u32[]{:S(2)}) collective-permute-start(f32[2,128,512]{2,1,0:T(8,128)S(1)} %pad_maximum_fusion), channel_id=1, source_target_pairs={{0,1},{1,2},{2,3},{3,4},{4,5},{5,6},{6,7},{7,8},{8,9},{9,10},{10,1... | collective-permute-start | bytes 1572872 | tf_op jit(solution)/shard_map/ppermute | solution.py:15
  73.3 29.1 %copy-start.8 = (bf16[128,512]{1,0:T(8,128)(2,1)S(1)}, bf16[128,512]{1,0:T(8,128)(2,1)}, u32[]{:S(2)}) copy-start(bf16[128,512]{1,0:T(8,128)(2,1)} %param.13) | copy-start | bytes 393220
  77.5 0.8 copy-start.6
  78.2 24.2 %collective-permute-start.1 = (f32[128,512]{1,0:T(8,128)S(1)}, f32[128,512]{1,0:T(8,128)S(1)}, u32[]{:S(2)}, u32[]{:S(2)}) collective-permute-start(f32[128,512]{1,0:T(8,128)S(1)} %slice_add_fusion), channel_id=1, source_target_pairs={{0,2},{1,3},{2,4},{3,5},{4,6},{5,7},{6,8},{7,9},{8,10},{9,11},{10,... | collective-permute-start | bytes 786440 | tf_op jit(solution)/shard_map/ppermute | solution.py:15
  81.6 20.9 %copy-start.7 = (f32[2,128,512]{2,1,0:T(8,128)S(1)}, f32[2,128,512]{2,1,0:T(8,128)}, u32[]{:S(2)}) copy-start(f32[2,128,512]{2,1,0:T(8,128)} %copy-done.6) | copy-start | bytes 1572868
  104.3 16.4 %collective-permute-start.4 = (bf16[128,512]{1,0:T(8,128)(2,1)S(1)}, bf16[128,512]{1,0:T(8,128)(2,1)S(1)}, u32[]{:S(2)}, u32[]{:S(2)}) collective-permute-start(bf16[128,512]{1,0:T(8,128)(2,1)S(1)} %get-tuple-element.2), channel_id=1, source_target_pairs={{0,61},{1,62},{2,63},{3,0},{4,1},{5,2},{6,3},{7,4},{8,5},{9,6},{10... | collective-permute-start | bytes 393224 | tf_op jit(solution)/shard_map/ppermute | solution.py:15
  113.4 9.9 %collective-permute-start.3 = (bf16[128,512]{1,0:T(8,128)(2,1)S(1)}, bf16[128,512]{1,0:T(8,128)(2,1)S(1)}, u32[]{:S(2)}, u32[]{:S(2)}) collective-permute-start(bf16[128,512]{1,0:T(8,128)(2,1)S(1)} %get-tuple-element.2), channel_id=1, source_target_pairs={{0,62},{1,63},{2,0},{3,1},{4,2},{5,3},{6,4},{7,5},{8,6},{9,7},{10,... | collective-permute-start | bytes 393224 | tf_op jit(solution)/shard_map/ppermute | solution.py:15
  115.3 9.6 %collective-permute-start.2 = (bf16[128,512]{1,0:T(8,128)(2,1)S(1)}, bf16[128,512]{1,0:T(8,128)(2,1)S(1)}, u32[]{:S(2)}, u32[]{:S(2)}) collective-permute-start(bf16[128,512]{1,0:T(8,128)(2,1)S(1)} %get-tuple-element.2), channel_id=1, source_target_pairs={{0,63},{1,0},{2,1},{3,2},{4,3},{5,4},{6,5},{7,6},{8,7},{9,8},{10,9... | collective-permute-start | bytes 393224 | tf_op jit(solution)/shard_map/ppermute | solution.py:15
  128.3 2.1 copy-start
  131.3 4.6 %collective-permute-start.5 = (f32[512,512]{1,0:T(8,128)S(1)}, f32[512,512]{1,0:T(8,128)S(1)}, u32[]{:S(2)}, u32[]{:S(2)}) collective-permute-start(f32[512,512]{1,0:T(8,128)S(1)} %get-tuple-element.6), channel_id=1, source_target_pairs={{0,1},{1,0},{2,3},{3,2},{4,5},{5,4},{6,7},{7,6},{8,9},{9,8},{10,11... | collective-permute-start | bytes 3145736 | tf_op jit(solution)/shard_map/ppermute | solution.py:33
  167.6 60.2 %copy-start.5 = (f32[128,512]{1,0:T(8,128)S(1)}, f32[128,512]{1,0:T(8,128)}, u32[]{:S(2)}) copy-start(f32[128,512]{1,0:T(8,128)} %get-tuple-element.3) | copy-start | bytes 786436
  220.8 8.5 %collective-permute-start.6 = (bf16[512,512]{1,0:T(8,128)(2,1)S(1)}, bf16[512,512]{1,0:T(8,128)(2,1)S(1)}, u32[]{:S(2)}, u32[]{:S(2)}) collective-permute-start(bf16[512,512]{1,0:T(8,128)(2,1)S(1)} %bitcast.82), channel_id=1, source_target_pairs={{0,1},{1,0},{2,3},{3,2},{4,5},{5,4},{6,7},{7,6},{8,9},{9,8},{10,11... | collective-permute-start | bytes 1572872 | tf_op jit(solution)/shard_map/ppermute | solution.py:33

commit v13 on v8

--- a/solution.py
+++ b/solution.py
@@ -77,8 +77,9 @@
     upstream = (cotangent.astype(jnp.float32) * slope).astype(jnp.bfloat16)
     grad_self = jnp.dot(features.T, upstream, preferred_element_type=jnp.float32)
 
-    window = [upstream] + [from_behind(upstream, -step) for step in range(1, REACH)]
-    window = jnp.stack(window)
+    ahead = from_behind(upstream, -1)
+    farther = from_behind(jnp.stack([upstream, ahead]), -2)
+    window = jnp.stack([upstream, ahead, farther[0], farther[1]])
     reached = jnp.take(window, offsets, axis=0).reshape(slots * tile_size, width)
     mixed = jnp.einsum("tij,tjx->tix", tiles, chosen, preferred_element_type=jnp.float32)
     mixed = jnp.where(live[:, None, None], mixed, 0.0).reshape(slots * tile_size, width)

time: 231 us -> 239 us (1.035)
  starting transfers between devices: 48.5 us -> 54.8 us
    ppermute x5 -> x4, starting transfers between devices: 31.2 us -> 37.6 us  [from_behind(): return lax.ppermute(value, COL, pairs)]
    ppermute x5 -> x4, waiting for transfers between devices: 29.8 us -> 29.9 us  [from_behind(): return lax.ppermute(value, COL, pairs)]
  transfers between devices with their start and end apart: 7 -> 6, of which waited for: 6 -> 6; matrix products, arithmetic and copies ran while one was open for 2% -> 2% of each run, Pallas kernels for 0% -> 0%
where the time goes in v13:
time: 239 us; the launch traced here: 238 us
  blocking collectives  80.7 us (34%)
  waiting for transfers between devices  79.3 us (33%)
  starting transfers between devices  54.8 us (23%)
  matrix products  7.6 us (3%)
  other arithmetic  7.19 us (3%)
  local copies, waits for them, and re-layouts  7.14 us (3%)
    all_to_all x3, blocking collectives, exchange_sum(): pieces = lax.all_to_all(pieces, axes, 0, 0, tiled=True)  57.3 us
    all_to_all x2, waiting for transfers between devices, exchange_gather(): copies = lax.all_to_all(copies, axes, 0, 0, tiled=True)  49.5 us
    ppermute x4, starting transfers between devices, from_behind(): return lax.ppermute(value, COL, pairs)  37.6 us
    ppermute x4, waiting for transfers between devices, from_behind(): return lax.ppermute(value, COL, pairs)  29.9 us
    all_to_all x2, blocking collectives, exchange_gather(): copies = lax.all_to_all(copies, axes, 0, 0, tiled=True)  23.4 us
    all_to_all x2, starting transfers between devices, exchange_gather(): copies = lax.all_to_all(copies, axes, 0, 0, tiled=True)  17.3 us
  transfers between devices with their start and end apart: 6, of which 6 were waited for; matrix products, arithmetic and copies ran while one was open for 2% of the time, Pallas kernels for 0%

profile of v13, /device:TPU:1, one launch (start us, length us, event | category | flops | bytes accessed | tf_op | source)
XLA Modules:
  0.0 238.4 jit_solution(5164154020365938830)
XLA Ops:
  0.6 2.4 %broadcast_in_dim.106 = bf16[16,128,512]{2,1,0:T(8,128)(2,1)} broadcast(bf16[128,512]{1,0:T(8,128)(2,1)} %param.7), dimensions={1,2} | broadcast | bytes 2228224 | tf_op jit(solution)/shard_map/broadcast_in_dim | solution.py:27
  3.1 0.0 copy-start.3
  3.1 0.0 copy-start.8
  3.1 0.0 copy-start.9
  3.1 10.3 %all-to-all-start = ((bf16[16,128,512]{2,1,0:T(8,128)(2,1)}), bf16[16,128,512]{2,1,0:T(8,128)(2,1)S(1)}, u32[]{:S(2)}, u32[]{:S(2)}) async-start(bf16[16,128,512]{2,1,0:T(8,128)(2,1)} %broadcast_in_dim.106), calls=%async_computation | async-start | bytes 4194304 | tf_op jit(solution)/shard_map/all_to_all | solution.py:28
  14.0 0.0 copy-done.3
  14.0 0.2 copy.15
  14.2 0.0 copy-done.8
  14.3 0.0 copy-done.9
  14.3 0.1 broadcast_bitcast_fusion
  14.4 1.1 broadcast_select_fusion.1
  15.5 38.7 %all-to-all-done = bf16[16,128,512]{2,1,0:T(8,128)(2,1)S(1)} async-done(((bf16[16,128,512]{2,1,0:T(8,128)(2,1)}), bf16[16,128,512]{2,1,0:T(8,128)(2,1)S(1)}, u32[]{:S(2)}, u32[]{:S(2)}) %all-to-all-start) | async-done | bytes 2097184 | tf_op jit(solution)/shard_map/all_to_all | solution.py:28
  54.2 0.6 gather_fusion
  54.8 0.0 copy-start.4
  54.8 1.2 bitcast_select_fusion
  56.0 0.2 copy-done.4
  56.2 2.6 %fusion.4 = f32[512,512]{1,0:T(8,128)S(1)} fusion(bf16[1024,512]{1,0:T(8,128)(2,1)} %bitcast_select_fusion, bf16[64,8,8,128]{3,2,1,0:T(8,128)(2,1)S(1)} %bitcast.90, bf16[1024,512]{1,0:T(8,128)(2,1)} %param.12), kind=kOutput, calls=%fused_computation.12 | convolution fusion | flops 1074266112 | bytes 3670016 | tf_op jit(solution)/shard_map/dot_general | solution.py:67
  58.8 0.0 copy-start.2
  58.8 0.0 copy-start.6
  58.8 0.0 copy-start.7
  58.9 12.4 %collective-permute-start = (f32[2,128,512]{2,1,0:T(8,128)S(1)}, f32[2,128,512]{2,1,0:T(8,128)S(1)}, u32[]{:S(2)}, u32[]{:S(2)}) collective-permute-start(f32[2,128,512]{2,1,0:T(8,128)S(1)} %pad_maximum_fusion.1), channel_id=1, source_target_pairs={{0,1},{1,2},{2,3},{3,4},{4,5},{5,6},{6,7},{7,8},{8,9},{9,10},{10,1... | collective-permute-start | bytes 1572872 | tf_op jit(solution)/shard_map/ppermute | solution.py:15
  71.3 6.1 %collective-permute-done = f32[2,128,512]{2,1,0:T(8,128)S(1)} collective-permute-done((f32[2,128,512]{2,1,0:T(8,128)S(1)}, f32[2,128,512]{2,1,0:T(8,128)S(1)}, u32[]{:S(2)}, u32[]{:S(2)}) %collective-permute-start) | collective-permute-done | bytes 524320 | tf_op jit(solution)/shard_map/ppermute | solution.py:15
  77.5 3.3 %collective-permute-start.1 = (f32[128,512]{1,0:T(8,128)S(1)}, f32[128,512]{1,0:T(8,128)S(1)}, u32[]{:S(2)}, u32[]{:S(2)}) collective-permute-start(f32[128,512]{1,0:T(8,128)S(1)} %slice_add_fusion), channel_id=1, source_target_pairs={{0,2},{1,3},{2,4},{3,5},{4,6},{5,7},{6,8},{7,9},{8,10},{9,11},{10,... | collective-permute-start | bytes 786440 | tf_op jit(solution)/shard_map/ppermute | solution.py:15
  80.8 0.0 copy-done.2
  80.8 0.0 copy-done.6
  80.9 0.2 fusion.18
  81.1 21.1 %collective-permute-done.1 = f32[128,512]{1,0:T(8,128)S(1)} collective-permute-done((f32[128,512]{1,0:T(8,128)S(1)}, f32[128,512]{1,0:T(8,128)S(1)}, u32[]{:S(2)}, u32[]{:S(2)}) %collective-permute-start.1) | collective-permute-done | bytes 262176 | tf_op jit(solution)/shard_map/ppermute | solution.py:15
  102.2 0.0 copy-done.7
  102.2 0.8 multiply_convert_fusion
  103.0 11.6 %collective-permute-start.2 = (bf16[128,512]{1,0:T(8,128)(2,1)S(1)}, bf16[128,512]{1,0:T(8,128)(2,1)S(1)}, u32[]{:S(2)}, u32[]{:S(2)}) collective-permute-start(bf16[128,512]{1,0:T(8,128)(2,1)S(1)} %get-tuple-element.2), channel_id=1, source_target_pairs={{0,63},{1,0},{2,1},{3,2},{4,3},{5,4},{6,5},{7,6},{8,7},{9,8},{10,9... | collective-permute-start | bytes 393224 | tf_op jit(solution)/shard_map/ppermute | solution.py:15
  114.6 0.9 collective-permute-done.2
  115.6 10.2 %collective-permute-start.3 = (bf16[2,128,512]{2,1,0:T(8,128)(2,1)S(1)}, bf16[2,128,512]{2,1,0:T(8,128)(2,1)S(1)}, u32[]{:S(2)}, u32[]{:S(2)}) collective-permute-start(bf16[2,128,512]{2,1,0:T(8,128)(2,1)S(1)} %pad_maximum_fusion.3), channel_id=1, source_target_pairs={{0,62},{1,63},{2,0},{3,1},{4,2},{5,3},{6,4},{7,5},{8,6},{9,7},{10,... | collective-permute-start | bytes 786440 | tf_op jit(solution)/shard_map/ppermute | solution.py:15
  125.8 0.6 fusion.10
  126.4 1.3 convolution_bitcast_fusion.1
  127.7 1.8 collective-permute-done.3
  129.5 0.1 pad_maximum_fusion.2
  129.5 1.6 gather_fusion.1
  131.1 0.0 copy-start.1
  131.1 2.1 convolution_bitcast_fusion
  133.2 0.0 copy-done.1
  133.2 0.0 copy-start
  133.2 0.8 fusion.3
  134.0 0.4 copy-done
  134.5 0.2 pad_maximum_fusion
  134.6 5.1 %all_to_all.35 = f32[2,512,512]{2,1,0:T(8,128)S(1)} all-to-all(f32[2,512,512]{2,1,0:T(8,128)S(1)} %bitcast.84), channel_id=1, replica_groups=mesh['zlo'=2,'x'=8,'zhi'=4,'y'=8,'core'=2] {'core'}, dimensions={0} | all-to-all | bytes 4194304 | tf_op jit(solution)/shard_map/all_to_all | solution.py:21
  139.7 0.3 reduce_sum.27
  139.9 30.9 %all_to_all.36 = f32[16,32,512]{2,1,0:T(8,128)S(1)} all-to-all(f32[16,32,512]{2,1,0:T(8,128)S(1)} %bitcast.85), channel_id=1, replica_groups=mesh['zlo'=2,'x'=8,'zhi'=4,'y'=8,'core'=2] {'zlo','x'}, dimensions={0} | all-to-all | bytes 2097152 | tf_op jit(solution)/shard_map/all_to_all | solution.py:21
  170.9 0.0 copy-start.5
  170.9 0.1 reduce_sum.28
  170.9 0.1 copy.17
  171.0 21.3 %all_to_all.37 = f32[32,1,512]{2,1,0:T(1,128)S(1)} all-to-all(f32[32,1,512]{2,1,0:T(1,128)S(1)} %copy.17), channel_id=1, replica_groups=mesh['zlo'=2,'x'=8,'zhi'=4,'y'=8,'core'=2] {'zhi','y'}, dimensions={0} | all-to-all | bytes 131072 | tf_op jit(solution)/shard_map/all_to_all | solution.py:21
  192.3 0.1 reduce_sum.29
  192.5 0.5 broadcast.211
  193.0 0.8 reduce.1
  193.8 14.1 %all_to_all.38 = bf16[32,2,256]{2,1,0:T(2,128)(2,1)S(1)} all-to-all(bf16[32,2,256]{2,1,0:T(2,128)(2,1)S(1)} %reshape.223), channel_id=1, replica_groups=mesh['zlo'=2,'x'=8,'zhi'=4,'y'=8,'core'=2] {'zhi','y'}, dimensions={0} | all-to-all | bytes 65536 | tf_op jit(solution)/shard_map/all_to_all | solution.py:28
  207.9 0.8 broadcast_in_dim.115
  208.8 7.0 %all-to-all-start.5 = ((bf16[16,32,512]{2,1,0:T(8,128)(2,1)}), bf16[16,32,512]{2,1,0:T(8,128)(2,1)S(1)}, u32[]{:S(2)}, u32[]{:S(2)}) async-start(bf16[16,32,512]{2,1,0:T(8,128)(2,1)} %broadcast_in_dim.115), calls=%async_computation.5 | async-start | bytes 1048576 | tf_op jit(solution)/shard_map/all_to_all | solution.py:28
  215.8 0.0 copy-done.5
  215.8 0.7 multiply_convert_fusion.1
  216.6 10.8 %all-to-all-done.5 = bf16[16,32,512]{2,1,0:T(8,128)(2,1)S(1)} async-done(((bf16[16,32,512]{2,1,0:T(8,128)(2,1)}), bf16[16,32,512]{2,1,0:T(8,128)(2,1)S(1)}, u32[]{:S(2)}, u32[]{:S(2)}) %all-to-all-start.5) | async-done | bytes 524320 | tf_op jit(solution)/shard_map/all_to_all | solution.py:28
  227.3 0.1 broadcast_in_dim.117
  227.4 9.3 %all_to_all.39 = bf16[2,512,512]{2,1,0:T(8,128)(2,1)S(1)} all-to-all(bf16[2,512,512]{2,1,0:T(8,128)(2,1)S(1)} %broadcast_in_dim.117), channel_id=1, replica_groups=mesh['zlo'=2,'x'=8,'zhi'=4,'y'=8,'core'=2] {'core'}, dimensions={0} | all-to-all | bytes 2097152 | tf_op jit(solution)/shard_map/all_to_all | solution.py:28
  236.7 1.7 bitcast_convert_fusion.6
  (18 shorter events, 0.3 us)
Async XLA Ops:
  3.1 10.9 %copy-start.3 = (bf16[1,8,128,128]{3,2,1,0:T(8,128)(2,1)S(1)}, bf16[1,8,128,128]{3,2,1,0:T(8,128)(2,1)}, u32[]{:S(2)}) copy-start(bf16[1,8,128,128]{3,2,1,0:T(8,128)(2,1)} %param.8) | copy-start | bytes 786436
  3.1 11.1 %copy-start.8 = (s32[1,8]{1,0:T(1,128)S(1)}, s32[1,8]{1,0:T(1,128)}, u32[]{:S(2)}) copy-start(s32[1,8]{1,0:T(1,128)} %param.10) | copy-start | bytes 100
  3.1 11.2 %copy-start.9 = (s32[1,8]{1,0:T(1,128)S(1)}, s32[1,8]{1,0:T(1,128)}, u32[]{:S(2)}) copy-start(s32[1,8]{1,0:T(1,128)} %param.9) | copy-start | bytes 100
  3.1 51.1 %all-to-all-start = ((bf16[16,128,512]{2,1,0:T(8,128)(2,1)}), bf16[16,128,512]{2,1,0:T(8,128)(2,1)S(1)}, u32[]{:S(2)}, u32[]{:S(2)}) async-start(bf16[16,128,512]{2,1,0:T(8,128)(2,1)} %broadcast_in_dim.106), calls=%async_computation | async-start | bytes 4194304 | tf_op jit(solution)/shard_map/all_to_all | solution.py:28
  54.8 1.4 copy-start.4
  58.8 22.0 %copy-start.2 = (bf16[128,512]{1,0:T(8,128)(2,1)S(1)}, bf16[128,512]{1,0:T(8,128)(2,1)}, u32[]{:S(2)}) copy-start(bf16[128,512]{1,0:T(8,128)(2,1)} %param.7) | copy-start | bytes 393220
  58.8 22.0 %copy-start.6 = (bf16[1024,512]{1,0:T(8,128)(2,1)S(1)}, bf16[1024,512]{1,0:T(8,128)(2,1)}, u32[]{:S(2)}) copy-start(bf16[1024,512]{1,0:T(8,128)(2,1)} %param.12) | copy-start | bytes 3145732
  58.8 43.3 %copy-start.7 = (bf16[128,512]{1,0:T(8,128)(2,1)S(1)}, bf16[128,512]{1,0:T(8,128)(2,1)}, u32[]{:S(2)}) copy-start(bf16[128,512]{1,0:T(8,128)(2,1)} %param.13) | copy-start | bytes 393220
  58.9 18.5 %collective-permute-start = (f32[2,128,512]{2,1,0:T(8,128)S(1)}, f32[2,128,512]{2,1,0:T(8,128)S(1)}, u32[]{:S(2)}, u32[]{:S(2)}) collective-permute-start(f32[2,128,512]{2,1,0:T(8,128)S(1)} %pad_maximum_fusion.1), channel_id=1, source_target_pairs={{0,1},{1,2},{2,3},{3,4},{4,5},{5,6},{6,7},{7,8},{8,9},{9,10},{10,1... | collective-permute-start | bytes 1572872 | tf_op jit(solution)/shard_map/ppermute | solution.py:15
  77.5 24.7 %collective-permute-start.1 = (f32[128,512]{1,0:T(8,128)S(1)}, f32[128,512]{1,0:T(8,128)S(1)}, u32[]{:S(2)}, u32[]{:S(2)}) collective-permute-start(f32[128,512]{1,0:T(8,128)S(1)} %slice_add_fusion), channel_id=1, source_target_pairs={{0,2},{1,3},{2,4},{3,5},{4,6},{5,7},{6,8},{7,9},{8,10},{9,11},{10,... | collective-permute-start | bytes 786440 | tf_op jit(solution)/shard_map/ppermute | solution.py:15
  103.0 12.6 %collective-permute-start.2 = (bf16[128,512]{1,0:T(8,128)(2,1)S(1)}, bf16[128,512]{1,0:T(8,128)(2,1)S(1)}, u32[]{:S(2)}, u32[]{:S(2)}) collective-permute-start(bf16[128,512]{1,0:T(8,128)(2,1)S(1)} %get-tuple-element.2), channel_id=1, source_target_pairs={{0,63},{1,0},{2,1},{3,2},{4,3},{5,4},{6,5},{7,6},{8,7},{9,8},{10,9... | collective-permute-start | bytes 393224 | tf_op jit(solution)/shard_map/ppermute | solution.py:15
  115.6 13.9 %collective-permute-start.3 = (bf16[2,128,512]{2,1,0:T(8,128)(2,1)S(1)}, bf16[2,128,512]{2,1,0:T(8,128)(2,1)S(1)}, u32[]{:S(2)}, u32[]{:S(2)}) collective-permute-start(bf16[2,128,512]{2,1,0:T(8,128)(2,1)S(1)} %pad_maximum_fusion.3), channel_id=1, source_target_pairs={{0,62},{1,63},{2,0},{3,1},{4,2},{5,3},{6,4},{7,5},{8,6},{9,7},{10,... | collective-permute-start | bytes 786440 | tf_op jit(solution)/shard_map/ppermute | solution.py:15
  131.1 2.1 copy-start.1
  133.2 1.2 copy-start
  170.9 45.0 %copy-start.5 = (f32[128,512]{1,0:T(8,128)S(1)}, f32[128,512]{1,0:T(8,128)}, u32[]{:S(2)}) copy-start(f32[128,512]{1,0:T(8,128)} %get-tuple-element.3) | copy-start | bytes 786436
  208.8 18.5 %all-to-all-start.5 = ((bf16[16,32,512]{2,1,0:T(8,128)(2,1)}), bf16[16,32,512]{2,1,0:T(8,128)(2,1)S(1)}, u32[]{:S(2)}, u32[]{:S(2)}) async-start(bf16[16,32,512]{2,1,0:T(8,128)(2,1)} %broadcast_in_dim.115), calls=%async_computation.5 | async-start | bytes 1048576 | tf_op jit(solution)/shard_map/all_to_all | solution.py:28
